TPU v7x, 32 devices: a whole 2x2x4 slice. The times are simulated.
32 devices in a mesh: req: 4 (over y, x), mp: 8 (over z, core).
Axes of the slice: x: 2, y: 2, z: 4, core: 2. Of those that a mesh axis runs over, the one named last changes fastest.
Arguments:
- tokens: bfloat16 [1024, 2048], P('req'), may hold values from -6 to 6
- lengths: int32 [4, 8], P('req'), may hold values from 1 to 80, 256 in all within a row
- response: int32 [1024], P('req'), may hold values 0 or 1
- targets: int32 [1024], replicated, may hold values from 0 to 32063, as said below
- attn_gain: float32 [2, 2048], replicated, may hold values from 0.5 to 1.5
- w_query: bfloat16 [2, 2048, 2048], P(None, None, 'mp')
- w_key: bfloat16 [2, 2048, 512], replicated, may hold values from -0.125 to 0.125
- w_value: bfloat16 [2, 2048, 512], replicated, may hold values from -0.125 to 0.125
- output_weight: bfloat16 [2, 2048, 2048], P(None, 'mp'), may hold values from -0.125 to 0.125
- mlp_gain: float32 [2, 2048], replicated, may hold values from 0.5 to 1.5
- w_gate: bfloat16 [2, 2048, 8192], P(None, None, 'mp'), may hold values from -0.125 to 0.125
- w_up: bfloat16 [2, 2048, 8192], P(None, None, 'mp'), may hold values from -0.125 to 0.125
- w_down: bfloat16 [2, 8192, 2048], P(None, 'mp'), may hold values from -0.0625 to 0.0625
- final_gain: float32 [2, 2048], replicated, may hold values from 0.5 to 1.5
- w_head: bfloat16 [2, 2048, 32064], P(None, None, ('req', 'mp'))
Outputs:
- token_diff: float32 [1024], P(('req', 'mp'))
- request_sum: float32 [4, 8], P('req')
- request_peak: float32 [4, 8], P('req')
Inputs may be any that keep to these rules, and one draw needn't show every extreme that they name: `lengths`: each row sums to 256; some request of each tenant has exactly 80 tokens. `targets`: vocabulary ids.
All inputs are finite; a program needn't handle non-finite values. No bound on the sum of `response` on one device may be relied on, other than what follows from the above.
Results may differ from a plain program's by a relative error of at most 0.04.
Values may be sent and summed in bfloat16 or wider, within the bound.
No kernel may reach another device: no remote copies, remote signals or barrier semaphores. Data moves between devices by JAX's collectives and lax.ppermute only.
A program may use at most 128 MiB of HBM per device.

v0:
```python
import jax
import jax.numpy as jnp
from jax import lax
from jax.sharding import PartitionSpec as P

HEADS = 32
KV_HEADS = 8
HEAD_DIM = 64


epsilon = 1e-05
theta = 500000.0


def merged(part, axis, combine):
    gathered = jax.tree.map(lambda a: lax.all_gather(a, axis), part)

    def take(source):
        return jax.tree.map(lambda a: lax.dynamic_index_in_dim(a, source, 0, False), gathered)

    return lax.fori_loop(
        1, lax.axis_size(axis), lambda source, state: combine(state, take(source)), take(0)
    )


def rms_scale(entries, scaling):
    entries = entries.astype(jnp.float32)
    inverse = lax.rsqrt(jnp.mean(entries * entries, axis=-1, keepdims=True) + epsilon)
    return entries * inverse * scaling


def rotate(entries, positions):
    halfway = entries.shape[-1] // 2
    frequency = theta ** (-jnp.arange(halfway, dtype=jnp.float32) * 2.0 / entries.shape[-1])
    angles = positions.astype(jnp.float32)[:, None] * frequency[None, :]
    cosine = jnp.cos(angles)
    sine_part = jnp.sin(angles)
    former = entries[..., :halfway]
    latter = entries[..., halfway:]
    return jnp.concatenate(
        [former * cosine - latter * sine_part, latter * cosine + former * sine_part], axis=-1
    )


def request_layout(length_row, slot_count):
    end_slot = jnp.cumsum(length_row, dtype=jnp.int32)
    start_slot = end_slot - length_row
    slot_ids = jnp.arange(slot_count, dtype=jnp.int32)
    member = (slot_ids[:, None] >= start_slot[None, :]) & (slot_ids[:, None] < end_slot[None, :])
    segment = jnp.sum((slot_ids[:, None] >= end_slot[None, :]).astype(jnp.int32), axis=1)
    offset = jnp.sum(jnp.where(member, start_slot[None, :], 0), axis=1)
    return (member, segment, slot_ids - offset)


def allowed_pairs(segment):
    slot_ids = jnp.arange(segment.shape[0], dtype=jnp.int32)
    return (segment[:, None] == segment[None, :]) & (slot_ids[None, :] <= slot_ids[:, None])


def attend_heads(query, key_rows, value_rows, positions, allowed, repeat_times):
    slot_count = query.shape[0]
    query = rotate(query.reshape(slot_count, -1, HEAD_DIM).transpose(1, 0, 2), positions).astype(
        jnp.bfloat16
    )
    key_rows = rotate(
        key_rows.reshape(slot_count, -1, HEAD_DIM).transpose(1, 0, 2), positions
    ).astype(jnp.bfloat16)
    value_rows = (
        value_rows.reshape(slot_count, -1, HEAD_DIM).transpose(1, 0, 2).astype(jnp.bfloat16)
    )
    key_rows = jnp.repeat(key_rows, repeat_times, axis=0)
    value_rows = jnp.repeat(value_rows, repeat_times, axis=0)
    scores = jnp.einsum(
        "hqd,hkd->hqk", query.astype(jnp.float32), key_rows.astype(jnp.float32)
    ) * HEAD_DIM ** (-0.5)
    scores = jnp.where(allowed[None], scores, -1e30)
    highest = jnp.max(scores, axis=-1, keepdims=True)
    weights = jnp.exp(scores - highest)
    probs = (weights / jnp.sum(weights, axis=-1, keepdims=True)).astype(jnp.bfloat16)
    attended = jnp.einsum(
        "hqk,hkd->hqd", probs.astype(jnp.float32), value_rows.astype(jnp.float32)
    ).astype(jnp.bfloat16)
    return attended.transpose(1, 0, 2).reshape(slot_count, -1)


def per_device(
    tokens,
    lengths,
    response,
    targets,
    attn_gain,
    w_query,
    w_key,
    w_value,
    output_weight,
    mlp_gain,
    w_gate,
    w_up,
    w_down,
    final_gain,
    w_head,
):
    group_rows = tokens.shape[0]
    own_rows = group_rows // lax.axis_size("mp")
    mp_index = lax.axis_index("mp")
    member, segment, positions = request_layout(lengths[0], group_rows)
    allowed = allowed_pairs(segment)
    heads_here = w_query.shape[2] // HEAD_DIM
    sharing = HEADS // KV_HEADS
    kv_here = max(1, heads_here // sharing)
    kv_first = mp_index * heads_here // sharing * HEAD_DIM
    key_cols = lax.dynamic_slice_in_dim(w_key, kv_first, kv_here * HEAD_DIM, 2)
    value_columns = lax.dynamic_slice_in_dim(w_value, kv_first, kv_here * HEAD_DIM, 2)
    attended_list = []
    for model in range(2):
        normed = rms_scale(tokens, attn_gain[model]).astype(jnp.bfloat16)
        query = jnp.dot(normed, w_query[model], preferred_element_type=jnp.float32)
        keys_here = jnp.dot(normed, key_cols[model], preferred_element_type=jnp.float32)
        values_here = jnp.dot(normed, value_columns[model], preferred_element_type=jnp.float32)
        attended_list.append(
            attend_heads(
                query, keys_here, values_here, positions, allowed, min(sharing, heads_here)
            )
        )
    attended = jnp.stack(attended_list, axis=1)
    selected_rows = attended
    mixed = lax.psum_scatter(
        jnp.einsum(
            "kbq,bqo->kbo", selected_rows, output_weight, preferred_element_type=jnp.float32
        ),
        "mp",
        scatter_dimension=0,
        tiled=True,
    )
    own_tokens = lax.dynamic_slice_in_dim(tokens, mp_index * own_rows, own_rows, 0)
    residual = own_tokens.astype(jnp.float32)[:, None, :] + mixed
    normed_mid = rms_scale(residual, mlp_gain).astype(jnp.bfloat16)
    row_block = lax.all_gather(normed_mid, "mp", axis=0, tiled=True)
    gate_part = jnp.einsum("nmd,mdf->nmf", row_block, w_gate, preferred_element_type=jnp.float32)
    lift_part = jnp.einsum("nmd,mdf->nmf", row_block, w_up, preferred_element_type=jnp.float32)
    hidden = (jax.nn.silu(gate_part) * lift_part).astype(jnp.bfloat16)
    selected_rows = hidden
    final = residual + lax.psum_scatter(
        jnp.einsum("nmf,mfd->nmd", selected_rows, w_down, preferred_element_type=jnp.float32),
        "mp",
        scatter_dimension=0,
        tiled=True,
    )
    closing = rms_scale(final, final_gain).astype(jnp.bfloat16)
    vocab_here = w_head.shape[2]
    vocab_first = lax.axis_index(("req", "mp")) * vocab_here
    column_ids = jnp.arange(vocab_here, dtype=jnp.int32)
    logits = jnp.einsum(
        "nmd,mdv->mnv",
        lax.all_gather(closing, ("req", "mp"), axis=0, tiled=True),
        w_head,
        preferred_element_type=jnp.float32,
    )
    peak_part = jnp.max(logits, axis=-1)
    total_part = jnp.sum(jnp.exp(logits - peak_part[..., None]), axis=-1)
    wanted = targets - vocab_first
    hit_part = jnp.sum(
        jnp.where(column_ids[None, None, :] == wanted[None, :, None], logits, 0.0), axis=-1
    )

    def join(first_stats, second_stats):
        peak_one, total_one, hit_one = first_stats
        peak_two, total_two, hit_two = second_stats
        highest = jnp.maximum(peak_one, peak_two)
        return (
            highest,
            total_one * jnp.exp(peak_one - highest) + total_two * jnp.exp(peak_two - highest),
            hit_one + hit_two,
        )

    peak_all, total_all, hit_all = merged((peak_part, total_part, hit_part), ("req", "mp"), join)
    log_likelihood = hit_all - (peak_all + jnp.log(total_all))
    gap = log_likelihood[0] - log_likelihood[1]
    group_gap = lax.dynamic_slice_in_dim(
        gap, lax.axis_index("req") * group_rows, group_rows, 0
    ) * response.astype(jnp.float32)
    token_out = lax.dynamic_slice_in_dim(group_gap, mp_index * own_rows, own_rows, 0)
    member_weights = member.astype(jnp.float32)
    request_sum = jnp.dot(group_gap, member_weights, precision=lax.Precision.HIGHEST)
    request_peak = jnp.max(member_weights * jnp.abs(group_gap)[:, None], axis=0)
    return (token_out, request_sum[None, :], request_peak[None, :])


def solution(mesh):
    placed = (
        P("req", None),
        P("req", None),
        P("req"),
        P(),
        P(),
        P(None, None, "mp"),
        P(),
        P(),
        P(None, "mp", None),
        P(),
        P(None, None, "mp"),
        P(None, None, "mp"),
        P(None, "mp", None),
        P(),
        P(None, None, ("req", "mp")),
    )
    return jax.shard_map(
        per_device,
        mesh=mesh,
        in_specs=placed,
        out_specs=(P(("req", "mp")), P("req", None), P("req", None)),
        check_vma=False,
    )
```

profile of v0, /device:TPU:1, one launch (start us, length us, event | category | flops | bytes accessed | tf_op | source)
XLA Modules:
  0.0 424.1 jit_solution(8450373626498625544)
XLA Ops:
  7.2 0.5 multiply_power_fusion
  7.8 1.6 fusion.10
  9.3 0.8 fusion.98
  10.2 0.8 reduce-window.4
  11.0 0.7 fusion.76
  11.8 2.7 slice_bitcast_fusion.1
  14.4 2.3 copy.34
  16.7 2.2 convolution_bitcast_fusion.5
  18.9 2.1 convolution_bitcast_fusion.4
  21.0 1.2 convolution_bitcast_fusion.2
  22.2 1.4 copy.32
  23.7 2.1 convolution_bitcast_fusion.3
  25.9 0.2 multiply_cosine_fusion.1
  26.1 0.2 fusion.65
  26.4 0.6 pad_maximum_fusion
  27.1 1.4 fusion.20
  28.4 0.5 fusion.105
  29.0 1.3 fusion.19
  30.3 1.1 fusion.100
  31.5 1.7 convolution_convert_fusion.3
  33.2 2.3 convolution_convert_fusion.2
  35.6 2.0 convolution_convert_fusion.1
  37.6 0.1 copy.36
  37.7 1.9 convolution_convert_fusion
  39.7 0.1 copy.37
  39.8 2.6 convolution_bitcast_fusion.1
  42.6 50.2 %reduce-scatter.3.cloned.1.call-done = f32[32,2,2048]{2,0,1:T(8,128)} async-done(((f32[256,2,2048]{2,0,1:T(8,128)}), f32[32,2,2048]{2,0,1:T(8,128)}) %reduce-scatter.3.cloned.1.call-update) | async-done | bytes 524304 | tf_op jit(solution)/shard_map/reduce_scatter | solution.py:127
  92.8 1.2 multiply_reduce_fusion.1
  93.9 1.9 multiply_convert_fusion.1
  95.9 0.2 reduce-scatter.5.cloned.1.call-start
  96.1 29.8 %all-gather.9.cloned.1.call-done = bf16[256,2,2048]{2,0,1:T(8,128)(2,1)} async-done(((bf16[32,2,2048]{2,0,1:T(8,128)(2,1)}), bf16[256,2,2048]{2,0,1:T(8,128)(2,1)}) %all-gather.9.cloned.1.call-update) | async-done | bytes 2097168 | tf_op jit(solution)/shard_map/all_gather | solution.py:138
  125.9 7.8 %fusion.111 = f32[2,256,1024]{2,1,0:T(8,128)} fusion(bf16[256,2,2048]{2,0,1:T(8,128)(2,1)} %all-gather.9.cloned.1.call-done, bf16[2,2048,1024]{2,1,0:T(8,128)(2,1)} %param.27), kind=kOutput, calls=%fused_computation.157 | convolution fusion | flops 2147483648 | bytes 12582912 | tf_op jit(solution)/shard_map/nmd,mdf->nmf/dot_general | solution.py:139
  133.7 13.1 %convolution_bitcast_fusion = f32[256,2,2048]{2,0,1:T(8,128)} fusion(bf16[2,1024,2048]{2,1,0:T(8,128)(2,1)} %param.29, f32[2,256,1024]{2,1,0:T(8,128)} %fusion.111, bf16[256,2,2048]{2,0,1:T(8,128)(2,1)S(1)} %copy-done.2, bf16[2,2048,1024]{2,1,0:T(8,128)(2,1)} %param.28), kind=kOutput, calls=%fused_computation.13 | convolution fusion | flops 4298113024 | bytes 25165824 | tf_op jit(solution)/shard_map/nmf,mfd->nmd/dot_general | solution.py:144
  146.9 0.3 all-gather.11.cloned.1.call-start
  147.1 46.9 %reduce-scatter.5.cloned.1.call-done = f32[32,2,2048]{2,0,1:T(8,128)} async-done(((f32[256,2,2048]{2,0,1:T(8,128)}), f32[32,2,2048]{2,0,1:T(8,128)}) %reduce-scatter.5.cloned.1.call-update) | async-done | bytes 524304 | tf_op jit(solution)/shard_map/reduce_scatter | solution.py:143
  194.1 1.2 multiply_reduce_fusion
  195.3 1.9 multiply_convert_fusion
  197.2 0.7 iota_compare_fusion
  197.9 77.4 %all-gather.11.cloned.1.call-done = bf16[1024,2,2048]{2,0,1:T(8,128)(2,1)} async-done(((bf16[32,2,2048]{2,0,1:T(8,128)(2,1)}), bf16[1024,2,2048]{2,0,1:T(8,128)(2,1)}) %all-gather.11.cloned.1.call-update) | async-done | bytes 8388624 | tf_op jit(solution)/shard_map/all_gather | solution.py:155
  275.4 16.9 %fusion.110 = (f32[2,1024]{1,0:T(2,128)S(1)}, f32[2,1024,1002]{1,2,0:T(8,128)}) fusion(bf16[1024,2,2048]{2,0,1:T(8,128)(2,1)} %all-gather.11.cloned.1.call-done, bf16[2,2048,1002]{1,0,2:T(2,128)(2,1)} %param.31), kind=kOutput, calls=%fused_computation.156 | convolution fusion | flops 8407435264 | bytes 24813568 | tf_op jit(solution)/shard_map/nmd,mdv->mnv/dot_general | solution.py:153
  292.2 4.6 %select_reduce_fusion = (f32[2,1024]{1,0:T(2,128)S(1)}, f32[2,1024]{1,0:T(2,128)S(1)}) fusion(f32[2,1024,1002]{1,2,0:T(8,128)} %get-tuple-element.228, pred[1024,1002]{0,1:T(8,128)(4,1)S(1)} %iota_compare_fusion, f32[2,1024]{1,0:T(2,128)S(1)} %get-tuple-element.227), kind=kLoop, calls=%fused_computation.10 | loop fusion | flops 8204288 | bytes 9259008 | tf_op jit(solution)/shard_map/reduce_sum | solution.py:162
  296.8 40.3 %all-gather.5 = f32[32,2,1024]{2,1,0:T(2,128)S(1)} all-gather(f32[1,2,1024]{2,1,0:T(2,128)S(1)} %bitcast.132), channel_id=4, replica_groups=mesh['req'=4,'mp'=8] {'req','mp'}, dimensions={0}, use_global_device_ids=true | all-gather | bytes 270336 | tf_op jit(solution)/shard_map/all_gather | solution.py:16
  337.1 37.7 %all-gather.4 = f32[32,2,1024]{2,1,0:T(2,128)S(1)} all-gather(f32[1,2,1024]{2,1,0:T(2,128)S(1)} %bitcast.131), channel_id=3, replica_groups=mesh['req'=4,'mp'=8] {'req','mp'}, dimensions={0}, use_global_device_ids=true | all-gather | bytes 270336 | tf_op jit(solution)/shard_map/all_gather | solution.py:16
  374.8 39.0 %all-gather.3 = f32[32,2,1024]{2,1,0:T(2,128)S(1)} all-gather(f32[1,2,1024]{2,1,0:T(2,128)S(1)} %bitcast.130), channel_id=2, replica_groups=mesh['req'=4,'mp'=8] {'req','mp'}, dimensions={0}, use_global_device_ids=true | all-gather | bytes 270336 | tf_op jit(solution)/shard_map/all_gather | solution.py:16
  413.8 1.7 while.19
  415.6 0.7 select_reduce_fusion.1
  416.3 0.6 dynamic_slice.65
  416.9 0.7 fusion.67
  (97 shorter events, 1.8 us)
Async XLA Ops:
  7.2 32.6 %copy-start = (bf16[2,256,2048]{2,1,0:T(8,128)(2,1)S(1)}, bf16[2,256,2048]{2,1,0:T(8,128)(2,1)}, u32[]{:S(2)}) copy-start(bf16[2,256,2048]{2,1,0:T(8,128)(2,1)} %param.25) | copy-start | bytes 6291460
  7.2 85.6 %reduce-scatter.3.cloned.1.call-start = ((), (), s32[]{:S(2)}) async-start(), calls=%async_computation.2 | async-start | bytes 4718592 | tf_op jit(solution)/shard_map/reduce_scatter | solution.py:127
  9.3 9.6 %copy-start.18 = (f32[256]{0:T(256)}, f32[256]{0:T(256)S(1)}, u32[]{:S(2)}) copy-start(f32[256]{0:T(256)S(1)} %add_rsqrt_fusion.2) | copy-start | bytes 3076
  10.1 6.6 %copy-start.10 = (f32[1,2048]{1,0:T(1,128)}, f32[1,2048]{1,0:T(1,128)S(1)}, u32[]{:S(2)}) copy-start(f32[1,2048]{1,0:T(1,128)S(1)} %get-tuple-element.219) | copy-start | bytes 24580
  11.0 3.4 copy-start.14
  11.7 2.8 copy-start.16
  16.7 4.3 %copy-start.4 = (bf16[256,2048]{1,0:T(8,128)(2,1)S(1)}, bf16[256,2048]{1,0:T(8,128)(2,1)}, u32[]{:S(2)}) copy-start(bf16[256,2048]{1,0:T(8,128)(2,1)} %param.17) | copy-start | bytes 3145732
  16.7 4.3 %copy-start.6 = (bf16[256,2048]{1,0:T(8,128)(2,1)S(1)}, bf16[256,2048]{1,0:T(8,128)(2,1)}, u32[]{:S(2)}) copy-start(bf16[256,2048]{1,0:T(8,128)(2,1)} %copy.34) | copy-start | bytes 3145732
  23.7 2.3 copy-start.13
  27.0 2.0 copy-start.7
  29.0 2.5 copy-start.5
  29.0 2.5 copy-start.11
  29.0 2.5 copy-start.19
  35.6 2.2 copy-start.21
  42.4 51.5 %copy-start.8 = (f32[2,2048]{1,0:T(2,128)S(1)}, f32[2,2048]{1,0:T(2,128)}, u32[]{:S(2)}) copy-start(f32[2,2048]{1,0:T(2,128)} %param.26) | copy-start | bytes 49156
  42.5 83.4 %all-gather.9.cloned.1.call-start = ((), (), s32[]{:S(2)}) async-start(), calls=%async_computation.3 | async-start | bytes 2359296 | tf_op jit(solution)/shard_map/all_gather | solution.py:138
  95.9 98.2 %reduce-scatter.5.cloned.1.call-start = ((), (), s32[]{:S(2)}) async-start(), calls=%async_computation.4 | async-start | bytes 4718592 | tf_op jit(solution)/shard_map/reduce_scatter | solution.py:143
  125.9 7.8 %copy-start.2 = (bf16[256,2,2048]{2,0,1:T(8,128)(2,1)S(1)}, bf16[256,2,2048]{2,0,1:T(8,128)(2,1)}, u32[]{:S(2)}) copy-start(bf16[256,2,2048]{2,0,1:T(8,128)(2,1)} %all-gather.9.cloned.1.call-done) | copy-start | bytes 6291460
  146.8 47.2 %copy-start.3 = (f32[32,2,2048]{2,0,1:T(8,128)S(1)}, f32[32,2,2048]{2,0,1:T(8,128)}, u32[]{:S(2)}) copy-start(f32[32,2,2048]{2,0,1:T(8,128)} %reduce-scatter.3.cloned.1.call-done) | copy-start | bytes 1572868
  146.8 48.4 %copy-start.9 = (f32[2,2048]{1,0:T(2,128)S(1)}, f32[2,2048]{1,0:T(2,128)}, u32[]{:S(2)}) copy-start(f32[2,2048]{1,0:T(2,128)} %param.30) | copy-start | bytes 49156
  146.9 50.3 %copy-start.12 = (s32[1024]{0:T(1024)S(1)}, s32[1024]{0:T(1024)}, u32[]{:S(2)}) copy-start(s32[1024]{0:T(1024)} %param.20) | copy-start | bytes 12292
  146.9 128.5 %all-gather.11.cloned.1.call-start = ((), (), s32[]{:S(2)}) async-start(), calls=%async_computation.5 | async-start | bytes 8650752 | tf_op jit(solution)/shard_map/all_gather | solution.py:155
  292.2 123.4 %copy-start.20 = (s32[256]{0:T(256)S(1)}, s32[256]{0:T(256)}, u32[]{:S(2)}) copy-start(s32[256]{0:T(256)} %param.19) | copy-start | bytes 3076
  292.2 123.4 %copy-start.15 = (s32[8,1]{0,1:T(1,128)S(1)}, s32[8,1]{0,1:T(1,128)}, u32[]{:S(2)}) copy-start(s32[8,1]{0,1:T(1,128)} %copy-done.14) | copy-start | bytes 100
  292.2 123.4 %copy-start.17 = (s32[8]{0:T(128)S(1)}, s32[8]{0:T(128)}, u32[]{:S(2)}) copy-start(s32[8]{0:T(128)} %copy-done.16) | copy-start | bytes 100
  292.2 125.4 %copy-start.1 = (bf16[2,256,2048]{2,1,0:T(8,128)(2,1)S(1)}, bf16[2,256,2048]{2,1,0:T(8,128)(2,1)}, u32[]{:S(2)}) copy-start(bf16[2,256,2048]{2,1,0:T(8,128)(2,1)} %param.25) | copy-start | bytes 6291460
Sparse Core Ops, SparseCore 0:
  42.6 50.1 reduce-scatter.2
  96.0 29.8 all-gather.8
  147.0 47.0 reduce-scatter.4
  197.3 78.0 all-gather.10
where the time goes:
time: 425 us; the launch traced here: 424 us
  waiting for transfers between devices  204 us (48%)
  blocking collectives  117 us (28%)
  matrix products  61.2 us (14%)
  other arithmetic  18.2 us (4%)
  between operations  14.1 us (3%)
  local copies, waits for them, and re-layouts  8.11 us (2%)
    all_gather x3, blocking collectives, merged(): gathered = jax.tree.map(lambda a: lax.all_gather(a, axis), part)  117 us
    all_gather x1, waiting for transfers between devices, per_device(): lax.all_gather(closing, ('req', 'mp'), axis=0, tiled=True)  77.4 us
    reduce_scatter x1, waiting for transfers between devices, per_device(): lax.psum_scatter(jnp.einsum('kbq,bqo->kbo', selected_rows, output_weight,...  50.2 us
    reduce_scatter x1, waiting for transfers between devices, per_device(): lax.psum_scatter(jnp.einsum('nmf,mfd->nmd', selected_rows, w_down, prefer...  46.9 us
    all_gather x1, waiting for transfers between devices, per_device(): row_block = lax.all_gather(normed_mid, 'mp', axis=0, tiled=True)  29.8 us
    dot_general x1, matrix products, per_device(): jnp.einsum('nmd,mdv->mnv', lax.all_gather(closing, ('req', 'mp'), axis=0,...  16.9 us
    dot_general x1, matrix products, per_device(): jnp.einsum('nmf,mfd->nmd', selected_rows, w_down, preferred_element_type=...  13.1 us
  transfers between devices with their start and end apart: 4, of which 4 were waited for; matrix products, arithmetic and copies ran while one was open for 0% of the time, Pallas kernels for 0%

commit v1 on v0

--- a/solution.py
+++ b/solution.py
@@ -163,22 +163,20 @@
         jnp.where(column_ids[None, None, :] == wanted[None, :, None], logits, 0.0), axis=-1
     )
 
-    def join(first_stats, second_stats):
-        peak_one, total_one, hit_one = first_stats
-        peak_two, total_two, hit_two = second_stats
-        highest = jnp.maximum(peak_one, peak_two)
-        return (
-            highest,
-            total_one * jnp.exp(peak_one - highest) + total_two * jnp.exp(peak_two - highest),
-            hit_one + hit_two,
-        )
-
-    peak_all, total_all, hit_all = merged((peak_part, total_part, hit_part), ("req", "mp"), join)
+    groups = lax.axis_size("req")
+    parts = lax.axis_size("mp")
+    stats = jnp.stack([peak_part, total_part, hit_part])
+    tenant_stats = stats.reshape(3, 2, groups, group_rows).transpose(2, 0, 1, 3)
+    outgoing = jnp.broadcast_to(
+        tenant_stats[:, None], (groups, parts, 3, 2, group_rows)
+    ).reshape(groups * parts, 3, 2, group_rows)
+    incoming = lax.all_to_all(outgoing, ("req", "mp"), 0, 0, tiled=True)
+    peak_all = jnp.max(incoming[:, 0], axis=0)
+    total_all = jnp.sum(incoming[:, 1] * jnp.exp(incoming[:, 0] - peak_all[None]), axis=0)
+    hit_all = jnp.sum(incoming[:, 2], axis=0)
     log_likelihood = hit_all - (peak_all + jnp.log(total_all))
     gap = log_likelihood[0] - log_likelihood[1]
-    group_gap = lax.dynamic_slice_in_dim(
-        gap, lax.axis_index("req") * group_rows, group_rows, 0
-    ) * response.astype(jnp.float32)
+    group_gap = gap * response.astype(jnp.float32)
     token_out = lax.dynamic_slice_in_dim(group_gap, mp_index * own_rows, own_rows, 0)
     member_weights = member.astype(jnp.float32)
     request_sum = jnp.dot(group_gap, member_weights, precision=lax.Precision.HIGHEST)

time: 425 us -> 319 us (0.75)
  blocking collectives: 117 us -> 12.3 us
    all_gather x3 -> x0, blocking collectives: 117 us -> none  [merged(): gathered = jax.tree.map(lambda a: lax.all_gather(a, axis), part)]
    all_to_all x0 -> x1, blocking collectives: none -> 12.3 us  [per_device(): incoming = lax.all_to_all(outgoing, ('req', 'mp'), 0, 0, tiled=True)]
where the time goes in v1:
time: 319 us; the launch traced here: 318 us
  waiting for transfers between devices  204 us (64%)
  matrix products  61.2 us (19%)
  other arithmetic  17.2 us (5%)
  between operations  14.2 us (4%)
  blocking collectives  12.3 us (4%)
  local copies, waits for them, and re-layouts  8.22 us (3%)
    all_gather x1, waiting for transfers between devices, per_device(): lax.all_gather(closing, ('req', 'mp'), axis=0, tiled=True)  77.4 us
    reduce_scatter x1, waiting for transfers between devices, per_device(): lax.psum_scatter(jnp.einsum('kbq,bqo->kbo', selected_rows, output_weight,...  50.2 us
    reduce_scatter x1, waiting for transfers between devices, per_device(): lax.psum_scatter(jnp.einsum('nmf,mfd->nmd', selected_rows, w_down, prefer...  46.9 us
    all_gather x1, waiting for transfers between devices, per_device(): row_block = lax.all_gather(normed_mid, 'mp', axis=0, tiled=True)  29.8 us
    dot_general x1, matrix products, per_device(): jnp.einsum('nmd,mdv->mnv', lax.all_gather(closing, ('req', 'mp'), axis=0,...  16.9 us
    dot_general x1, matrix products, per_device(): jnp.einsum('nmf,mfd->nmd', selected_rows, w_down, preferred_element_type=...  13.1 us
    all_to_all x1, blocking collectives, per_device(): incoming = lax.all_to_all(outgoing, ('req', 'mp'), 0, 0, tiled=True)  12.3 us
    dot_general x1, matrix products, per_device(): jnp.einsum('nmd,mdf->nmf', row_block, w_gate, preferred_element_type=jnp....  7.82 us
  transfers between devices with their start and end apart: 4, of which 4 were waited for; matrix products, arithmetic and copies ran while one was open for 0% of the time, Pallas kernels for 0%

profile of v1, /device:TPU:1, one launch (start us, length us, event | category | flops | bytes accessed | tf_op | source)
XLA Modules:
  0.0 318.0 jit_solution(12517944855225286087)
XLA Ops:
  7.2 0.5 multiply_power_fusion
  7.8 1.6 fusion.8
  9.3 0.8 fusion.98
  10.2 0.8 reduce-window.4
  11.0 0.7 fusion.76
  11.7 0.1 select_reduce_fusion.2
  11.8 2.7 slice_bitcast_fusion.1
  14.4 2.3 copy.36
  16.7 2.2 convolution_bitcast_fusion.5
  18.9 2.1 convolution_bitcast_fusion.4
  21.0 1.2 convolution_bitcast_fusion.2
  22.2 1.4 copy.34
  23.7 2.1 convolution_bitcast_fusion.3
  25.8 0.1 fusion.25
  25.9 0.2 multiply_cosine_fusion.1
  26.1 0.2 fusion.66
  26.4 0.6 pad_maximum_fusion
  27.1 1.4 fusion.18
  28.4 0.5 fusion.104
  29.0 1.3 fusion.17
  30.3 1.1 fusion.99
  31.5 1.7 convolution_convert_fusion.3
  33.2 2.3 convolution_convert_fusion.2
  35.6 2.0 convolution_convert_fusion.1
  37.6 0.1 copy.38
  37.7 1.9 convolution_convert_fusion
  39.7 0.1 copy.39
  39.8 2.6 convolution_bitcast_fusion.1
  42.6 50.2 %reduce-scatter.3.cloned.1.call-done = f32[32,2,2048]{2,0,1:T(8,128)} async-done(((f32[256,2,2048]{2,0,1:T(8,128)}), f32[32,2,2048]{2,0,1:T(8,128)}) %reduce-scatter.3.cloned.1.call-update) | async-done | bytes 524304 | tf_op jit(solution)/shard_map/reduce_scatter | solution.py:127
  92.8 1.2 multiply_reduce_fusion.1
  93.9 1.9 multiply_convert_fusion.1
  95.9 0.2 reduce-scatter.5.cloned.1.call-start
  96.1 29.8 %all-gather.3.cloned.1.call-done = bf16[256,2,2048]{2,0,1:T(8,128)(2,1)} async-done(((bf16[32,2,2048]{2,0,1:T(8,128)(2,1)}), bf16[256,2,2048]{2,0,1:T(8,128)(2,1)}) %all-gather.3.cloned.1.call-update) | async-done | bytes 2097168 | tf_op jit(solution)/shard_map/all_gather | solution.py:138
  125.9 7.8 %fusion.110 = f32[2,256,1024]{2,1,0:T(8,128)} fusion(bf16[256,2,2048]{2,0,1:T(8,128)(2,1)} %all-gather.3.cloned.1.call-done, bf16[2,2048,1024]{2,1,0:T(8,128)(2,1)} %param.25), kind=kOutput, calls=%fused_computation.153 | convolution fusion | flops 2147483648 | bytes 12582912 | tf_op jit(solution)/shard_map/nmd,mdf->nmf/dot_general | solution.py:139
  133.7 13.1 %convolution_bitcast_fusion = f32[256,2,2048]{2,0,1:T(8,128)} fusion(bf16[2,1024,2048]{2,1,0:T(8,128)(2,1)} %param.27, f32[2,256,1024]{2,1,0:T(8,128)} %fusion.110, bf16[256,2,2048]{2,0,1:T(8,128)(2,1)S(1)} %copy-done.2, bf16[2,2048,1024]{2,1,0:T(8,128)(2,1)} %param.26), kind=kOutput, calls=%fused_computation.7 | convolution fusion | flops 4298113024 | bytes 25165824 | tf_op jit(solution)/shard_map/nmf,mfd->nmd/dot_general | solution.py:144
  146.9 0.3 all-gather.5.cloned.1.call-start
  147.1 46.9 %reduce-scatter.5.cloned.1.call-done = f32[32,2,2048]{2,0,1:T(8,128)} async-done(((f32[256,2,2048]{2,0,1:T(8,128)}), f32[32,2,2048]{2,0,1:T(8,128)}) %reduce-scatter.5.cloned.1.call-update) | async-done | bytes 524304 | tf_op jit(solution)/shard_map/reduce_scatter | solution.py:143
  194.1 1.2 multiply_reduce_fusion
  195.3 1.9 multiply_convert_fusion
  197.2 0.7 iota_compare_fusion
  197.9 77.4 %all-gather.5.cloned.1.call-done = bf16[1024,2,2048]{2,0,1:T(8,128)(2,1)} async-done(((bf16[32,2,2048]{2,0,1:T(8,128)(2,1)}), bf16[1024,2,2048]{2,0,1:T(8,128)(2,1)}) %all-gather.5.cloned.1.call-update) | async-done | bytes 8388624 | tf_op jit(solution)/shard_map/all_gather | solution.py:155
  275.4 16.9 %fusion.109 = (f32[2,1024]{1,0:T(2,128)S(1)}, f32[2,1024,1002]{1,2,0:T(8,128)}) fusion(bf16[1024,2,2048]{2,0,1:T(8,128)(2,1)} %all-gather.5.cloned.1.call-done, bf16[2,2048,1002]{1,0,2:T(2,128)(2,1)} %param.29), kind=kOutput, calls=%fused_computation.152 | convolution fusion | flops 8407435264 | bytes 24813568 | tf_op jit(solution)/shard_map/nmd,mdv->mnv/dot_general | solution.py:153
  292.3 4.6 %exponential_reduce_fusion = (f32[2,1024]{1,0:T(2,128)S(1)}, f32[2,1024]{1,0:T(2,128)S(1)}) fusion(f32[2,1024,1002]{1,2,0:T(8,128)} %get-tuple-element.28, f32[2,1024]{1,0:T(2,128)S(1)} %get-tuple-element.27, pred[1024,1002]{0,1:T(8,128)(4,1)S(1)} %iota_compare_fusion), kind=kLoop, calls=%fused_computation.5 | loop fusion | flops 8204288 | bytes 9259008 | tf_op jit(solution)/shard_map/reduce_sum | solution.py:160
  297.0 12.3 %all_to_all.5 = f32[32,3,2,256]{3,2,1,0:T(2,128)S(1)} all-to-all(f32[32,3,2,256]{3,2,1,0:T(2,128)S(1)} %bitcast.121), channel_id=1, replica_groups=mesh['req'=4,'mp'=8] {'req','mp'}, dimensions={0} | all-to-all | bytes 393216 | tf_op jit(solution)/shard_map/all_to_all | solution.py:173
  309.3 0.1 fusion.37
  309.5 0.7 select_reduce_fusion.1
  310.2 0.6 dynamic_slice.15
  310.8 0.7 fusion.68
  (68 shorter events, 0.6 us)
Async XLA Ops:
  7.2 32.6 %copy-start = (bf16[2,256,2048]{2,1,0:T(8,128)(2,1)S(1)}, bf16[2,256,2048]{2,1,0:T(8,128)(2,1)}, u32[]{:S(2)}) copy-start(bf16[2,256,2048]{2,1,0:T(8,128)(2,1)} %param.23) | copy-start | bytes 6291460
  7.2 85.6 %reduce-scatter.3.cloned.1.call-start = ((), (), s32[]{:S(2)}) async-start(), calls=%async_computation.3 | async-start | bytes 4718592 | tf_op jit(solution)/shard_map/reduce_scatter | solution.py:127
  9.3 9.6 %copy-start.18 = (f32[256]{0:T(256)}, f32[256]{0:T(256)S(1)}, u32[]{:S(2)}) copy-start(f32[256]{0:T(256)S(1)} %add_rsqrt_fusion.2) | copy-start | bytes 3076
  10.1 6.6 %copy-start.10 = (f32[1,2048]{1,0:T(1,128)}, f32[1,2048]{1,0:T(1,128)S(1)}, u32[]{:S(2)}) copy-start(f32[1,2048]{1,0:T(1,128)S(1)} %get-tuple-element.21) | copy-start | bytes 24580
  11.0 3.4 %copy-start.14 = (s32[8,1]{0,1:T(1,128)}, s32[8,1]{0,1:T(1,128)S(1)}, u32[]{:S(2)}) copy-start(s32[8,1]{0,1:T(1,128)S(1)} %reduce-window.4) | copy-start | bytes 100
  11.7 2.8 copy-start.16
  16.7 4.3 %copy-start.4 = (bf16[256,2048]{1,0:T(8,128)(2,1)S(1)}, bf16[256,2048]{1,0:T(8,128)(2,1)}, u32[]{:S(2)}) copy-start(bf16[256,2048]{1,0:T(8,128)(2,1)} %param.15) | copy-start | bytes 3145732
  16.7 4.3 %copy-start.6 = (bf16[256,2048]{1,0:T(8,128)(2,1)S(1)}, bf16[256,2048]{1,0:T(8,128)(2,1)}, u32[]{:S(2)}) copy-start(bf16[256,2048]{1,0:T(8,128)(2,1)} %copy.36) | copy-start | bytes 3145732
  23.7 2.3 copy-start.13
  27.0 2.0 copy-start.7
  29.0 2.5 copy-start.5
  29.0 2.5 copy-start.11
  29.0 2.5 copy-start.19
  35.6 2.2 copy-start.21
  42.4 51.5 %copy-start.8 = (f32[2,2048]{1,0:T(2,128)S(1)}, f32[2,2048]{1,0:T(2,128)}, u32[]{:S(2)}) copy-start(f32[2,2048]{1,0:T(2,128)} %param.24) | copy-start | bytes 49156
  42.5 83.4 %all-gather.3.cloned.1.call-start = ((), (), s32[]{:S(2)}) async-start(), calls=%async_computation.4 | async-start | bytes 2359296 | tf_op jit(solution)/shard_map/all_gather | solution.py:138
  95.9 98.2 %reduce-scatter.5.cloned.1.call-start = ((), (), s32[]{:S(2)}) async-start(), calls=%async_computation.5 | async-start | bytes 4718592 | tf_op jit(solution)/shard_map/reduce_scatter | solution.py:143
  125.9 7.8 %copy-start.2 = (bf16[256,2,2048]{2,0,1:T(8,128)(2,1)S(1)}, bf16[256,2,2048]{2,0,1:T(8,128)(2,1)}, u32[]{:S(2)}) copy-start(bf16[256,2,2048]{2,0,1:T(8,128)(2,1)} %all-gather.3.cloned.1.call-done) | copy-start | bytes 6291460
  146.8 47.2 %copy-start.3 = (f32[32,2,2048]{2,0,1:T(8,128)S(1)}, f32[32,2,2048]{2,0,1:T(8,128)}, u32[]{:S(2)}) copy-start(f32[32,2,2048]{2,0,1:T(8,128)} %reduce-scatter.3.cloned.1.call-done) | copy-start | bytes 1572868
  146.8 48.4 %copy-start.9 = (f32[2,2048]{1,0:T(2,128)S(1)}, f32[2,2048]{1,0:T(2,128)}, u32[]{:S(2)}) copy-start(f32[2,2048]{1,0:T(2,128)} %param.28) | copy-start | bytes 49156
  146.9 50.3 %copy-start.12 = (s32[1024]{0:T(1024)S(1)}, s32[1024]{0:T(1024)}, u32[]{:S(2)}) copy-start(s32[1024]{0:T(1024)} %param.18) | copy-start | bytes 12292
  146.9 128.5 %all-gather.5.cloned.1.call-start = ((), (), s32[]{:S(2)}) async-start(), calls=%async_computation.6 | async-start | bytes 8650752 | tf_op jit(solution)/shard_map/all_gather | solution.py:155
  292.2 17.2 %copy-start.20 = (s32[256]{0:T(256)S(1)}, s32[256]{0:T(256)}, u32[]{:S(2)}) copy-start(s32[256]{0:T(256)} %param.17) | copy-start | bytes 3076
  292.2 17.2 %copy-start.15 = (s32[8,1]{0,1:T(1,128)S(1)}, s32[8,1]{0,1:T(1,128)}, u32[]{:S(2)}) copy-start(s32[8,1]{0,1:T(1,128)} %copy-done.14) | copy-start | bytes 100
  292.3 17.2 %copy-start.17 = (s32[8]{0:T(128)S(1)}, s32[8]{0:T(128)}, u32[]{:S(2)}) copy-start(s32[8]{0:T(128)} %copy-done.16) | copy-start | bytes 100
  292.3 19.2 %copy-start.1 = (bf16[2,256,2048]{2,1,0:T(8,128)(2,1)S(1)}, bf16[2,256,2048]{2,1,0:T(8,128)(2,1)}, u32[]{:S(2)}) copy-start(bf16[2,256,2048]{2,1,0:T(8,128)(2,1)} %param.23) | copy-start | bytes 6291460
Sparse Core Ops, SparseCore 0:
  42.6 50.1 reduce-scatter.2
  96.0 29.8 all-gather.2
  147.0 47.0 reduce-scatter.4
  197.3 78.0 all-gather.4

commit v2 on v1

--- a/solution.py
+++ b/solution.py
@@ -127,11 +127,11 @@
     mixed = lax.psum_scatter(
         jnp.einsum(
             "kbq,bqo->kbo", selected_rows, output_weight, preferred_element_type=jnp.float32
-        ),
+        ).astype(jnp.bfloat16),
         "mp",
         scatter_dimension=0,
         tiled=True,
-    )
+    ).astype(jnp.float32)
     own_tokens = lax.dynamic_slice_in_dim(tokens, mp_index * own_rows, own_rows, 0)
     residual = own_tokens.astype(jnp.float32)[:, None, :] + mixed
     normed_mid = rms_scale(residual, mlp_gain).astype(jnp.bfloat16)
@@ -141,11 +141,13 @@
     hidden = (jax.nn.silu(gate_part) * lift_part).astype(jnp.bfloat16)
     selected_rows = hidden
     final = residual + lax.psum_scatter(
-        jnp.einsum("nmf,mfd->nmd", selected_rows, w_down, preferred_element_type=jnp.float32),
+        jnp.einsum(
+            "nmf,mfd->nmd", selected_rows, w_down, preferred_element_type=jnp.float32
+        ).astype(jnp.bfloat16),
         "mp",
         scatter_dimension=0,
         tiled=True,
-    )
+    ).astype(jnp.float32)
     closing = rms_scale(final, final_gain).astype(jnp.bfloat16)
     vocab_here = w_head.shape[2]
     vocab_first = lax.axis_index(("req", "mp")) * vocab_here

time: 319 us -> 290 us (0.909)
  waiting for transfers between devices: 204 us -> 177 us
    reduce_scatter x1, waiting for transfers between devices: 50.2 us -> 35.4 us  [per_device(): lax.psum_scatter(jnp.einsum('kbq,bqo->kbo', selected_rows, output_weight,...]
    reduce_scatter x1, waiting for transfers between devices: 46.9 us -> 32.2 us  [per_device(): lax.psum_scatter(jnp.einsum('nmf,mfd->nmd', selected_rows, w_down, prefer...]
where the time goes in v2:
time: 290 us; the launch traced here: 289 us
  waiting for transfers between devices  177 us (61%)
  matrix products  60 us (21%)
  other arithmetic  16.9 us (6%)
  between operations  14.1 us (5%)
  blocking collectives  12.3 us (4%)
  local copies, waits for them, and re-layouts  8.22 us (3%)
    all_gather x1, waiting for transfers between devices, per_device(): lax.all_gather(closing, ('req', 'mp'), axis=0, tiled=True)  78.3 us
    reduce_scatter x1, waiting for transfers between devices, per_device(): lax.psum_scatter(jnp.einsum('kbq,bqo->kbo', selected_rows, output_weight,...  35.4 us
    reduce_scatter x1, waiting for transfers between devices, per_device(): lax.psum_scatter(jnp.einsum('nmf,mfd->nmd', selected_rows, w_down, prefer...  32.2 us
    all_gather x1, waiting for transfers between devices, per_device(): row_block = lax.all_gather(normed_mid, 'mp', axis=0, tiled=True)  30.9 us
    dot_general x1, matrix products, per_device(): jnp.einsum('nmd,mdv->mnv', lax.all_gather(closing, ('req', 'mp'), axis=0,...  16.9 us
    dot_general x1, matrix products, per_device(): jnp.einsum('nmf,mfd->nmd', selected_rows, w_down, preferred_element_type=...  12.5 us
    all_to_all x1, blocking collectives, per_device(): incoming = lax.all_to_all(outgoing, ('req', 'mp'), 0, 0, tiled=True)  12.3 us
    dot_general x1, matrix products, per_device(): jnp.einsum('nmd,mdf->nmf', row_block, w_gate, preferred_element_type=jnp....  7.79 us
  transfers between devices with their start and end apart: 4, of which 4 were waited for; matrix products, arithmetic and copies ran while one was open for 0% of the time, Pallas kernels for 0%

profile of v2, /device:TPU:1, one launch (start us, length us, event | category | flops | bytes accessed | tf_op | source)
XLA Modules:
  0.0 289.0 jit_solution(9929756520780141737)
XLA Ops:
  7.2 0.5 multiply_power_fusion
  7.8 1.6 fusion.10
  9.3 0.8 fusion.100
  10.2 0.8 reduce-window.4
  11.0 0.7 fusion.78
  11.7 0.1 select_reduce_fusion.2
  11.8 2.7 slice_bitcast_fusion.1
  14.4 2.3 copy.36
  16.7 2.2 convolution_bitcast_fusion.3
  18.9 2.1 convolution_bitcast_fusion.2
  21.0 1.2 convolution_bitcast_fusion
  22.2 1.4 copy.34
  23.7 2.1 convolution_bitcast_fusion.1
  25.8 0.1 fusion.27
  25.9 0.2 multiply_cosine_fusion.1
  26.1 0.2 fusion.68
  26.4 0.6 pad_maximum_fusion
  27.1 1.4 fusion.20
  28.4 0.5 fusion.106
  29.0 1.3 fusion.19
  30.3 1.1 fusion.101
  31.5 1.7 convolution_convert_fusion.5
  33.2 2.3 convolution_convert_fusion.4
  35.6 2.0 convolution_convert_fusion.3
  37.6 0.1 copy.38
  37.7 1.9 convolution_convert_fusion.2
  39.7 0.1 copy.39
  39.8 2.1 fusion.4
  42.0 35.4 %reduce-scatter.3.cloned.1.call-done = bf16[32,2,2048]{2,0,1:T(8,128)(2,1)} async-done(((bf16[256,2,2048]{2,0,1:T(8,128)(2,1)}), bf16[32,2,2048]{2,0,1:T(8,128)(2,1)}) %reduce-scatter.3.cloned.1.call-update) | async-done | bytes 262160 | tf_op jit(solution)/shard_map/reduce_scatter | solution.py:127
  77.4 1.1 multiply_reduce_fusion.1
  78.5 1.8 multiply_convert_fusion.1
  80.3 0.2 reduce-scatter.5.cloned.1.call-start
  80.5 30.9 %all-gather.3.cloned.1.call-done = bf16[256,2,2048]{2,0,1:T(8,128)(2,1)} async-done(((bf16[32,2,2048]{2,0,1:T(8,128)(2,1)}), bf16[256,2,2048]{2,0,1:T(8,128)(2,1)}) %all-gather.3.cloned.1.call-update) | async-done | bytes 2097168 | tf_op jit(solution)/shard_map/all_gather | solution.py:138
  111.4 7.8 %fusion.112 = f32[2,256,1024]{2,1,0:T(8,128)} fusion(bf16[256,2,2048]{2,0,1:T(8,128)(2,1)} %all-gather.3.cloned.1.call-done, bf16[2,2048,1024]{2,1,0:T(8,128)(2,1)} %param.25), kind=kOutput, calls=%fused_computation.156 | convolution fusion | flops 2147483648 | bytes 12582912 | tf_op jit(solution)/shard_map/nmd,mdf->nmf/dot_general | solution.py:139
  119.2 12.5 %fusion.5 = bf16[256,2,2048]{2,0,1:T(8,128)(2,1)} fusion(bf16[2,1024,2048]{2,1,0:T(8,128)(2,1)} %param.27, f32[2,256,1024]{2,1,0:T(8,128)} %fusion.112, bf16[256,2,2048]{2,0,1:T(8,128)(2,1)S(1)} %copy-done.2, bf16[2,2048,1024]{2,1,0:T(8,128)(2,1)} %param.26), kind=kOutput, calls=%fused_computation.10 | convolution fusion | flops 4299161600 | bytes 23068672 | tf_op jit(solution)/shard_map/nmf,mfd->nmd/dot_general | solution.py:144
  131.8 0.3 all-gather.5.cloned.1.call-start
  132.1 32.2 %reduce-scatter.5.cloned.1.call-done = bf16[32,2,2048]{2,0,1:T(8,128)(2,1)} async-done(((bf16[256,2,2048]{2,0,1:T(8,128)(2,1)}), bf16[32,2,2048]{2,0,1:T(8,128)(2,1)}) %reduce-scatter.5.cloned.1.call-update) | async-done | bytes 262160 | tf_op jit(solution)/shard_map/reduce_scatter | solution.py:143
  164.3 1.1 multiply_reduce_fusion
  165.5 1.8 multiply_convert_fusion
  167.3 0.7 iota_compare_fusion
  168.0 78.3 %all-gather.5.cloned.1.call-done = bf16[1024,2,2048]{2,0,1:T(8,128)(2,1)} async-done(((bf16[32,2,2048]{2,0,1:T(8,128)(2,1)}), bf16[1024,2,2048]{2,0,1:T(8,128)(2,1)}) %all-gather.5.cloned.1.call-update) | async-done | bytes 8388624 | tf_op jit(solution)/shard_map/all_gather | solution.py:157
  246.3 16.9 %fusion.111 = (f32[2,1024]{1,0:T(2,128)S(1)}, f32[2,1024,1002]{1,2,0:T(8,128)}) fusion(bf16[1024,2,2048]{2,0,1:T(8,128)(2,1)} %all-gather.5.cloned.1.call-done, bf16[2,2048,1002]{1,0,2:T(2,128)(2,1)} %param.29), kind=kOutput, calls=%fused_computation.155 | convolution fusion | flops 8407435264 | bytes 24813568 | tf_op jit(solution)/shard_map/nmd,mdv->mnv/dot_general | solution.py:155
  263.3 4.6 %exponential_reduce_fusion = (f32[2,1024]{1,0:T(2,128)S(1)}, f32[2,1024]{1,0:T(2,128)S(1)}) fusion(f32[2,1024,1002]{1,2,0:T(8,128)} %get-tuple-element.28, f32[2,1024]{1,0:T(2,128)S(1)} %get-tuple-element.27, pred[1024,1002]{0,1:T(8,128)(4,1)S(1)} %iota_compare_fusion), kind=kLoop, calls=%fused_computation.5 | loop fusion | flops 8204288 | bytes 9259008 | tf_op jit(solution)/shard_map/reduce_sum | solution.py:162
  268.0 12.3 %all_to_all.5 = f32[32,3,2,256]{3,2,1,0:T(2,128)S(1)} all-to-all(f32[32,3,2,256]{3,2,1,0:T(2,128)S(1)} %bitcast.121), channel_id=1, replica_groups=mesh['req'=4,'mp'=8] {'req','mp'}, dimensions={0} | all-to-all | bytes 393216 | tf_op jit(solution)/shard_map/all_to_all | solution.py:175
  280.3 0.1 fusion.39
  280.5 0.7 select_reduce_fusion.1
  281.2 0.6 dynamic_slice.15
  281.7 0.7 fusion.70
  (68 shorter events, 0.6 us)
Async XLA Ops:
  7.2 32.6 %copy-start = (bf16[2,256,2048]{2,1,0:T(8,128)(2,1)S(1)}, bf16[2,256,2048]{2,1,0:T(8,128)(2,1)}, u32[]{:S(2)}) copy-start(bf16[2,256,2048]{2,1,0:T(8,128)(2,1)} %param.23) | copy-start | bytes 6291460
  7.2 70.2 %reduce-scatter.3.cloned.1.call-start = ((), (), s32[]{:S(2)}) async-start(), calls=%async_computation.3 | async-start | bytes 2359296 | tf_op jit(solution)/shard_map/reduce_scatter | solution.py:127
  9.3 9.6 %copy-start.18 = (f32[256]{0:T(256)}, f32[256]{0:T(256)S(1)}, u32[]{:S(2)}) copy-start(f32[256]{0:T(256)S(1)} %add_rsqrt_fusion.2) | copy-start | bytes 3076
  10.1 6.6 %copy-start.10 = (f32[1,2048]{1,0:T(1,128)}, f32[1,2048]{1,0:T(1,128)S(1)}, u32[]{:S(2)}) copy-start(f32[1,2048]{1,0:T(1,128)S(1)} %get-tuple-element.21) | copy-start | bytes 24580
  11.0 3.4 %copy-start.14 = (s32[8,1]{0,1:T(1,128)}, s32[8,1]{0,1:T(1,128)S(1)}, u32[]{:S(2)}) copy-start(s32[8,1]{0,1:T(1,128)S(1)} %reduce-window.4) | copy-start | bytes 100
  11.7 2.8 copy-start.16
  16.7 4.3 %copy-start.4 = (bf16[256,2048]{1,0:T(8,128)(2,1)S(1)}, bf16[256,2048]{1,0:T(8,128)(2,1)}, u32[]{:S(2)}) copy-start(bf16[256,2048]{1,0:T(8,128)(2,1)} %param.15) | copy-start | bytes 3145732
  16.7 4.3 %copy-start.6 = (bf16[256,2048]{1,0:T(8,128)(2,1)S(1)}, bf16[256,2048]{1,0:T(8,128)(2,1)}, u32[]{:S(2)}) copy-start(bf16[256,2048]{1,0:T(8,128)(2,1)} %copy.36) | copy-start | bytes 3145732
  23.7 2.3 copy-start.13
  27.0 2.0 copy-start.7
  29.0 2.5 copy-start.5
  29.0 2.5 copy-start.11
  29.0 2.5 copy-start.19
  35.6 2.2 copy-start.21
  41.9 36.6 %copy-start.9 = (f32[2,2048]{1,0:T(2,128)S(1)}, f32[2,2048]{1,0:T(2,128)}, u32[]{:S(2)}) copy-start(f32[2,2048]{1,0:T(2,128)} %param.24) | copy-start | bytes 49156
  41.9 69.5 %all-gather.3.cloned.1.call-start = ((), (), s32[]{:S(2)}) async-start(), calls=%async_computation.4 | async-start | bytes 2359296 | tf_op jit(solution)/shard_map/all_gather | solution.py:138
  80.3 84.0 %reduce-scatter.5.cloned.1.call-start = ((), (), s32[]{:S(2)}) async-start(), calls=%async_computation.5 | async-start | bytes 2359296 | tf_op jit(solution)/shard_map/reduce_scatter | solution.py:143
  111.4 7.8 %copy-start.2 = (bf16[256,2,2048]{2,0,1:T(8,128)(2,1)S(1)}, bf16[256,2,2048]{2,0,1:T(8,128)(2,1)}, u32[]{:S(2)}) copy-start(bf16[256,2,2048]{2,0,1:T(8,128)(2,1)} %all-gather.3.cloned.1.call-done) | copy-start | bytes 6291460
  131.8 32.5 %copy-start.3 = (bf16[32,2,2048]{2,0,1:T(8,128)(2,1)S(1)}, bf16[32,2,2048]{2,0,1:T(8,128)(2,1)}, u32[]{:S(2)}) copy-start(bf16[32,2,2048]{2,0,1:T(8,128)(2,1)} %reduce-scatter.3.cloned.1.call-done) | copy-start | bytes 786436
  131.8 33.7 %copy-start.8 = (f32[2,2048]{1,0:T(2,128)S(1)}, f32[2,2048]{1,0:T(2,128)}, u32[]{:S(2)}) copy-start(f32[2,2048]{1,0:T(2,128)} %param.28) | copy-start | bytes 49156
  131.8 35.5 %copy-start.12 = (s32[1024]{0:T(1024)S(1)}, s32[1024]{0:T(1024)}, u32[]{:S(2)}) copy-start(s32[1024]{0:T(1024)} %param.18) | copy-start | bytes 12292
  131.8 114.5 %all-gather.5.cloned.1.call-start = ((), (), s32[]{:S(2)}) async-start(), calls=%async_computation.6 | async-start | bytes 8650752 | tf_op jit(solution)/shard_map/all_gather | solution.py:157
  263.2 17.2 %copy-start.20 = (s32[256]{0:T(256)S(1)}, s32[256]{0:T(256)}, u32[]{:S(2)}) copy-start(s32[256]{0:T(256)} %param.17) | copy-start | bytes 3076
  263.2 17.2 %copy-start.15 = (s32[8,1]{0,1:T(1,128)S(1)}, s32[8,1]{0,1:T(1,128)}, u32[]{:S(2)}) copy-start(s32[8,1]{0,1:T(1,128)} %copy-done.14) | copy-start | bytes 100
  263.2 17.2 %copy-start.17 = (s32[8]{0:T(128)S(1)}, s32[8]{0:T(128)}, u32[]{:S(2)}) copy-start(s32[8]{0:T(128)} %copy-done.16) | copy-start | bytes 100
  263.2 19.2 %copy-start.1 = (bf16[2,256,2048]{2,1,0:T(8,128)(2,1)S(1)}, bf16[2,256,2048]{2,1,0:T(8,128)(2,1)}, u32[]{:S(2)}) copy-start(bf16[2,256,2048]{2,1,0:T(8,128)(2,1)} %param.23) | copy-start | bytes 6291460
Sparse Core Ops, SparseCore 0:
  42.0 35.3 reduce-scatter.2
  80.4 30.9 all-gather.2
  131.9 32.3 reduce-scatter.4
  167.4 78.9 all-gather.4

commit v3 on v1

--- a/solution.py
+++ b/solution.py
@@ -111,61 +111,58 @@
     kv_first = mp_index * heads_here // sharing * HEAD_DIM
     key_cols = lax.dynamic_slice_in_dim(w_key, kv_first, kv_here * HEAD_DIM, 2)
     value_columns = lax.dynamic_slice_in_dim(w_value, kv_first, kv_here * HEAD_DIM, 2)
-    attended_list = []
+    own_tokens = lax.dynamic_slice_in_dim(tokens, mp_index * own_rows, own_rows, 0)
+    vocab_here = w_head.shape[2]
+    vocab_first = lax.axis_index(("req", "mp")) * vocab_here
+    column_ids = jnp.arange(vocab_here, dtype=jnp.int32)
+    wanted = targets - vocab_first
+    per_model = []
     for model in range(2):
         normed = rms_scale(tokens, attn_gain[model]).astype(jnp.bfloat16)
         query = jnp.dot(normed, w_query[model], preferred_element_type=jnp.float32)
         keys_here = jnp.dot(normed, key_cols[model], preferred_element_type=jnp.float32)
         values_here = jnp.dot(normed, value_columns[model], preferred_element_type=jnp.float32)
-        attended_list.append(
-            attend_heads(
-                query, keys_here, values_here, positions, allowed, min(sharing, heads_here)
-            )
+        attended = attend_heads(
+            query, keys_here, values_here, positions, allowed, min(sharing, heads_here)
         )
-    attended = jnp.stack(attended_list, axis=1)
-    selected_rows = attended
-    mixed = lax.psum_scatter(
-        jnp.einsum(
-            "kbq,bqo->kbo", selected_rows, output_weight, preferred_element_type=jnp.float32
-        ),
-        "mp",
-        scatter_dimension=0,
-        tiled=True,
-    )
-    own_tokens = lax.dynamic_slice_in_dim(tokens, mp_index * own_rows, own_rows, 0)
-    residual = own_tokens.astype(jnp.float32)[:, None, :] + mixed
-    normed_mid = rms_scale(residual, mlp_gain).astype(jnp.bfloat16)
-    row_block = lax.all_gather(normed_mid, "mp", axis=0, tiled=True)
-    gate_part = jnp.einsum("nmd,mdf->nmf", row_block, w_gate, preferred_element_type=jnp.float32)
-    lift_part = jnp.einsum("nmd,mdf->nmf", row_block, w_up, preferred_element_type=jnp.float32)
-    hidden = (jax.nn.silu(gate_part) * lift_part).astype(jnp.bfloat16)
-    selected_rows = hidden
-    final = residual + lax.psum_scatter(
-        jnp.einsum("nmf,mfd->nmd", selected_rows, w_down, preferred_element_type=jnp.float32),
-        "mp",
-        scatter_dimension=0,
-        tiled=True,
-    )
-    closing = rms_scale(final, final_gain).astype(jnp.bfloat16)
-    vocab_here = w_head.shape[2]
-    vocab_first = lax.axis_index(("req", "mp")) * vocab_here
-    column_ids = jnp.arange(vocab_here, dtype=jnp.int32)
-    logits = jnp.einsum(
-        "nmd,mdv->mnv",
-        lax.all_gather(closing, ("req", "mp"), axis=0, tiled=True),
-        w_head,
-        preferred_element_type=jnp.float32,
-    )
-    peak_part = jnp.max(logits, axis=-1)
-    total_part = jnp.sum(jnp.exp(logits - peak_part[..., None]), axis=-1)
-    wanted = targets - vocab_first
-    hit_part = jnp.sum(
-        jnp.where(column_ids[None, None, :] == wanted[None, :, None], logits, 0.0), axis=-1
-    )
+        mixed = lax.psum_scatter(
+            jnp.dot(
+                attended, output_weight[model], preferred_element_type=jnp.float32
+            ).astype(jnp.bfloat16),
+            "mp",
+            scatter_dimension=0,
+            tiled=True,
+        ).astype(jnp.float32)
+        residual = own_tokens.astype(jnp.float32) + mixed
+        normed_mid = rms_scale(residual, mlp_gain[model]).astype(jnp.bfloat16)
+        row_block = lax.all_gather(normed_mid, "mp", axis=0, tiled=True)
+        gate_part = jnp.dot(row_block, w_gate[model], preferred_element_type=jnp.float32)
+        lift_part = jnp.dot(row_block, w_up[model], preferred_element_type=jnp.float32)
+        hidden = (jax.nn.silu(gate_part) * lift_part).astype(jnp.bfloat16)
+        final = residual + lax.psum_scatter(
+            jnp.dot(hidden, w_down[model], preferred_element_type=jnp.float32).astype(
+                jnp.bfloat16
+            ),
+            "mp",
+            scatter_dimension=0,
+            tiled=True,
+        ).astype(jnp.float32)
+        closing = rms_scale(final, final_gain[model]).astype(jnp.bfloat16)
+        logits = jnp.dot(
+            lax.all_gather(closing, ("req", "mp"), axis=0, tiled=True),
+            w_head[model],
+            preferred_element_type=jnp.float32,
+        )
+        peak_part = jnp.max(logits, axis=-1)
+        total_part = jnp.sum(jnp.exp(logits - peak_part[:, None]), axis=-1)
+        hit_part = jnp.sum(
+            jnp.where(column_ids[None, :] == wanted[:, None], logits, 0.0), axis=-1
+        )
+        per_model.append(jnp.stack([peak_part, total_part, hit_part]))
 
     groups = lax.axis_size("req")
     parts = lax.axis_size("mp")
-    stats = jnp.stack([peak_part, total_part, hit_part])
+    stats = jnp.stack(per_model, axis=1)
     tenant_stats = stats.reshape(3, 2, groups, group_rows).transpose(2, 0, 1, 3)
     outgoing = jnp.broadcast_to(
         tenant_stats[:, None], (groups, parts, 3, 2, group_rows)

time: 319 us -> 390 us (1.22)
  waiting for transfers between devices: 204 us -> 252 us
  local copies, waits for them, and re-layouts: 8.22 us -> 23.2 us
  matrix products: 61.2 us -> 67.9 us
    all_gather x1 -> x2, waiting for transfers between devices: 77.4 us -> 97.7 us  [per_device(): lax.all_gather(closing, ('req', 'mp'), axis=0, tiled=True)]
    slice x0 -> x3, local copies, waits for them, and re-layouts: none -> 17.3 us  [the longest x1 17.2 us: per_device(): w_head[model]]
    reduce_scatter x2 -> x4, waiting for transfers between devices: 97.1 us -> 112 us  [the longest x2 61.4 us: per_device(): lax.psum_scatter(jnp.dot(hidden, w_down[model], preferred_element_type=jn...]
    all_gather x1 -> x2, waiting for transfers between devices: 29.8 us -> 41.4 us  [per_device(): row_block = lax.all_gather(normed_mid, 'mp', axis=0, tiled=True)]
    dot_general x4 -> x8, matrix products: 40.4 us -> 47.9 us  [the longest x2 22 us: per_device(): jnp.dot(lax.all_gather(closing, ('req', 'mp'), axis=0, tiled=True), w_hea...]
  transfers between devices with their start and end apart: 4 -> 8, of which waited for: 4 -> 8; matrix products, arithmetic and copies ran while one was open for 0% -> 12% of each run, Pallas kernels for 0% -> 0%
where the time goes in v3:
time: 390 us
  waiting for transfers between devices  252 us (65%)
  matrix products  67.9 us (17%)
  local copies, waits for them, and re-layouts  23.2 us (6%)
  other arithmetic  18.7 us (5%)
  between operations  14.5 us (4%)
  blocking collectives  12.5 us (3%)
    all_gather x2, waiting for transfers between devices, per_device(): lax.all_gather(closing, ('req', 'mp'), axis=0, tiled=True)  97.7 us
    reduce_scatter x2, waiting for transfers between devices, per_device(): lax.psum_scatter(jnp.dot(hidden, w_down[model], preferred_element_type=jn...  61.4 us
    reduce_scatter x2, waiting for transfers between devices, per_device(): lax.psum_scatter(jnp.dot(attended, output_weight[model], preferred_elemen...  50.9 us
    all_gather x2, waiting for transfers between devices, per_device(): row_block = lax.all_gather(normed_mid, 'mp', axis=0, tiled=True)  41.4 us
    dot_general x2, matrix products, per_device(): jnp.dot(lax.all_gather(closing, ('req', 'mp'), axis=0, tiled=True), w_hea...  22 us
    slice x1, local copies, waits for them, and re-layouts, per_device(): w_head[model]  17.2 us
    dot_general x2, matrix products, per_device(): jnp.dot(hidden, w_down[model], preferred_element_type=jnp.float32)  14.2 us
    all_to_all x1, blocking collectives, per_device(): incoming = lax.all_to_all(outgoing, ('req', 'mp'), 0, 0, tiled=True)  12.5 us
  transfers between devices with their start and end apart: 8, of which 8 were waited for; matrix products, arithmetic and copies ran while one was open for 12% of the time, Pallas kernels for 0%

profile of v3, /device:TPU:1, one launch (start us, length us, event | category | flops | bytes accessed | tf_op | source)
XLA Modules:
  0.0 389.6 jit_solution(17589801425028379562)
XLA Ops:
  7.8 1.5 fusion.32
  9.3 0.8 fusion.139
  10.1 0.8 reduce-window.4
  10.9 0.7 fusion.114
  11.7 1.7 slice_bitcast_fusion.1
  13.4 1.4 copy.41
  14.8 1.7 convolution_bitcast_fusion.3
  16.6 2.4 convolution_bitcast_fusion.2
  18.9 1.8 convolution_bitcast_fusion
  20.7 0.6 copy.38
  22.1 0.9 multiply_cosine_fusion.1
  22.9 1.0 fusion.104
  24.6 0.7 subtract_convert_fusion.1
  25.9 1.3 fusion.38
  27.2 1.6 fusion.140
  28.8 2.3 convolution_convert_fusion.5
  31.1 2.0 convolution_convert_fusion.3
  33.1 1.5 convolution_convert_fusion.1
  34.7 31.2 %reduce-scatter.5.cloned.1.call-done = bf16[32,2048]{1,0:T(8,128)(2,1)} async-done(((bf16[256,2048]{1,0:T(8,128)(2,1)}), bf16[32,2048]{1,0:T(8,128)(2,1)}) %reduce-scatter.5.cloned.1.call-update) | async-done | bytes 131088 | tf_op jit(solution)/shard_map/reduce_scatter | solution.py:128
  65.9 1.1 multiply_reduce_fusion.3
  67.0 1.6 multiply_convert_fusion.3
  69.3 1.7 convolution_convert_fusion.4
  71.0 1.4 fusion.37
  72.4 2.0 convolution_convert_fusion.2
  74.4 1.5 convolution_convert_fusion
  76.0 17.2 %all-gather.5.cloned.1.call-done = bf16[256,2048]{1,0:T(8,128)(2,1)} async-done(((bf16[32,2048]{1,0:T(8,128)(2,1)}), bf16[256,2048]{1,0:T(8,128)(2,1)}) %all-gather.5.cloned.1.call-update) | async-done | bytes 1048592 | tf_op jit(solution)/shard_map/all_gather | solution.py:138
  93.2 3.8 fusion.12
  97.0 6.9 %fusion.22 = bf16[256,2048]{1,0:T(8,128)(2,1)} fusion(bf16[2,1024,2048]{2,1,0:T(8,128)(2,1)} %param.27, bf16[256,2048]{1,0:T(8,128)(2,1)S(1)} %copy-done.23, bf16[2,2048,1024]{2,1,0:T(8,128)(2,1)} %param.26, f32[256,1024]{1,0:T(8,128)S(1)} %fusion.12), kind=kOutput, calls=%fused_computation.31 | convolution fusion | flops 2149580800 | bytes 11534336 | tf_op jit(solution)/shard_map/dot_general | solution.py:143
  104.0 19.7 %reduce-scatter.9.cloned.1.call-done = bf16[32,2048]{1,0:T(8,128)(2,1)} async-done(((bf16[256,2048]{1,0:T(8,128)(2,1)}), bf16[32,2048]{1,0:T(8,128)(2,1)}) %reduce-scatter.9.cloned.1.call-update) | async-done | bytes 131088 | tf_op jit(solution)/shard_map/reduce_scatter | solution.py:128
  123.8 32.9 %reduce-scatter.7.cloned.1.call-done = bf16[32,2048]{1,0:T(8,128)(2,1)} async-done(((bf16[256,2048]{1,0:T(8,128)(2,1)}), bf16[32,2048]{1,0:T(8,128)(2,1)}) %reduce-scatter.7.cloned.1.call-update) | async-done | bytes 131088 | tf_op jit(solution)/shard_map/reduce_scatter | solution.py:142
  156.7 1.2 multiply_reduce_fusion.2
  157.9 1.7 multiply_convert_fusion.1
  159.8 24.2 %all-gather.9.cloned.1.call-done = bf16[256,2048]{1,0:T(8,128)(2,1)} async-done(((bf16[32,2048]{1,0:T(8,128)(2,1)}), bf16[256,2048]{1,0:T(8,128)(2,1)}) %all-gather.9.cloned.1.call-update) | async-done | bytes 1048592 | tf_op jit(solution)/shard_map/all_gather | solution.py:138
  184.0 4.9 %fusion.6 = f32[256,1024]{1,0:T(8,128)} fusion(bf16[256,2048]{1,0:T(8,128)(2,1)} %all-gather.9.cloned.1.call-done, bf16[2,2048,1024]{2,1,0:T(8,128)(2,1)} %param.25), kind=kOutput, calls=%fused_computation.6 | convolution fusion | flops 1073741824 | bytes 6291456 | tf_op jit(solution)/shard_map/dot_general | solution.py:139
  188.9 7.3 %fusion.25 = bf16[256,2048]{1,0:T(8,128)(2,1)} fusion(bf16[2,1024,2048]{2,1,0:T(8,128)(2,1)} %param.27, bf16[256,2048]{1,0:T(8,128)(2,1)S(1)} %copy-done.24, bf16[2,2048,1024]{2,1,0:T(8,128)(2,1)} %param.26, f32[256,1024]{1,0:T(8,128)} %fusion.6), kind=kOutput, calls=%fused_computation.32 | convolution fusion | flops 2149580800 | bytes 11534336 | tf_op jit(solution)/shard_map/dot_general | solution.py:143
  196.3 28.5 %reduce-scatter.11.cloned.1.call-done = bf16[32,2048]{1,0:T(8,128)(2,1)} async-done(((bf16[256,2048]{1,0:T(8,128)(2,1)}), bf16[32,2048]{1,0:T(8,128)(2,1)}) %reduce-scatter.11.cloned.1.call-update) | async-done | bytes 131088 | tf_op jit(solution)/shard_map/reduce_scatter | solution.py:142
  224.8 1.8 multiply_convert_fusion.2
  226.6 1.7 multiply_convert_fusion
  228.3 0.7 all-gather.7.cloned.1.call-update
  229.1 17.2 %fusion.136 = (bf16[1,2048,1002]{1,0,2:T(2,128)(2,1)}, bf16[1,2048,1002]{1,0,2:T(2,128)(2,1)}) fusion(bf16[2,2048,1002]{1,0,2:T(2,128)(2,1)} %param.29), kind=kLoop, calls=%fused_computation.180 | loop fusion | bytes 16416768 | tf_op jit(solution)/shard_map/slice | solution.py:153
  246.3 45.8 %all-gather.11.cloned.1.call-done = bf16[1024,2048]{1,0:T(8,128)(2,1)} async-done(((bf16[32,2048]{1,0:T(8,128)(2,1)}), bf16[1024,2048]{1,0:T(8,128)(2,1)}) %all-gather.11.cloned.1.call-update) | async-done | bytes 4194320 | tf_op jit(solution)/shard_map/all_gather | solution.py:152
  292.1 11.6 %fusion.151 = (f32[1024]{0:T(1024)S(1)}, f32[1024,1002]{0,1:T(8,128)}) fusion(bf16[1024,2048]{1,0:T(8,128)(2,1)} %all-gather.11.cloned.1.call-done, bf16[1,2048,1002]{1,0,2:T(2,128)(2,1)} %get-tuple-element.14), kind=kOutput, calls=%fused_computation.187 | convolution fusion | flops 4203717632 | bytes 12406784 | tf_op jit(solution)/shard_map/dot_general | solution.py:151
  303.7 51.9 %all-gather.7.cloned.1.call-done = bf16[1024,2048]{1,0:T(8,128)(2,1)} async-done(((bf16[32,2048]{1,0:T(8,128)(2,1)}), bf16[1024,2048]{1,0:T(8,128)(2,1)}) %all-gather.7.cloned.1.call-update) | async-done | bytes 4194320 | tf_op jit(solution)/shard_map/all_gather | solution.py:152
  355.6 10.4 %fusion.150 = (f32[1024]{0:T(1024)S(1)}, f32[1024,1002]{0,1:T(8,128)S(1)}) fusion(bf16[1024,2048]{1,0:T(8,128)(2,1)} %all-gather.7.cloned.1.call-done, bf16[1,2048,1002]{1,0,2:T(2,128)(2,1)} %get-tuple-element.13), kind=kOutput, calls=%fused_computation.186 | convolution fusion | flops 4203717632 | bytes 12406784 | tf_op jit(solution)/shard_map/dot_general | solution.py:151
  366.1 2.0 exponential_reduce_fusion.1
  368.1 12.5 %all_to_all.5 = f32[32,3,2,256]{3,2,1,0:T(2,128)S(1)} all-to-all(f32[32,3,2,256]{3,2,1,0:T(2,128)S(1)} %bitcast.157), channel_id=1, replica_groups=mesh['req'=4,'mp'=8] {'req','mp'}, dimensions={0} | all-to-all | bytes 393216 | tf_op jit(solution)/shard_map/all_to_all | solution.py:170
  380.8 0.7 select_reduce_fusion.2
  382.1 0.7 fusion.106
  (89 shorter events, 4.7 us)
Async XLA Ops:
  7.2 7.7 %copy-start.1 = (bf16[256,2048]{1,0:T(8,128)(2,1)S(1)}, bf16[256,2048]{1,0:T(8,128)(2,1)}, u32[]{:S(2)}) copy-start(bf16[256,2048]{1,0:T(8,128)(2,1)} %param.15) | copy-start | bytes 3145732
  7.2 58.7 %reduce-scatter.5.cloned.1.call-start = ((), (), s32[]{:S(2)}) async-start(), calls=%async_computation.5 | async-start | bytes 1179648 | tf_op jit(solution)/shard_map/reduce_scatter | solution.py:128
  9.3 12.1 %copy-start.20 = (f32[256]{0:T(256)}, f32[256]{0:T(256)S(1)}, u32[]{:S(2)}) copy-start(f32[256]{0:T(256)S(1)} %add_rsqrt_fusion) | copy-start | bytes 3076
  10.1 11.3 %copy-start.13 = (f32[1,2048]{1,0:T(1,128)}, f32[1,2048]{1,0:T(1,128)S(1)}, u32[]{:S(2)}) copy-start(f32[1,2048]{1,0:T(1,128)S(1)} %get-tuple-element.33) | copy-start | bytes 24580
  10.9 5.6 %copy-start.16 = (s32[8,1]{0,1:T(1,128)}, s32[8,1]{0,1:T(1,128)S(1)}, u32[]{:S(2)}) copy-start(s32[8,1]{0,1:T(1,128)S(1)} %reduce-window.4) | copy-start | bytes 100
  11.6 5.0 %copy-start.18 = (s32[8]{0:T(128)}, s32[8]{0:T(128)S(1)}, u32[]{:S(2)}) copy-start(s32[8]{0:T(128)S(1)} %fusion.114) | copy-start | bytes 100
  23.9 4.9 %copy-start.14 = (f32[1,2048]{1,0:T(1,128)S(1)}, f32[1,2048]{1,0:T(1,128)}, u32[]{:S(2)}) copy-start(f32[1,2048]{1,0:T(1,128)} %copy-done.13) | copy-start | bytes 24580
  24.6 0.7 copy-start.10
  25.2 0.6 copy-start.7
  25.2 0.6 copy-start.8
  27.2 5.9 %copy-start.3 = (bf16[2,256,2048]{2,1,0:T(8,128)(2,1)S(1)}, bf16[2,256,2048]{2,1,0:T(8,128)(2,1)}, u32[]{:S(2)}) copy-start(bf16[2,256,2048]{2,1,0:T(8,128)(2,1)} %param.23) | copy-start | bytes 6291460
  31.1 3.5 copy-start.11
  31.1 37.6 %copy-start.6 = (bf16[4,256,32]{1,2,0:T(8,128)(2,1)S(1)}, bf16[4,256,32]{1,2,0:T(8,128)(2,1)}, u32[]{:S(2)}) copy-start(bf16[4,256,32]{1,2,0:T(8,128)(2,1)} %get-tuple-element.28) | copy-start | bytes 196612
  31.1 37.6 %copy-start.9 = (bf16[256,64]{0,1:T(8,128)(2,1)S(1)}, bf16[256,64]{0,1:T(8,128)(2,1)}, u32[]{:S(2)}) copy-start(bf16[256,64]{0,1:T(8,128)(2,1)} %get-tuple-element.46) | copy-start | bytes 98308
  33.1 36.1 %copy-start.21 = (f32[256]{0:T(256)S(1)}, f32[256]{0:T(256)}, u32[]{:S(2)}) copy-start(f32[256]{0:T(256)} %copy-done.20) | copy-start | bytes 3076
  34.6 58.6 %all-gather.5.cloned.1.call-start = ((), (), s32[]{:S(2)}) async-start(), calls=%async_computation.6 | async-start | bytes 1179648 | tf_op jit(solution)/shard_map/all_gather | solution.py:138
  68.6 55.1 %reduce-scatter.9.cloned.1.call-start = ((), (), s32[]{:S(2)}) async-start(), calls=%async_computation.9 | async-start | bytes 1179648 | tf_op jit(solution)/shard_map/reduce_scatter | solution.py:128
  76.0 80.7 %reduce-scatter.7.cloned.1.call-start = ((), (), s32[]{:S(2)}) async-start(), calls=%async_computation.7 | async-start | bytes 1179648 | tf_op jit(solution)/shard_map/reduce_scatter | solution.py:142
  93.2 3.8 copy-start.23
  97.0 59.7 %copy-start.2 = (bf16[32,2048]{1,0:T(8,128)(2,1)S(1)}, bf16[32,2048]{1,0:T(8,128)(2,1)}, u32[]{:S(2)}) copy-start(bf16[32,2048]{1,0:T(8,128)(2,1)} %reduce-scatter.5.cloned.1.call-done) | copy-start | bytes 393220
  104.0 80.0 %all-gather.9.cloned.1.call-start = ((), (), s32[]{:S(2)}) async-start(), calls=%async_computation.10 | async-start | bytes 1179648 | tf_op jit(solution)/shard_map/all_gather | solution.py:138
  159.6 65.2 %reduce-scatter.11.cloned.1.call-start = ((), (), s32[]{:S(2)}) async-start(), calls=%async_computation.11 | async-start | bytes 1179648 | tf_op jit(solution)/shard_map/reduce_scatter | solution.py:142
  184.0 4.9 %copy-start.24 = (bf16[256,2048]{1,0:T(8,128)(2,1)S(1)}, bf16[256,2048]{1,0:T(8,128)(2,1)}, u32[]{:S(2)}) copy-start(bf16[256,2048]{1,0:T(8,128)(2,1)} %all-gather.9.cloned.1.call-done) | copy-start | bytes 3145732
  188.9 7.4 %copy-start.12 = (f32[2,2048]{1,0:T(2,128)S(1)}, f32[2,2048]{1,0:T(2,128)}, u32[]{:S(2)}) copy-start(f32[2,2048]{1,0:T(2,128)} %param.28) | copy-start | bytes 49156
  188.9 35.9 %copy-start.4 = (bf16[32,2048]{1,0:T(8,128)(2,1)S(1)}, bf16[32,2048]{1,0:T(8,128)(2,1)}, u32[]{:S(2)}) copy-start(bf16[32,2048]{1,0:T(8,128)(2,1)} %reduce-scatter.9.cloned.1.call-done) | copy-start | bytes 393220
  188.9 35.9 %copy-start.5 = (bf16[32,2048]{1,0:T(8,128)(2,1)S(1)}, bf16[32,2048]{1,0:T(8,128)(2,1)}, u32[]{:S(2)}) copy-start(bf16[32,2048]{1,0:T(8,128)(2,1)} %reduce-scatter.7.cloned.1.call-done) | copy-start | bytes 393220
  188.9 40.1 %copy-start.15 = (s32[1024]{0:T(1024)S(1)}, s32[1024]{0:T(1024)}, u32[]{:S(2)}) copy-start(s32[1024]{0:T(1024)} %param.18) | copy-start | bytes 12292
  196.2 95.8 %all-gather.11.cloned.1.call-start = ((), (), s32[]{:S(2)}) async-start(), calls=%async_computation.12 | async-start | bytes 4325376 | tf_op jit(solution)/shard_map/all_gather | solution.py:152
  228.3 127.3 %all-gather.7.cloned.1.call-start = ((), (), s32[]{:S(2)}) async-start(), calls=%async_computation.8 | async-start | bytes 4325376 | tf_op jit(solution)/shard_map/all_gather | solution.py:152
  355.6 10.4 %copy-start = (f32[1024,1002]{0,1:T(8,128)S(1)}, f32[1024,1002]{0,1:T(8,128)}, u32[]{:S(2)}) copy-start(f32[1024,1002]{0,1:T(8,128)} %get-tuple-element.44) | copy-start | bytes 12312580
  366.0 14.8 %copy-start.22 = (s32[256]{0:T(256)S(1)}, s32[256]{0:T(256)}, u32[]{:S(2)}) copy-start(s32[256]{0:T(256)} %param.17) | copy-start | bytes 3076
  366.0 14.8 %copy-start.17 = (s32[8,1]{0,1:T(1,128)S(1)}, s32[8,1]{0,1:T(1,128)}, u32[]{:S(2)}) copy-start(s32[8,1]{0,1:T(1,128)} %copy-done.16) | copy-start | bytes 100
  366.1 14.8 %copy-start.19 = (s32[8]{0:T(128)S(1)}, s32[8]{0:T(128)}, u32[]{:S(2)}) copy-start(s32[8]{0:T(128)} %copy-done.18) | copy-start | bytes 100
Sparse Core Ops, SparseCore 0:
  34.7 31.1 reduce-scatter.4
  68.8 24.3 all-gather.4
  95.4 28.2 reduce-scatter.8
  125.9 30.7 reduce-scatter.6
  159.7 24.3 all-gather.8
  196.4 28.3 reduce-scatter.10
  228.4 63.6 all-gather.10
  295.1 60.4 all-gather.6

commit v4 on v2

--- a/solution.py
+++ b/solution.py
@@ -124,18 +124,15 @@
         )
     attended = jnp.stack(attended_list, axis=1)
     selected_rows = attended
-    mixed = lax.psum_scatter(
+    mixed = lax.psum(
         jnp.einsum(
             "kbq,bqo->kbo", selected_rows, output_weight, preferred_element_type=jnp.float32
         ).astype(jnp.bfloat16),
         "mp",
-        scatter_dimension=0,
-        tiled=True,
     ).astype(jnp.float32)
-    own_tokens = lax.dynamic_slice_in_dim(tokens, mp_index * own_rows, own_rows, 0)
-    residual = own_tokens.astype(jnp.float32)[:, None, :] + mixed
-    normed_mid = rms_scale(residual, mlp_gain).astype(jnp.bfloat16)
-    row_block = lax.all_gather(normed_mid, "mp", axis=0, tiled=True)
+    residual_rows = tokens.astype(jnp.float32)[:, None, :] + mixed
+    row_block = rms_scale(residual_rows, mlp_gain).astype(jnp.bfloat16)
+    residual = lax.dynamic_slice_in_dim(residual_rows, mp_index * own_rows, own_rows, 0)
     gate_part = jnp.einsum("nmd,mdf->nmf", row_block, w_gate, preferred_element_type=jnp.float32)
     lift_part = jnp.einsum("nmd,mdf->nmf", row_block, w_up, preferred_element_type=jnp.float32)
     hidden = (jax.nn.silu(gate_part) * lift_part).astype(jnp.bfloat16)

time: 290 us -> 295 us (1.017)
    psum x0 -> x1, waiting for transfers between devices: none -> 65.4 us  [per_device(): lax.psum(jnp.einsum('kbq,bqo->kbo', selected_rows, output_weight, preferr...]
    reduce_scatter x1 -> x0, waiting for transfers between devices: 35.4 us -> none  [per_device(): lax.psum_scatter(jnp.einsum('kbq,bqo->kbo', selected_rows, output_weight,...]
    all_gather x1 -> x0, waiting for transfers between devices: 30.9 us -> none  [per_device(): row_block = lax.all_gather(normed_mid, 'mp', axis=0, tiled=True)]
    add x0 -> x1, other arithmetic: none -> 4.08 us  [per_device(): residual_rows = tokens.astype(jnp.float32)[:, None, :] + mixed]
  transfers between devices with their start and end apart: 4 -> 3, of which waited for: 4 -> 3; matrix products, arithmetic and copies ran while one was open for 0% -> 0% of each run, Pallas kernels for 0% -> 0%
where the time goes in v4:
time: 295 us; the launch traced here: 294 us
  waiting for transfers between devices  178 us (60%)
  matrix products  59.9 us (20%)
  other arithmetic  19.2 us (7%)
  between operations  14.1 us (5%)
  blocking collectives  12.3 us (4%)
  local copies, waits for them, and re-layouts  10.2 us (3%)
    all_gather x1, waiting for transfers between devices, per_device(): lax.all_gather(closing, ('req', 'mp'), axis=0, tiled=True)  78.4 us
    psum x1, waiting for transfers between devices, per_device(): lax.psum(jnp.einsum('kbq,bqo->kbo', selected_rows, output_weight, preferr...  65.4 us
    reduce_scatter x1, waiting for transfers between devices, per_device(): lax.psum_scatter(jnp.einsum('nmf,mfd->nmd', selected_rows, w_down, prefer...  34.3 us
    dot_general x1, matrix products, per_device(): jnp.einsum('nmd,mdv->mnv', lax.all_gather(closing, ('req', 'mp'), axis=0,...  16.9 us
    dot_general x1, matrix products, per_device(): jnp.einsum('nmf,mfd->nmd', selected_rows, w_down, preferred_element_type=...  13.1 us
    all_to_all x1, blocking collectives, per_device(): incoming = lax.all_to_all(outgoing, ('req', 'mp'), 0, 0, tiled=True)  12.3 us
    dot_general x3, local copies, waits for them, and re-layouts, per_device(): query = jnp.dot(normed, w_query[model], preferred_element_type=jnp.float32)  7.69 us
    dot_general x1, matrix products, per_device(): jnp.einsum('nmd,mdf->nmf', row_block, w_gate, preferred_element_type=jnp....  7.25 us
  transfers between devices with their start and end apart: 3, of which 3 were waited for; matrix products, arithmetic and copies ran while one was open for 0% of the time, Pallas kernels for 0%

profile of v4, /device:TPU:1, one launch (start us, length us, event | category | flops | bytes accessed | tf_op | source)
XLA Modules:
  0.0 294.2 jit_solution(16184909879509824941)
XLA Ops:
  7.2 0.5 multiply_power_fusion
  7.8 1.6 multiply_reduce_fusion.1
  9.3 0.8 fusion.90
  10.2 0.8 reduce-window.4
  11.0 0.7 fusion.74
  11.7 0.1 select_reduce_fusion.2
  11.8 3.0 %slice_bitcast_fusion.1 = (bf16[256,2048]{0,1:T(8,128)(2,1)}, bf16[256,2048]{0,1:T(8,128)(2,1)}) fusion(bf16[2,2048,256]{2,1,0:T(8,128)(2,1)} %param.20), kind=kLoop, calls=%fused_computation.46 | loop fusion | bytes 4194304 | tf_op jit(solution)/shard_map/dot_general | solution.py:117
  14.8 2.4 copy.36
  17.2 1.8 convolution_bitcast_fusion.3
  19.0 2.4 convolution_bitcast_fusion.2
  21.4 0.6 convolution_bitcast_fusion
  21.9 2.3 copy.34
  24.2 1.8 convolution_bitcast_fusion.1
  26.1 0.1 fusion.23
  26.2 0.2 multiply_cosine_fusion.1
  26.4 0.2 fusion.64
  26.6 0.6 pad_maximum_fusion
  27.2 0.7 subtract_convert_fusion.1
  27.9 0.6 copy-done.6
  28.5 1.3 fusion.15
  29.9 1.4 fusion.96
  31.3 1.4 fusion.14
  32.7 1.1 fusion.91
  33.8 1.7 convolution_convert_fusion.5
  35.6 2.3 convolution_convert_fusion.4
  37.9 1.9 convolution_convert_fusion.3
  39.8 0.1 copy.38
  40.0 2.0 convolution_convert_fusion.2
  42.0 0.1 copy.39
  42.1 2.1 fusion.4
  44.2 0.2 reduce-scatter.2.cloned.1.call-start
  44.4 0.2 convert_element_type.101
  44.7 65.4 %all-reduce.2.cloned.1.call-done = bf16[256,2,2048]{2,0,1:T(8,128)(2,1)} async-done(((bf16[256,2,2048]{2,0,1:T(8,128)(2,1)}), bf16[256,2,2048]{2,0,1:T(8,128)(2,1)}) %all-reduce.2.cloned.1.call-update) | async-done | bytes 2097168 | tf_op jit(solution)/shard_map/psum | solution.py:127
  110.1 4.1 %convert_add_fusion = (f32[256,2,2048]{2,0,1:T(8,128)}, f32[256,2]{0,1:T(2,128)S(1)}) fusion(bf16[256,2,2048]{2,0,1:T(8,128)(2,1)} %all-reduce.2.cloned.1.call-done, f32[256,2048]{1,0:T(8,128)S(1)} %convert_element_type.101), kind=kLoop, calls=%fused_computation.8 | loop fusion | flops 4193792 | bytes 8390656 | tf_op jit(solution)/shard_map/add | solution.py:133
  114.2 7.2 %fusion.19 = f32[2,256,1024]{2,1,0:T(8,128)} fusion(bf16[2,2048,1024]{2,1,0:T(8,128)(2,1)} %param.25, f32[2,2048]{1,0:T(2,128)S(1)} %copy-done.23, f32[256,2]{0,1:T(2,128)S(1)} %add_rsqrt_fusion, bf16[256,2,2048]{2,0,1:T(8,128)(2,1)S(1)} %copy-done.3, f32[256,2048]{1,0:T(8,128)S(1)} %convert_element_type.101), kind=kOutput, calls=%fused_computation.47 | convolution fusion | flops 2152726528 | bytes 14698496 | tf_op jit(solution)/shard_map/nmd,mdf->nmf/dot_general | solution.py:136
  121.4 13.1 %fusion.5 = bf16[256,2,2048]{2,0,1:T(8,128)(2,1)} fusion(bf16[2,1024,2048]{2,1,0:T(8,128)(2,1)} %param.27, f32[2,256,1024]{2,1,0:T(8,128)} %fusion.19, bf16[2,2048,1024]{2,1,0:T(8,128)(2,1)} %param.26, f32[2,2048]{1,0:T(2,128)S(1)} %copy-done.23, f32[256,2]{0,1:T(2,128)S(1)} %add_rsqrt_fusion, bf16[256,2,2048]{2,0,1:T(8,128)(2,1)} %all-reduce.2.cloned.1.call-done, ...), kind=kOutput, calls=%fused_computation.13 | convolution fusion | flops 4304404480 | bytes 25184256 | tf_op jit(solution)/shard_map/nmf,mfd->nmd/dot_general | solution.py:141
  134.6 0.3 all-gather.2.cloned.1.call-start
  134.9 34.3 %reduce-scatter.2.cloned.1.call-done = bf16[32,2,2048]{2,0,1:T(8,128)(2,1)} async-done(((bf16[256,2,2048]{2,0,1:T(8,128)(2,1)}), bf16[32,2,2048]{2,0,1:T(8,128)(2,1)}) %reduce-scatter.2.cloned.1.call-update) | async-done | bytes 262160 | tf_op jit(solution)/shard_map/reduce_scatter | solution.py:140
  169.2 1.3 multiply_reduce_fusion.2
  170.5 2.0 multiply_convert_fusion.6
  172.5 0.7 iota_compare_fusion
  173.2 78.4 %all-gather.2.cloned.1.call-done = bf16[1024,2,2048]{2,0,1:T(8,128)(2,1)} async-done(((bf16[32,2,2048]{2,0,1:T(8,128)(2,1)}), bf16[1024,2,2048]{2,0,1:T(8,128)(2,1)}) %all-gather.2.cloned.1.call-update) | async-done | bytes 8388624 | tf_op jit(solution)/shard_map/all_gather | solution.py:154
  251.6 16.9 %fusion.101 = (f32[2,1024]{1,0:T(2,128)S(1)}, f32[2,1024,1002]{1,2,0:T(8,128)}) fusion(bf16[1024,2,2048]{2,0,1:T(8,128)(2,1)} %all-gather.2.cloned.1.call-done, bf16[2,2048,1002]{1,0,2:T(2,128)(2,1)} %param.29), kind=kOutput, calls=%fused_computation.151 | convolution fusion | flops 8407435264 | bytes 24813568 | tf_op jit(solution)/shard_map/nmd,mdv->mnv/dot_general | solution.py:152
  268.5 4.6 %exponential_reduce_fusion = (f32[2,1024]{1,0:T(2,128)S(1)}, f32[2,1024]{1,0:T(2,128)S(1)}) fusion(f32[2,1024,1002]{1,2,0:T(8,128)} %get-tuple-element.30, f32[2,1024]{1,0:T(2,128)S(1)} %get-tuple-element.29, pred[1024,1002]{0,1:T(8,128)(4,1)S(1)} %iota_compare_fusion), kind=kLoop, calls=%fused_computation.5 | loop fusion | flops 8204288 | bytes 9259008 | tf_op jit(solution)/shard_map/reduce_sum | solution.py:159
  273.2 12.3 %all_to_all.5 = f32[32,3,2,256]{3,2,1,0:T(2,128)S(1)} all-to-all(f32[32,3,2,256]{3,2,1,0:T(2,128)S(1)} %bitcast.119), channel_id=1, replica_groups=mesh['req'=4,'mp'=8] {'req','mp'}, dimensions={0} | all-to-all | bytes 393216 | tf_op jit(solution)/shard_map/all_to_all | solution.py:172
  285.7 0.7 select_reduce_fusion.1
  286.4 0.6 dynamic_slice.15
  287.0 0.7 fusion.66
  (70 shorter events, 0.6 us)
Async XLA Ops:
  7.2 35.0 %copy-start = (bf16[2,256,2048]{2,1,0:T(8,128)(2,1)S(1)}, bf16[2,256,2048]{2,1,0:T(8,128)(2,1)}, u32[]{:S(2)}) copy-start(bf16[2,256,2048]{2,1,0:T(8,128)(2,1)} %param.23) | copy-start | bytes 6291460
  7.2 102.9 %all-reduce.2.cloned.1.call-start = ((), (), s32[]{:S(2)}) async-start(), calls=%async_computation.2 | async-start | bytes 4194304 | tf_op jit(solution)/shard_map/psum | solution.py:127
  9.3 14.9 %copy-start.20 = (f32[256]{0:T(256)}, f32[256]{0:T(256)S(1)}, u32[]{:S(2)}) copy-start(f32[256]{0:T(256)S(1)} %add_rsqrt_fusion.2) | copy-start | bytes 3076
  10.1 14.1 %copy-start.12 = (f32[1,2048]{1,0:T(1,128)}, f32[1,2048]{1,0:T(1,128)S(1)}, u32[]{:S(2)}) copy-start(f32[1,2048]{1,0:T(1,128)S(1)} %get-tuple-element.23) | copy-start | bytes 24580
  11.0 3.8 %copy-start.16 = (s32[8,1]{0,1:T(1,128)}, s32[8,1]{0,1:T(1,128)S(1)}, u32[]{:S(2)}) copy-start(s32[8,1]{0,1:T(1,128)S(1)} %reduce-window.4) | copy-start | bytes 100
  11.7 3.1 %copy-start.18 = (s32[8]{0:T(128)}, s32[8]{0:T(128)S(1)}, u32[]{:S(2)}) copy-start(s32[8]{0:T(128)S(1)} %fusion.74) | copy-start | bytes 100
  14.8 2.4 copy-start.2
  17.2 4.2 %copy-start.4 = (bf16[256,2048]{1,0:T(8,128)(2,1)S(1)}, bf16[256,2048]{1,0:T(8,128)(2,1)}, u32[]{:S(2)}) copy-start(bf16[256,2048]{1,0:T(8,128)(2,1)} %copy.36) | copy-start | bytes 3145732
  24.2 1.9 copy-start.15
  24.2 2.2 copy-start.10
  27.2 0.7 copy-start.9
  27.9 0.6 copy-start.6
  27.9 0.6 copy-start.7
  27.9 3.4 %copy-start.5 = (bf16[4,256,32]{1,2,0:T(8,128)(2,1)S(1)}, bf16[4,256,32]{1,2,0:T(8,128)(2,1)}, u32[]{:S(2)}) copy-start(bf16[4,256,32]{1,2,0:T(8,128)(2,1)} %get-tuple-element.22) | copy-start | bytes 196612
  27.9 3.4 %copy-start.8 = (bf16[256,64]{0,1:T(8,128)(2,1)S(1)}, bf16[256,64]{0,1:T(8,128)(2,1)}, u32[]{:S(2)}) copy-start(bf16[256,64]{0,1:T(8,128)(2,1)} %get-tuple-element.32) | copy-start | bytes 98308
  31.3 2.6 copy-start.13
  31.3 2.6 copy-start.21
  37.9 2.0 copy-start.24
  44.2 125.0 %reduce-scatter.2.cloned.1.call-start = ((), (), s32[]{:S(2)}) async-start(), calls=%async_computation.3 | async-start | bytes 2359296 | tf_op jit(solution)/shard_map/reduce_scatter | solution.py:140
  44.7 69.5 %copy-start.23 = (f32[2,2048]{1,0:T(2,128)S(1)}, f32[2,2048]{1,0:T(2,128)}, u32[]{:S(2)}) copy-start(f32[2,2048]{1,0:T(2,128)} %param.24) | copy-start | bytes 49156
  110.1 4.1 %copy-start.3 = (bf16[256,2,2048]{2,0,1:T(8,128)(2,1)S(1)}, bf16[256,2,2048]{2,0,1:T(8,128)(2,1)}, u32[]{:S(2)}) copy-start(bf16[256,2,2048]{2,0,1:T(8,128)(2,1)} %all-reduce.2.cloned.1.call-done) | copy-start | bytes 6291460
  134.6 35.9 %copy-start.11 = (f32[2,2048]{1,0:T(2,128)S(1)}, f32[2,2048]{1,0:T(2,128)}, u32[]{:S(2)}) copy-start(f32[2,2048]{1,0:T(2,128)} %param.28) | copy-start | bytes 49156
  134.6 37.9 %copy-start.14 = (s32[1024]{0:T(1024)S(1)}, s32[1024]{0:T(1024)}, u32[]{:S(2)}) copy-start(s32[1024]{0:T(1024)} %param.18) | copy-start | bytes 12292
  134.6 117.0 %all-gather.2.cloned.1.call-start = ((), (), s32[]{:S(2)}) async-start(), calls=%async_computation.4 | async-start | bytes 8650752 | tf_op jit(solution)/shard_map/all_gather | solution.py:154
  268.4 17.2 %copy-start.22 = (s32[256]{0:T(256)S(1)}, s32[256]{0:T(256)}, u32[]{:S(2)}) copy-start(s32[256]{0:T(256)} %param.17) | copy-start | bytes 3076
  268.4 17.2 %copy-start.17 = (s32[8,1]{0,1:T(1,128)S(1)}, s32[8,1]{0,1:T(1,128)}, u32[]{:S(2)}) copy-start(s32[8,1]{0,1:T(1,128)} %copy-done.16) | copy-start | bytes 100
  268.5 17.2 %copy-start.19 = (s32[8]{0:T(128)S(1)}, s32[8]{0:T(128)}, u32[]{:S(2)}) copy-start(s32[8]{0:T(128)} %copy-done.18) | copy-start | bytes 100
  268.5 19.2 %copy-start.1 = (bf16[2,256,2048]{2,1,0:T(8,128)(2,1)S(1)}, bf16[2,256,2048]{2,1,0:T(8,128)(2,1)}, u32[]{:S(2)}) copy-start(bf16[2,256,2048]{2,1,0:T(8,128)(2,1)} %param.23) | copy-start | bytes 6291460
Sparse Core Ops, SparseCore 0:
  44.3 65.7 all-reduce.1
  134.7 34.3 reduce-scatter.1
  172.6 78.9 all-gather.1

commit v5 on v2

--- a/solution.py
+++ b/solution.py
@@ -71,14 +71,14 @@
     key_rows = jnp.repeat(key_rows, repeat_times, axis=0)
     value_rows = jnp.repeat(value_rows, repeat_times, axis=0)
     scores = jnp.einsum(
-        "hqd,hkd->hqk", query.astype(jnp.float32), key_rows.astype(jnp.float32)
+        "hqd,hkd->hqk", query, key_rows, preferred_element_type=jnp.float32
     ) * HEAD_DIM ** (-0.5)
     scores = jnp.where(allowed[None], scores, -1e30)
     highest = jnp.max(scores, axis=-1, keepdims=True)
     weights = jnp.exp(scores - highest)
     probs = (weights / jnp.sum(weights, axis=-1, keepdims=True)).astype(jnp.bfloat16)
     attended = jnp.einsum(
-        "hqk,hkd->hqd", probs.astype(jnp.float32), value_rows.astype(jnp.float32)
+        "hqk,hkd->hqd", probs, value_rows, preferred_element_type=jnp.float32
     ).astype(jnp.bfloat16)
     return attended.transpose(1, 0, 2).reshape(slot_count, -1)
 

time: 290 us -> 290 us (level)
  no operation moved by 1% of the time
where the time goes in v5:
time: 290 us; the launch traced here: 289 us
  waiting for transfers between devices  177 us (61%)
  matrix products  60 us (21%)
  other arithmetic  16.9 us (6%)
  between operations  14.1 us (5%)
  blocking collectives  12.3 us (4%)
  local copies, waits for them, and re-layouts  8.22 us (3%)
    all_gather x1, waiting for transfers between devices, per_device(): lax.all_gather(closing, ('req', 'mp'), axis=0, tiled=True)  78.3 us
    reduce_scatter x1, waiting for transfers between devices, per_device(): lax.psum_scatter(jnp.einsum('kbq,bqo->kbo', selected_rows, output_weight,...  35.4 us
    reduce_scatter x1, waiting for transfers between devices, per_device(): lax.psum_scatter(jnp.einsum('nmf,mfd->nmd', selected_rows, w_down, prefer...  32.2 us
    all_gather x1, waiting for transfers between devices, per_device(): row_block = lax.all_gather(normed_mid, 'mp', axis=0, tiled=True)  30.9 us
    dot_general x1, matrix products, per_device(): jnp.einsum('nmd,mdv->mnv', lax.all_gather(closing, ('req', 'mp'), axis=0,...  16.9 us
    dot_general x1, matrix products, per_device(): jnp.einsum('nmf,mfd->nmd', selected_rows, w_down, preferred_element_type=...  12.5 us
    all_to_all x1, blocking collectives, per_device(): incoming = lax.all_to_all(outgoing, ('req', 'mp'), 0, 0, tiled=True)  12.3 us
    dot_general x1, matrix products, per_device(): jnp.einsum('nmd,mdf->nmf', row_block, w_gate, preferred_element_type=jnp....  7.79 us
  transfers between devices with their start and end apart: 4, of which 4 were waited for; matrix products, arithmetic and copies ran while one was open for 0% of the time, Pallas kernels for 0%

profile of v5, /device:TPU:1, one launch (start us, length us, event | category | flops | bytes accessed | tf_op | source)
XLA Modules:
  0.0 289.0 jit_solution(9929756520780141737)
XLA Ops:
  7.2 0.5 multiply_power_fusion
  7.8 1.6 fusion.10
  9.3 0.8 fusion.100
  10.2 0.8 reduce-window.4
  11.0 0.7 fusion.78
  11.7 0.1 select_reduce_fusion.2
  11.8 2.7 slice_bitcast_fusion.1
  14.4 2.3 copy.36
  16.7 2.2 convolution_bitcast_fusion.3
  18.9 2.1 convolution_bitcast_fusion.2
  21.0 1.2 convolution_bitcast_fusion
  22.2 1.4 copy.34
  23.7 2.1 convolution_bitcast_fusion.1
  25.8 0.1 fusion.27
  25.9 0.2 multiply_cosine_fusion.1
  26.1 0.2 fusion.68
  26.4 0.6 pad_maximum_fusion
  27.1 1.4 fusion.20
  28.4 0.5 fusion.106
  29.0 1.3 fusion.19
  30.3 1.1 fusion.101
  31.5 1.7 convolution_convert_fusion.5
  33.2 2.3 convolution_convert_fusion.4
  35.6 2.0 convolution_convert_fusion.3
  37.6 0.1 copy.38
  37.7 1.9 convolution_convert_fusion.2
  39.7 0.1 copy.39
  39.8 2.1 fusion.4
  42.0 35.4 %reduce-scatter.3.cloned.1.call-done = bf16[32,2,2048]{2,0,1:T(8,128)(2,1)} async-done(((bf16[256,2,2048]{2,0,1:T(8,128)(2,1)}), bf16[32,2,2048]{2,0,1:T(8,128)(2,1)}) %reduce-scatter.3.cloned.1.call-update) | async-done | bytes 262160 | tf_op jit(solution)/shard_map/reduce_scatter | solution.py:127
  77.4 1.1 multiply_reduce_fusion.1
  78.5 1.8 multiply_convert_fusion.1
  80.3 0.2 reduce-scatter.5.cloned.1.call-start
  80.5 30.9 %all-gather.3.cloned.1.call-done = bf16[256,2,2048]{2,0,1:T(8,128)(2,1)} async-done(((bf16[32,2,2048]{2,0,1:T(8,128)(2,1)}), bf16[256,2,2048]{2,0,1:T(8,128)(2,1)}) %all-gather.3.cloned.1.call-update) | async-done | bytes 2097168 | tf_op jit(solution)/shard_map/all_gather | solution.py:138
  111.4 7.8 %fusion.112 = f32[2,256,1024]{2,1,0:T(8,128)} fusion(bf16[256,2,2048]{2,0,1:T(8,128)(2,1)} %all-gather.3.cloned.1.call-done, bf16[2,2048,1024]{2,1,0:T(8,128)(2,1)} %param.25), kind=kOutput, calls=%fused_computation.156 | convolution fusion | flops 2147483648 | bytes 12582912 | tf_op jit(solution)/shard_map/nmd,mdf->nmf/dot_general | solution.py:139
  119.2 12.5 %fusion.5 = bf16[256,2,2048]{2,0,1:T(8,128)(2,1)} fusion(bf16[2,1024,2048]{2,1,0:T(8,128)(2,1)} %param.27, f32[2,256,1024]{2,1,0:T(8,128)} %fusion.112, bf16[256,2,2048]{2,0,1:T(8,128)(2,1)S(1)} %copy-done.2, bf16[2,2048,1024]{2,1,0:T(8,128)(2,1)} %param.26), kind=kOutput, calls=%fused_computation.10 | convolution fusion | flops 4299161600 | bytes 23068672 | tf_op jit(solution)/shard_map/nmf,mfd->nmd/dot_general | solution.py:144
  131.8 0.3 all-gather.5.cloned.1.call-start
  132.1 32.2 %reduce-scatter.5.cloned.1.call-done = bf16[32,2,2048]{2,0,1:T(8,128)(2,1)} async-done(((bf16[256,2,2048]{2,0,1:T(8,128)(2,1)}), bf16[32,2,2048]{2,0,1:T(8,128)(2,1)}) %reduce-scatter.5.cloned.1.call-update) | async-done | bytes 262160 | tf_op jit(solution)/shard_map/reduce_scatter | solution.py:143
  164.3 1.1 multiply_reduce_fusion
  165.5 1.8 multiply_convert_fusion
  167.3 0.7 iota_compare_fusion
  168.0 78.3 %all-gather.5.cloned.1.call-done = bf16[1024,2,2048]{2,0,1:T(8,128)(2,1)} async-done(((bf16[32,2,2048]{2,0,1:T(8,128)(2,1)}), bf16[1024,2,2048]{2,0,1:T(8,128)(2,1)}) %all-gather.5.cloned.1.call-update) | async-done | bytes 8388624 | tf_op jit(solution)/shard_map/all_gather | solution.py:157
  246.3 16.9 %fusion.111 = (f32[2,1024]{1,0:T(2,128)S(1)}, f32[2,1024,1002]{1,2,0:T(8,128)}) fusion(bf16[1024,2,2048]{2,0,1:T(8,128)(2,1)} %all-gather.5.cloned.1.call-done, bf16[2,2048,1002]{1,0,2:T(2,128)(2,1)} %param.29), kind=kOutput, calls=%fused_computation.155 | convolution fusion | flops 8407435264 | bytes 24813568 | tf_op jit(solution)/shard_map/nmd,mdv->mnv/dot_general | solution.py:155
  263.3 4.6 %exponential_reduce_fusion = (f32[2,1024]{1,0:T(2,128)S(1)}, f32[2,1024]{1,0:T(2,128)S(1)}) fusion(f32[2,1024,1002]{1,2,0:T(8,128)} %get-tuple-element.28, f32[2,1024]{1,0:T(2,128)S(1)} %get-tuple-element.27, pred[1024,1002]{0,1:T(8,128)(4,1)S(1)} %iota_compare_fusion), kind=kLoop, calls=%fused_computation.5 | loop fusion | flops 8204288 | bytes 9259008 | tf_op jit(solution)/shard_map/reduce_sum | solution.py:162
  268.0 12.3 %all_to_all.5 = f32[32,3,2,256]{3,2,1,0:T(2,128)S(1)} all-to-all(f32[32,3,2,256]{3,2,1,0:T(2,128)S(1)} %bitcast.121), channel_id=1, replica_groups=mesh['req'=4,'mp'=8] {'req','mp'}, dimensions={0} | all-to-all | bytes 393216 | tf_op jit(solution)/shard_map/all_to_all | solution.py:175
  280.3 0.1 fusion.39
  280.5 0.7 select_reduce_fusion.1
  281.2 0.6 dynamic_slice.15
  281.7 0.7 fusion.70
  (68 shorter events, 0.6 us)
Async XLA Ops:
  7.2 32.6 %copy-start = (bf16[2,256,2048]{2,1,0:T(8,128)(2,1)S(1)}, bf16[2,256,2048]{2,1,0:T(8,128)(2,1)}, u32[]{:S(2)}) copy-start(bf16[2,256,2048]{2,1,0:T(8,128)(2,1)} %param.23) | copy-start | bytes 6291460
  7.2 70.2 %reduce-scatter.3.cloned.1.call-start = ((), (), s32[]{:S(2)}) async-start(), calls=%async_computation.3 | async-start | bytes 2359296 | tf_op jit(solution)/shard_map/reduce_scatter | solution.py:127
  9.3 9.6 %copy-start.18 = (f32[256]{0:T(256)}, f32[256]{0:T(256)S(1)}, u32[]{:S(2)}) copy-start(f32[256]{0:T(256)S(1)} %add_rsqrt_fusion.2) | copy-start | bytes 3076
  10.1 6.6 %copy-start.10 = (f32[1,2048]{1,0:T(1,128)}, f32[1,2048]{1,0:T(1,128)S(1)}, u32[]{:S(2)}) copy-start(f32[1,2048]{1,0:T(1,128)S(1)} %get-tuple-element.21) | copy-start | bytes 24580
  11.0 3.4 %copy-start.14 = (s32[8,1]{0,1:T(1,128)}, s32[8,1]{0,1:T(1,128)S(1)}, u32[]{:S(2)}) copy-start(s32[8,1]{0,1:T(1,128)S(1)} %reduce-window.4) | copy-start | bytes 100
  11.7 2.8 copy-start.16
  16.7 4.3 %copy-start.4 = (bf16[256,2048]{1,0:T(8,128)(2,1)S(1)}, bf16[256,2048]{1,0:T(8,128)(2,1)}, u32[]{:S(2)}) copy-start(bf16[256,2048]{1,0:T(8,128)(2,1)} %param.15) | copy-start | bytes 3145732
  16.7 4.3 %copy-start.6 = (bf16[256,2048]{1,0:T(8,128)(2,1)S(1)}, bf16[256,2048]{1,0:T(8,128)(2,1)}, u32[]{:S(2)}) copy-start(bf16[256,2048]{1,0:T(8,128)(2,1)} %copy.36) | copy-start | bytes 3145732
  23.7 2.3 copy-start.13
  27.0 2.0 copy-start.7
  29.0 2.5 copy-start.5
  29.0 2.5 copy-start.11
  29.0 2.5 copy-start.19
  35.6 2.2 copy-start.21
  41.9 36.6 %copy-start.9 = (f32[2,2048]{1,0:T(2,128)S(1)}, f32[2,2048]{1,0:T(2,128)}, u32[]{:S(2)}) copy-start(f32[2,2048]{1,0:T(2,128)} %param.24) | copy-start | bytes 49156
  41.9 69.5 %all-gather.3.cloned.1.call-start = ((), (), s32[]{:S(2)}) async-start(), calls=%async_computation.4 | async-start | bytes 2359296 | tf_op jit(solution)/shard_map/all_gather | solution.py:138
  80.3 84.0 %reduce-scatter.5.cloned.1.call-start = ((), (), s32[]{:S(2)}) async-start(), calls=%async_computation.5 | async-start | bytes 2359296 | tf_op jit(solution)/shard_map/reduce_scatter | solution.py:143
  111.4 7.8 %copy-start.2 = (bf16[256,2,2048]{2,0,1:T(8,128)(2,1)S(1)}, bf16[256,2,2048]{2,0,1:T(8,128)(2,1)}, u32[]{:S(2)}) copy-start(bf16[256,2,2048]{2,0,1:T(8,128)(2,1)} %all-gather.3.cloned.1.call-done) | copy-start | bytes 6291460
  131.8 32.5 %copy-start.3 = (bf16[32,2,2048]{2,0,1:T(8,128)(2,1)S(1)}, bf16[32,2,2048]{2,0,1:T(8,128)(2,1)}, u32[]{:S(2)}) copy-start(bf16[32,2,2048]{2,0,1:T(8,128)(2,1)} %reduce-scatter.3.cloned.1.call-done) | copy-start | bytes 786436
  131.8 33.7 %copy-start.8 = (f32[2,2048]{1,0:T(2,128)S(1)}, f32[2,2048]{1,0:T(2,128)}, u32[]{:S(2)}) copy-start(f32[2,2048]{1,0:T(2,128)} %param.28) | copy-start | bytes 49156
  131.8 35.5 %copy-start.12 = (s32[1024]{0:T(1024)S(1)}, s32[1024]{0:T(1024)}, u32[]{:S(2)}) copy-start(s32[1024]{0:T(1024)} %param.18) | copy-start | bytes 12292
  131.8 114.5 %all-gather.5.cloned.1.call-start = ((), (), s32[]{:S(2)}) async-start(), calls=%async_computation.6 | async-start | bytes 8650752 | tf_op jit(solution)/shard_map/all_gather | solution.py:157
  263.2 17.2 %copy-start.20 = (s32[256]{0:T(256)S(1)}, s32[256]{0:T(256)}, u32[]{:S(2)}) copy-start(s32[256]{0:T(256)} %param.17) | copy-start | bytes 3076
  263.2 17.2 %copy-start.15 = (s32[8,1]{0,1:T(1,128)S(1)}, s32[8,1]{0,1:T(1,128)}, u32[]{:S(2)}) copy-start(s32[8,1]{0,1:T(1,128)} %copy-done.14) | copy-start | bytes 100
  263.2 17.2 %copy-start.17 = (s32[8]{0:T(128)S(1)}, s32[8]{0:T(128)}, u32[]{:S(2)}) copy-start(s32[8]{0:T(128)} %copy-done.16) | copy-start | bytes 100
  263.2 19.2 %copy-start.1 = (bf16[2,256,2048]{2,1,0:T(8,128)(2,1)S(1)}, bf16[2,256,2048]{2,1,0:T(8,128)(2,1)}, u32[]{:S(2)}) copy-start(bf16[2,256,2048]{2,1,0:T(8,128)(2,1)} %param.23) | copy-start | bytes 6291460
Sparse Core Ops, SparseCore 0:
  42.0 35.3 reduce-scatter.2
  80.4 30.9 all-gather.2
  131.9 32.3 reduce-scatter.4
  167.4 78.9 all-gather.4

commit v6 on v5

--- a/solution.py
+++ b/solution.py
@@ -58,16 +58,10 @@
 
 
 def attend_heads(query, key_rows, value_rows, positions, allowed, repeat_times):
-    slot_count = query.shape[0]
-    query = rotate(query.reshape(slot_count, -1, HEAD_DIM).transpose(1, 0, 2), positions).astype(
-        jnp.bfloat16
-    )
-    key_rows = rotate(
-        key_rows.reshape(slot_count, -1, HEAD_DIM).transpose(1, 0, 2), positions
-    ).astype(jnp.bfloat16)
-    value_rows = (
-        value_rows.reshape(slot_count, -1, HEAD_DIM).transpose(1, 0, 2).astype(jnp.bfloat16)
-    )
+    slot_count = query.shape[1]
+    query = rotate(query, positions).astype(jnp.bfloat16)
+    key_rows = rotate(key_rows, positions).astype(jnp.bfloat16)
+    value_rows = value_rows.astype(jnp.bfloat16)
     key_rows = jnp.repeat(key_rows, repeat_times, axis=0)
     value_rows = jnp.repeat(value_rows, repeat_times, axis=0)
     scores = jnp.einsum(
@@ -114,9 +108,25 @@
     attended_list = []
     for model in range(2):
         normed = rms_scale(tokens, attn_gain[model]).astype(jnp.bfloat16)
-        query = jnp.dot(normed, w_query[model], preferred_element_type=jnp.float32)
-        keys_here = jnp.dot(normed, key_cols[model], preferred_element_type=jnp.float32)
-        values_here = jnp.dot(normed, value_columns[model], preferred_element_type=jnp.float32)
+        width = normed.shape[1]
+        query = jnp.einsum(
+            "td,dhe->hte",
+            normed,
+            w_query[model].reshape(width, heads_here, HEAD_DIM),
+            preferred_element_type=jnp.float32,
+        )
+        keys_here = jnp.einsum(
+            "td,dhe->hte",
+            normed,
+            key_cols[model].reshape(width, kv_here, HEAD_DIM),
+            preferred_element_type=jnp.float32,
+        )
+        values_here = jnp.einsum(
+            "td,dhe->hte",
+            normed,
+            value_columns[model].reshape(width, kv_here, HEAD_DIM),
+            preferred_element_type=jnp.float32,
+        )
         attended_list.append(
             attend_heads(
                 query, keys_here, values_here, positions, allowed, min(sharing, heads_here)

time: 290 us -> 283 us (0.976)
  local copies, waits for them, and re-layouts: 8.22 us -> 2.12 us
    dot_general x3 -> x0, local copies, waits for them, and re-layouts: 6.39 us -> none  [per_device(): query = jnp.dot(normed, w_query[model], preferred_element_type=jnp.float32)]
    unnamed x0 -> x2, matrix products: none -> 4.42 us
    dot_general x6 -> x4, matrix products: 11.7 us -> 7.91 us  [the longest x2 4.31 us: per_device(): jnp.einsum('td,dhe->hte', normed, value_columns[model].reshape(width, kv_...]
where the time goes in v6:
time: 283 us
  waiting for transfers between devices  177 us (63%)
  matrix products  61.2 us (22%)
  other arithmetic  15.7 us (6%)
  between operations  14.1 us (5%)
  blocking collectives  12.3 us (4%)
    all_gather x1, waiting for transfers between devices, per_device(): lax.all_gather(closing, ('req', 'mp'), axis=0, tiled=True)  78.3 us
    reduce_scatter x1, waiting for transfers between devices, per_device(): lax.psum_scatter(jnp.einsum('kbq,bqo->kbo', selected_rows, output_weight,...  35.5 us
    reduce_scatter x1, waiting for transfers between devices, per_device(): lax.psum_scatter(jnp.einsum('nmf,mfd->nmd', selected_rows, w_down, prefer...  32.3 us
    all_gather x1, waiting for transfers between devices, per_device(): row_block = lax.all_gather(normed_mid, 'mp', axis=0, tiled=True)  30.8 us
    dot_general x1, matrix products, per_device(): jnp.einsum('nmd,mdv->mnv', lax.all_gather(closing, ('req', 'mp'), axis=0,...  16.8 us
    dot_general x1, matrix products, per_device(): jnp.einsum('nmf,mfd->nmd', selected_rows, w_down, preferred_element_type=...  12.5 us
    all_to_all x1, blocking collectives, per_device(): incoming = lax.all_to_all(outgoing, ('req', 'mp'), 0, 0, tiled=True)  12.3 us
    dot_general x1, matrix products, per_device(): jnp.einsum('nmd,mdf->nmf', row_block, w_gate, preferred_element_type=jnp....  7.79 us
  transfers between devices with their start and end apart: 4, of which 4 were waited for; matrix products, arithmetic and copies ran while one was open for 0% of the time, Pallas kernels for 0%

profile of v6, /device:TPU:1, one launch (start us, length us, event | category | flops | bytes accessed | tf_op | source)
XLA Modules:
  0.0 282.9 jit_solution(1056622060839248833)
XLA Ops:
  7.2 0.0 reduce-scatter.3.cloned.1.call-start
  7.3 1.7 fusion.10
  9.0 0.8 fusion.106
  9.8 3.0 %fusion.23 = f32[256,256]{0,1} fusion(bf16[2,2048,256]{2,1,0:T(8,128)(2,1)} %param.20, bf16[256,2048]{1,0:T(8,128)(2,1)} %param.15, f32[2048]{0:T(1024)S(1)} %bitcast.136, f32[256]{0:T(256)S(1)} %add_rsqrt_fusion.2), kind=kOutput, calls=%fused_computation.41 | convolution fusion | flops 270532608 | bytes 2368512
  12.8 1.4 fusion.25
  14.2 1.8 convolution_bitcast_fusion.1
  16.0 1.8 convolution_bitcast_fusion
  17.9 0.2 reduce-window.4
  18.0 0.1 select_reduce_fusion.2
  18.1 0.1 fusion.33
  18.3 0.3 copy-done.8
  18.6 0.2 multiply_cosine_fusion.1
  18.8 0.2 fusion.74
  19.0 1.2 subtract_convert_fusion.1
  20.2 1.4 fusion.20
  21.5 1.1 fusion.112
  22.7 1.3 fusion.19
  24.0 1.1 fusion.107
  25.2 1.9 fusion.21
  27.0 2.4 fusion.22
  29.5 2.0 convolution_convert_fusion.3
  31.5 0.1 copy.38
  31.6 1.9 convolution_convert_fusion.2
  33.6 0.1 copy.39
  33.7 2.1 fusion.4
  35.8 0.0 reduce-scatter.3.cloned.1.call-update
  35.8 0.0 all-gather.3.cloned.1.call-start
  35.9 35.5 %reduce-scatter.3.cloned.1.call-done = bf16[32,2,2048]{2,0,1:T(8,128)(2,1)} async-done(((bf16[256,2,2048]{2,0,1:T(8,128)(2,1)}), bf16[32,2,2048]{2,0,1:T(8,128)(2,1)}) %reduce-scatter.3.cloned.1.call-update) | async-done | bytes 262160 | tf_op jit(solution)/shard_map/reduce_scatter | solution.py:137
  71.4 1.1 multiply_reduce_fusion.1
  72.5 1.8 multiply_convert_fusion.1
  74.3 0.2 reduce-scatter.5.cloned.1.call-start
  74.5 30.8 %all-gather.3.cloned.1.call-done = bf16[256,2,2048]{2,0,1:T(8,128)(2,1)} async-done(((bf16[32,2,2048]{2,0,1:T(8,128)(2,1)}), bf16[256,2,2048]{2,0,1:T(8,128)(2,1)}) %all-gather.3.cloned.1.call-update) | async-done | bytes 2097168 | tf_op jit(solution)/shard_map/all_gather | solution.py:148
  105.3 7.8 %fusion.118 = f32[2,256,1024]{2,1,0:T(8,128)} fusion(bf16[256,2,2048]{2,0,1:T(8,128)(2,1)} %all-gather.3.cloned.1.call-done, bf16[2,2048,1024]{2,1,0:T(8,128)(2,1)} %param.25), kind=kOutput, calls=%fused_computation.158 | convolution fusion | flops 2147483648 | bytes 12582912 | tf_op jit(solution)/shard_map/nmd,mdf->nmf/dot_general | solution.py:149
  113.1 12.5 %fusion.5 = bf16[256,2,2048]{2,0,1:T(8,128)(2,1)} fusion(bf16[2,1024,2048]{2,1,0:T(8,128)(2,1)} %param.27, f32[2,256,1024]{2,1,0:T(8,128)} %fusion.118, bf16[256,2,2048]{2,0,1:T(8,128)(2,1)S(1)} %copy-done.2, bf16[2,2048,1024]{2,1,0:T(8,128)(2,1)} %param.26), kind=kOutput, calls=%fused_computation.10 | convolution fusion | flops 4299161600 | bytes 23068672 | tf_op jit(solution)/shard_map/nmf,mfd->nmd/dot_general | solution.py:154
  125.7 0.3 all-gather.5.cloned.1.call-start
  125.9 32.3 %reduce-scatter.5.cloned.1.call-done = bf16[32,2,2048]{2,0,1:T(8,128)(2,1)} async-done(((bf16[256,2,2048]{2,0,1:T(8,128)(2,1)}), bf16[32,2,2048]{2,0,1:T(8,128)(2,1)}) %reduce-scatter.5.cloned.1.call-update) | async-done | bytes 262160 | tf_op jit(solution)/shard_map/reduce_scatter | solution.py:153
  158.2 1.1 multiply_reduce_fusion
  159.4 1.8 multiply_convert_fusion
  161.2 0.7 iota_compare_fusion
  161.9 78.3 %all-gather.5.cloned.1.call-done = bf16[1024,2,2048]{2,0,1:T(8,128)(2,1)} async-done(((bf16[32,2,2048]{2,0,1:T(8,128)(2,1)}), bf16[1024,2,2048]{2,0,1:T(8,128)(2,1)}) %all-gather.5.cloned.1.call-update) | async-done | bytes 8388624 | tf_op jit(solution)/shard_map/all_gather | solution.py:167
  240.2 16.8 %fusion.117 = (f32[2,1024]{1,0:T(2,128)S(1)}, f32[2,1024,1002]{1,2,0:T(8,128)}) fusion(bf16[1024,2,2048]{2,0,1:T(8,128)(2,1)} %all-gather.5.cloned.1.call-done, bf16[2,2048,1002]{1,0,2:T(2,128)(2,1)} %param.29), kind=kOutput, calls=%fused_computation.157 | convolution fusion | flops 8407435264 | bytes 24813568 | tf_op jit(solution)/shard_map/nmd,mdv->mnv/dot_general | solution.py:165
  257.1 4.6 %exponential_reduce_fusion = (f32[2,1024]{1,0:T(2,128)S(1)}, f32[2,1024]{1,0:T(2,128)S(1)}) fusion(f32[2,1024,1002]{1,2,0:T(8,128)} %get-tuple-element.26, f32[2,1024]{1,0:T(2,128)S(1)} %get-tuple-element.25, pred[1024,1002]{0,1:T(8,128)(4,1)S(1)} %iota_compare_fusion), kind=kLoop, calls=%fused_computation.5 | loop fusion | flops 8204288 | bytes 9259008 | tf_op jit(solution)/shard_map/reduce_sum | solution.py:172
  261.8 0.1 broadcast_in_dim.45
  261.8 12.3 %all_to_all.5 = f32[32,3,2,256]{3,2,1,0:T(2,128)S(1)} all-to-all(f32[32,3,2,256]{3,2,1,0:T(2,128)S(1)} %bitcast.131), channel_id=1, replica_groups=mesh['req'=4,'mp'=8] {'req','mp'}, dimensions={0} | all-to-all | bytes 393216 | tf_op jit(solution)/shard_map/all_to_all | solution.py:185
  274.2 0.1 fusion.45
  274.4 0.7 select_reduce_fusion.1
  275.1 0.6 dynamic_slice.15
  275.6 0.7 fusion.76
  (59 shorter events, 0.4 us)
Async XLA Ops:
  7.2 26.5 %copy-start = (bf16[2,256,2048]{2,1,0:T(8,128)(2,1)S(1)}, bf16[2,256,2048]{2,1,0:T(8,128)(2,1)}, u32[]{:S(2)}) copy-start(bf16[2,256,2048]{2,1,0:T(8,128)(2,1)} %param.23) | copy-start | bytes 6291460
  7.2 64.2 %reduce-scatter.3.cloned.1.call-start = ((), (), s32[]{:S(2)}) async-start(), calls=%async_computation.3 | async-start | bytes 2359296 | tf_op jit(solution)/shard_map/reduce_scatter | solution.py:137
  7.3 5.6 %copy-start.4 = (bf16[256,2048]{1,0:T(8,128)(2,1)S(1)}, bf16[256,2048]{1,0:T(8,128)(2,1)}, u32[]{:S(2)}) copy-start(bf16[256,2048]{1,0:T(8,128)(2,1)} %param.15) | copy-start | bytes 3145732
  9.0 7.1 %copy-start.12 = (f32[256]{0:T(256)}, f32[256]{0:T(256)S(1)}, u32[]{:S(2)}) copy-start(f32[256]{0:T(256)S(1)} %add_rsqrt_fusion.2) | copy-start | bytes 3076
  9.8 3.1 %copy-start.15 = (bf16[2,2048,256]{2,1,0:T(8,128)(2,1)S(1)}, bf16[2,2048,256]{2,1,0:T(8,128)(2,1)}, u32[]{:S(2)}) copy-start(bf16[2,2048,256]{2,1,0:T(8,128)(2,1)} %param.20) | copy-start | bytes 6291460
  14.2 3.6 %copy-start.16 = (s32[1,8]{1,0:T(1,128)S(1)}, s32[1,8]{1,0:T(1,128)}, u32[]{:S(2)}) copy-start(s32[1,8]{1,0:T(1,128)} %param.16) | copy-start | bytes 100
  18.0 0.5 copy-start.8
  18.0 0.5 copy-start.10
  22.7 2.5 copy-start.13
  25.2 4.3 %copy-start.17 = (f32[4,256]{1,0:T(4,128)S(1)}, f32[4,256]{1,0:T(4,128)}, u32[]{:S(2)}) copy-start(f32[4,256]{1,0:T(4,128)} %fusion.112) | copy-start | bytes 12292
  29.5 2.2 copy-start.18
  35.8 36.7 %copy-start.6 = (f32[2,2048]{1,0:T(2,128)S(1)}, f32[2,2048]{1,0:T(2,128)}, u32[]{:S(2)}) copy-start(f32[2,2048]{1,0:T(2,128)} %param.24) | copy-start | bytes 49156
  35.8 69.5 %all-gather.3.cloned.1.call-start = ((), (), s32[]{:S(2)}) async-start(), calls=%async_computation.4 | async-start | bytes 2359296 | tf_op jit(solution)/shard_map/all_gather | solution.py:148
  74.3 83.9 %reduce-scatter.5.cloned.1.call-start = ((), (), s32[]{:S(2)}) async-start(), calls=%async_computation.5 | async-start | bytes 2359296 | tf_op jit(solution)/shard_map/reduce_scatter | solution.py:153
  105.3 7.8 %copy-start.2 = (bf16[256,2,2048]{2,0,1:T(8,128)(2,1)S(1)}, bf16[256,2,2048]{2,0,1:T(8,128)(2,1)}, u32[]{:S(2)}) copy-start(bf16[256,2,2048]{2,0,1:T(8,128)(2,1)} %all-gather.3.cloned.1.call-done) | copy-start | bytes 6291460
  125.6 32.6 %copy-start.3 = (bf16[32,2,2048]{2,0,1:T(8,128)(2,1)S(1)}, bf16[32,2,2048]{2,0,1:T(8,128)(2,1)}, u32[]{:S(2)}) copy-start(bf16[32,2,2048]{2,0,1:T(8,128)(2,1)} %reduce-scatter.3.cloned.1.call-done) | copy-start | bytes 786436
  125.6 33.8 %copy-start.5 = (f32[2,2048]{1,0:T(2,128)S(1)}, f32[2,2048]{1,0:T(2,128)}, u32[]{:S(2)}) copy-start(f32[2,2048]{1,0:T(2,128)} %param.28) | copy-start | bytes 49156
  125.6 35.6 %copy-start.7 = (s32[1024]{0:T(1024)S(1)}, s32[1024]{0:T(1024)}, u32[]{:S(2)}) copy-start(s32[1024]{0:T(1024)} %param.18) | copy-start | bytes 12292
  125.7 114.6 %all-gather.5.cloned.1.call-start = ((), (), s32[]{:S(2)}) async-start(), calls=%async_computation.6 | async-start | bytes 8650752 | tf_op jit(solution)/shard_map/all_gather | solution.py:167
  257.1 17.2 %copy-start.14 = (s32[256]{0:T(256)S(1)}, s32[256]{0:T(256)}, u32[]{:S(2)}) copy-start(s32[256]{0:T(256)} %param.17) | copy-start | bytes 3076
  257.1 17.2 %copy-start.9 = (s32[8,1]{0,1:T(1,128)S(1)}, s32[8,1]{0,1:T(1,128)}, u32[]{:S(2)}) copy-start(s32[8,1]{0,1:T(1,128)} %copy-done.8) | copy-start | bytes 100
  257.1 17.2 %copy-start.11 = (s32[8]{0:T(128)S(1)}, s32[8]{0:T(128)}, u32[]{:S(2)}) copy-start(s32[8]{0:T(128)} %copy-done.10) | copy-start | bytes 100
  257.1 19.2 %copy-start.1 = (bf16[2,256,2048]{2,1,0:T(8,128)(2,1)S(1)}, bf16[2,256,2048]{2,1,0:T(8,128)(2,1)}, u32[]{:S(2)}) copy-start(bf16[2,256,2048]{2,1,0:T(8,128)(2,1)} %param.23) | copy-start | bytes 6291460
Sparse Core Ops, SparseCore 0:
  35.9 35.4 reduce-scatter.2
  74.4 30.8 all-gather.2
  125.8 32.4 reduce-scatter.4
  161.3 78.8 all-gather.4

commit v7 on v5

--- a/solution.py
+++ b/solution.py
@@ -58,16 +58,10 @@
 
 
 def attend_heads(query, key_rows, value_rows, positions, allowed, repeat_times):
-    slot_count = query.shape[0]
-    query = rotate(query.reshape(slot_count, -1, HEAD_DIM).transpose(1, 0, 2), positions).astype(
-        jnp.bfloat16
-    )
-    key_rows = rotate(
-        key_rows.reshape(slot_count, -1, HEAD_DIM).transpose(1, 0, 2), positions
-    ).astype(jnp.bfloat16)
-    value_rows = (
-        value_rows.reshape(slot_count, -1, HEAD_DIM).transpose(1, 0, 2).astype(jnp.bfloat16)
-    )
+    slot_count = query.shape[1]
+    query = rotate(query, positions).astype(jnp.bfloat16)
+    key_rows = rotate(key_rows, positions).astype(jnp.bfloat16)
+    value_rows = value_rows.astype(jnp.bfloat16)
     key_rows = jnp.repeat(key_rows, repeat_times, axis=0)
     value_rows = jnp.repeat(value_rows, repeat_times, axis=0)
     scores = jnp.einsum(
@@ -112,14 +106,35 @@
     key_cols = lax.dynamic_slice_in_dim(w_key, kv_first, kv_here * HEAD_DIM, 2)
     value_columns = lax.dynamic_slice_in_dim(w_value, kv_first, kv_here * HEAD_DIM, 2)
     attended_list = []
+    normed = rms_scale(tokens[None], attn_gain[:, None, :]).astype(jnp.bfloat16)
+    width = tokens.shape[1]
+    query = jnp.einsum(
+        "mtd,mdhe->mhte",
+        normed,
+        w_query.reshape(2, width, heads_here, HEAD_DIM),
+        preferred_element_type=jnp.float32,
+    )
+    keys_here = jnp.einsum(
+        "mtd,mdhe->mhte",
+        normed,
+        key_cols.reshape(2, width, kv_here, HEAD_DIM),
+        preferred_element_type=jnp.float32,
+    )
+    values_here = jnp.einsum(
+        "mtd,mdhe->mhte",
+        normed,
+        value_columns.reshape(2, width, kv_here, HEAD_DIM),
+        preferred_element_type=jnp.float32,
+    )
     for model in range(2):
-        normed = rms_scale(tokens, attn_gain[model]).astype(jnp.bfloat16)
-        query = jnp.dot(normed, w_query[model], preferred_element_type=jnp.float32)
-        keys_here = jnp.dot(normed, key_cols[model], preferred_element_type=jnp.float32)
-        values_here = jnp.dot(normed, value_columns[model], preferred_element_type=jnp.float32)
         attended_list.append(
             attend_heads(
-                query, keys_here, values_here, positions, allowed, min(sharing, heads_here)
+                query[model],
+                keys_here[model],
+                values_here[model],
+                positions,
+                allowed,
+                min(sharing, heads_here),
             )
         )
     attended = jnp.stack(attended_list, axis=1)

time: 290 us -> 278 us (0.959)
  local copies, waits for them, and re-layouts: 8.22 us -> 1.05 us
  matrix products: 60 us -> 55.4 us
    dot_general x3 -> x0, local copies, waits for them, and re-layouts: 6.39 us -> none  [per_device(): query = jnp.dot(normed, w_query[model], preferred_element_type=jnp.float32)]
    dot_general x6 -> x2, matrix products: 11.7 us -> 6.56 us  [the longest x1 3.28 us: per_device(): jnp.einsum('mtd,mdhe->mhte', normed, value_columns.reshape(2, width, kv_h...]
    unnamed x0 -> x1, matrix products: none -> 3.19 us
  transfers between devices with their start and end apart: 4 -> 4, of which waited for: 4 -> 4; matrix products, arithmetic and copies ran while one was open for 0% -> 1% of each run, Pallas kernels for 0% -> 0%
where the time goes in v7:
time: 278 us
  waiting for transfers between devices  176 us (63%)
  matrix products  55.4 us (20%)
  other arithmetic  18.3 us (7%)
  between operations  14.1 us (5%)
  blocking collectives  12.3 us (4%)
    all_gather x1, waiting for transfers between devices, per_device(): lax.all_gather(closing, ('req', 'mp'), axis=0, tiled=True)  78.3 us
    reduce_scatter x1, waiting for transfers between devices, per_device(): lax.psum_scatter(jnp.einsum('kbq,bqo->kbo', selected_rows, output_weight,...  34.5 us
    reduce_scatter x1, waiting for transfers between devices, per_device(): lax.psum_scatter(jnp.einsum('nmf,mfd->nmd', selected_rows, w_down, prefer...  32.3 us
    all_gather x1, waiting for transfers between devices, per_device(): row_block = lax.all_gather(normed_mid, 'mp', axis=0, tiled=True)  30.9 us
    dot_general x1, matrix products, per_device(): jnp.einsum('nmd,mdv->mnv', lax.all_gather(closing, ('req', 'mp'), axis=0,...  16.9 us
    dot_general x1, matrix products, per_device(): jnp.einsum('nmf,mfd->nmd', selected_rows, w_down, preferred_element_type=...  12.5 us
    all_to_all x1, blocking collectives, per_device(): incoming = lax.all_to_all(outgoing, ('req', 'mp'), 0, 0, tiled=True)  12.3 us
    dot_general x1, matrix products, per_device(): jnp.einsum('nmd,mdf->nmf', row_block, w_gate, preferred_element_type=jnp....  7.79 us
  transfers between devices with their start and end apart: 4, of which 4 were waited for; matrix products, arithmetic and copies ran while one was open for 1% of the time, Pallas kernels for 0%

profile of v7, /device:TPU:1, one launch (start us, length us, event | category | flops | bytes accessed | tf_op | source)
XLA Modules:
  0.0 277.7 jit_solution(3347843028871157335)
XLA Ops:
  7.2 0.0 reduce-scatter.3.cloned.1.call-start
  7.3 1.6 fusion.9
  8.9 2.8 %convert_multiply_fusion = f32[256,2048]{1,0:T(8,128)} fusion(bf16[256,2048]{1,0:T(8,128)(2,1)} %param.15, f32[256]{0:T(256)S(1)} %add_rsqrt_fusion.2), kind=kLoop, calls=%fused_computation.15 | loop fusion | flops 1048576 | bytes 3146752 | tf_op jit(solution)/shard_map/mul | solution.py:29
  11.7 3.3 %fusion.5 = f32[2,64,256]{2,1,0:T(8,128)S(1)} fusion(f32[2,2048]{1,0:T(2,128)S(1)} %copy-done.4, f32[256,2048]{1,0:T(8,128)} %convert_multiply_fusion, bf16[2,2048,512]{2,1,0:T(8,128)(2,1)} %param.21, s32[]{:T(128)S(6)} %select_n.31), kind=kOutput, calls=%fused_computation.9 | convolution fusion | flops 136314880 | bytes 3293188 | tf_op jit(solution)/shard_map/mtd,mdhe->mhte/dot_general | solution.py:117
  15.1 0.2 reduce-window.4
  15.2 0.1 select_reduce_fusion.2
  15.3 3.2 %fusion.6 = f32[2,256,256]{1,2,0:S(1)} fusion(bf16[2,2048,256]{2,1,0:T(8,128)(2,1)} %param.20, f32[2,2048]{1,0:T(2,128)S(1)} %copy-done.4, f32[256,2048]{1,0:T(8,128)} %convert_multiply_fusion), kind=kOutput, calls=%fused_computation.10 | convolution fusion | flops 538968064 | bytes 4734976
  18.6 0.1 fusion.34
  18.7 0.2 multiply_cosine_fusion.1
  18.9 0.2 fusion.75
  19.1 0.1 subtract_convert_fusion.1
  19.2 0.3 fusion.25
  19.6 1.1 fusion.104
  20.7 1.3 fusion.24
  22.0 0.5 fusion.99
  22.6 3.3 %fusion.27 = bf16[2,1,256,64]{2,3,0,1:T(8,128)(2,1)S(1)} fusion(f32[2,2048]{1,0:T(2,128)S(1)} %copy-done.4, f32[256,2048]{1,0:T(8,128)} %convert_multiply_fusion, bf16[2,2048,512]{2,1,0:T(8,128)(2,1)} %param.22, s32[]{:T(128)S(6)} %select_n.31), kind=kOutput, calls=%fused_computation.42 | convolution fusion | flops 136347648 | bytes 3227652 | tf_op jit(solution)/shard_map/mtd,mdhe->mhte/dot_general | solution.py:123
  25.9 0.4 convolution_convert_fusion.3
  26.3 0.1 copy.55
  26.4 1.9 convolution_convert_fusion.2
  28.3 0.1 copy.56
  28.5 2.1 fusion.7
  30.5 0.0 reduce-scatter.3.cloned.1.call-update
  30.6 0.0 all-gather.3.cloned.1.call-start
  30.6 0.9 dynamic-slice_convert_fusion
  31.5 34.5 %reduce-scatter.3.cloned.1.call-done = bf16[32,2,2048]{2,0,1:T(8,128)(2,1)} async-done(((bf16[256,2,2048]{2,0,1:T(8,128)(2,1)}), bf16[32,2,2048]{2,0,1:T(8,128)(2,1)}) %reduce-scatter.3.cloned.1.call-update) | async-done | bytes 262160 | tf_op jit(solution)/shard_map/reduce_scatter | solution.py:142
  66.1 1.1 multiply_reduce_fusion.1
  67.2 1.8 multiply_convert_fusion.9
  69.0 0.0 all-gather.3.cloned.1.call-update
  69.0 0.2 reduce-scatter.5.cloned.1.call-start
  69.2 30.9 %all-gather.3.cloned.1.call-done = bf16[256,2,2048]{2,0,1:T(8,128)(2,1)} async-done(((bf16[32,2,2048]{2,0,1:T(8,128)(2,1)}), bf16[256,2,2048]{2,0,1:T(8,128)(2,1)}) %all-gather.3.cloned.1.call-update) | async-done | bytes 2097168 | tf_op jit(solution)/shard_map/all_gather | solution.py:153
  100.1 7.8 %fusion.110 = f32[2,256,1024]{2,1,0:T(8,128)} fusion(bf16[256,2,2048]{2,0,1:T(8,128)(2,1)} %all-gather.3.cloned.1.call-done, bf16[2,2048,1024]{2,1,0:T(8,128)(2,1)} %param.25), kind=kOutput, calls=%fused_computation.155 | convolution fusion | flops 2147483648 | bytes 12582912 | tf_op jit(solution)/shard_map/nmd,mdf->nmf/dot_general | solution.py:154
  107.9 12.5 %fusion.8 = bf16[256,2,2048]{2,0,1:T(8,128)(2,1)} fusion(bf16[2,1024,2048]{2,1,0:T(8,128)(2,1)} %param.27, f32[2,256,1024]{2,1,0:T(8,128)} %fusion.110, bf16[256,2,2048]{2,0,1:T(8,128)(2,1)S(1)} %copy-done.2, bf16[2,2048,1024]{2,1,0:T(8,128)(2,1)} %param.26), kind=kOutput, calls=%fused_computation.14 | convolution fusion | flops 4299161600 | bytes 23068672 | tf_op jit(solution)/shard_map/nmf,mfd->nmd/dot_general | solution.py:159
  120.4 0.0 reduce-scatter.5.cloned.1.call-update
  120.5 0.3 all-gather.5.cloned.1.call-start
  120.7 32.3 %reduce-scatter.5.cloned.1.call-done = bf16[32,2,2048]{2,0,1:T(8,128)(2,1)} async-done(((bf16[256,2,2048]{2,0,1:T(8,128)(2,1)}), bf16[32,2,2048]{2,0,1:T(8,128)(2,1)}) %reduce-scatter.5.cloned.1.call-update) | async-done | bytes 262160 | tf_op jit(solution)/shard_map/reduce_scatter | solution.py:158
  153.0 1.1 multiply_reduce_fusion
  154.2 1.8 multiply_convert_fusion.8
  156.0 0.0 all-gather.5.cloned.1.call-update
  156.0 0.7 iota_compare_fusion
  156.8 78.3 %all-gather.5.cloned.1.call-done = bf16[1024,2,2048]{2,0,1:T(8,128)(2,1)} async-done(((bf16[32,2,2048]{2,0,1:T(8,128)(2,1)}), bf16[1024,2,2048]{2,0,1:T(8,128)(2,1)}) %all-gather.5.cloned.1.call-update) | async-done | bytes 8388624 | tf_op jit(solution)/shard_map/all_gather | solution.py:172
  235.1 16.9 %fusion.109 = (f32[2,1024]{1,0:T(2,128)S(1)}, f32[2,1024,1002]{1,2,0:T(8,128)}) fusion(bf16[1024,2,2048]{2,0,1:T(8,128)(2,1)} %all-gather.5.cloned.1.call-done, bf16[2,2048,1002]{1,0,2:T(2,128)(2,1)} %param.29), kind=kOutput, calls=%fused_computation.154 | convolution fusion | flops 8407435264 | bytes 24813568 | tf_op jit(solution)/shard_map/nmd,mdv->mnv/dot_general | solution.py:170
  252.0 4.6 %exponential_reduce_fusion = (f32[2,1024]{1,0:T(2,128)S(1)}, f32[2,1024]{1,0:T(2,128)S(1)}) fusion(f32[2,1024,1002]{1,2,0:T(8,128)} %get-tuple-element.28, f32[2,1024]{1,0:T(2,128)S(1)} %get-tuple-element.27, pred[1024,1002]{0,1:T(8,128)(4,1)S(1)} %iota_compare_fusion), kind=kLoop, calls=%fused_computation.5 | loop fusion | flops 8204288 | bytes 9259008 | tf_op jit(solution)/shard_map/reduce_sum | solution.py:177
  256.6 0.1 broadcast_in_dim.45
  256.7 12.3 %all_to_all.5 = f32[32,3,2,256]{3,2,1,0:T(2,128)S(1)} all-to-all(f32[32,3,2,256]{3,2,1,0:T(2,128)S(1)} %bitcast.108), channel_id=1, replica_groups=mesh['req'=4,'mp'=8] {'req','mp'}, dimensions={0} | all-to-all | bytes 393216 | tf_op jit(solution)/shard_map/all_to_all | solution.py:190
  269.1 0.1 fusion.46
  269.2 0.7 select_reduce_fusion.1
  269.9 0.6 dynamic_slice.15
  270.5 0.7 fusion.77
  (52 shorter events, 0.4 us)
Async XLA Ops:
  7.2 21.3 %copy-start = (bf16[2,256,2048]{2,1,0:T(8,128)(2,1)S(1)}, bf16[2,256,2048]{2,1,0:T(8,128)(2,1)}, u32[]{:S(2)}) copy-start(bf16[2,256,2048]{2,1,0:T(8,128)(2,1)} %param.23) | copy-start | bytes 6291460
  7.2 58.9 %reduce-scatter.3.cloned.1.call-start = ((), (), s32[]{:S(2)}) async-start(), calls=%async_computation.3 | async-start | bytes 2359296 | tf_op jit(solution)/shard_map/reduce_scatter | solution.py:142
  7.3 4.5 %copy-start.4 = (f32[2,2048]{1,0:T(2,128)S(1)}, f32[2,2048]{1,0:T(2,128)}, u32[]{:S(2)}) copy-start(f32[2,2048]{1,0:T(2,128)} %param.19) | copy-start | bytes 49156
  11.7 3.3 %copy-start.13 = (s32[1,8]{1,0:T(1,128)S(1)}, s32[1,8]{1,0:T(1,128)}, u32[]{:S(2)}) copy-start(s32[1,8]{1,0:T(1,128)} %param.16) | copy-start | bytes 100
  15.2 3.3 %copy-start.8 = (s32[8,1]{0,1:T(1,128)}, s32[8,1]{0,1:T(1,128)S(1)}, u32[]{:S(2)}) copy-start(s32[8,1]{0,1:T(1,128)S(1)} %reduce-window.4) | copy-start | bytes 100
  15.2 3.3 %copy-start.10 = (s32[8]{0:T(128)}, s32[8]{0:T(128)S(1)}, u32[]{:S(2)}) copy-start(s32[8]{0:T(128)S(1)} %fusion.83) | copy-start | bytes 100
  22.6 3.3 %copy-start.14 = (f32[4,256]{1,0:T(4,128)S(1)}, f32[4,256]{1,0:T(4,128)}, u32[]{:S(2)}) copy-start(f32[4,256]{1,0:T(4,128)} %fusion.104) | copy-start | bytes 12292
  30.5 36.6 %copy-start.6 = (f32[2,2048]{1,0:T(2,128)S(1)}, f32[2,2048]{1,0:T(2,128)}, u32[]{:S(2)}) copy-start(f32[2,2048]{1,0:T(2,128)} %param.24) | copy-start | bytes 49156
  30.6 69.6 %all-gather.3.cloned.1.call-start = ((), (), s32[]{:S(2)}) async-start(), calls=%async_computation.4 | async-start | bytes 2359296 | tf_op jit(solution)/shard_map/all_gather | solution.py:153
  69.0 84.0 %reduce-scatter.5.cloned.1.call-start = ((), (), s32[]{:S(2)}) async-start(), calls=%async_computation.5 | async-start | bytes 2359296 | tf_op jit(solution)/shard_map/reduce_scatter | solution.py:158
  100.1 7.8 %copy-start.2 = (bf16[256,2,2048]{2,0,1:T(8,128)(2,1)S(1)}, bf16[256,2,2048]{2,0,1:T(8,128)(2,1)}, u32[]{:S(2)}) copy-start(bf16[256,2,2048]{2,0,1:T(8,128)(2,1)} %all-gather.3.cloned.1.call-done) | copy-start | bytes 6291460
  120.4 32.6 %copy-start.3 = (bf16[32,2,2048]{2,0,1:T(8,128)(2,1)S(1)}, bf16[32,2,2048]{2,0,1:T(8,128)(2,1)}, u32[]{:S(2)}) copy-start(bf16[32,2,2048]{2,0,1:T(8,128)(2,1)} %reduce-scatter.3.cloned.1.call-done) | copy-start | bytes 786436
  120.4 33.8 %copy-start.5 = (f32[2,2048]{1,0:T(2,128)S(1)}, f32[2,2048]{1,0:T(2,128)}, u32[]{:S(2)}) copy-start(f32[2,2048]{1,0:T(2,128)} %param.28) | copy-start | bytes 49156
  120.4 35.6 %copy-start.7 = (s32[1024]{0:T(1024)S(1)}, s32[1024]{0:T(1024)}, u32[]{:S(2)}) copy-start(s32[1024]{0:T(1024)} %param.18) | copy-start | bytes 12292
  120.5 114.6 %all-gather.5.cloned.1.call-start = ((), (), s32[]{:S(2)}) async-start(), calls=%async_computation.6 | async-start | bytes 8650752 | tf_op jit(solution)/shard_map/all_gather | solution.py:172
  251.9 17.2 %copy-start.12 = (s32[256]{0:T(256)S(1)}, s32[256]{0:T(256)}, u32[]{:S(2)}) copy-start(s32[256]{0:T(256)} %param.17) | copy-start | bytes 3076
  252.0 17.2 %copy-start.9 = (s32[8,1]{0,1:T(1,128)S(1)}, s32[8,1]{0,1:T(1,128)}, u32[]{:S(2)}) copy-start(s32[8,1]{0,1:T(1,128)} %copy-done.8) | copy-start | bytes 100
  252.0 17.2 %copy-start.11 = (s32[8]{0:T(128)S(1)}, s32[8]{0:T(128)}, u32[]{:S(2)}) copy-start(s32[8]{0:T(128)} %copy-done.10) | copy-start | bytes 100
  252.0 19.2 %copy-start.1 = (bf16[2,256,2048]{2,1,0:T(8,128)(2,1)S(1)}, bf16[2,256,2048]{2,1,0:T(8,128)(2,1)}, u32[]{:S(2)}) copy-start(bf16[2,256,2048]{2,1,0:T(8,128)(2,1)} %param.23) | copy-start | bytes 6291460
Sparse Core Ops, SparseCore 0:
  30.7 35.3 reduce-scatter.2
  69.1 30.9 all-gather.2
  120.6 32.4 reduce-scatter.4
  156.1 78.9 all-gather.4

commit v8 on v7

--- a/solution.py
+++ b/solution.py
@@ -103,8 +103,6 @@
     sharing = HEADS // KV_HEADS
     kv_here = max(1, heads_here // sharing)
     kv_first = mp_index * heads_here // sharing * HEAD_DIM
-    key_cols = lax.dynamic_slice_in_dim(w_key, kv_first, kv_here * HEAD_DIM, 2)
-    value_columns = lax.dynamic_slice_in_dim(w_value, kv_first, kv_here * HEAD_DIM, 2)
     attended_list = []
     normed = rms_scale(tokens[None], attn_gain[:, None, :]).astype(jnp.bfloat16)
     width = tokens.shape[1]
@@ -114,17 +112,29 @@
         w_query.reshape(2, width, heads_here, HEAD_DIM),
         preferred_element_type=jnp.float32,
     )
-    keys_here = jnp.einsum(
-        "mtd,mdhe->mhte",
-        normed,
-        key_cols.reshape(2, width, kv_here, HEAD_DIM),
-        preferred_element_type=jnp.float32,
-    )
-    values_here = jnp.einsum(
-        "mtd,mdhe->mhte",
-        normed,
-        value_columns.reshape(2, width, kv_here, HEAD_DIM),
-        preferred_element_type=jnp.float32,
+    kv_heads = w_key.shape[2] // HEAD_DIM
+    kv_head_first = kv_first // HEAD_DIM
+    keys_here = lax.dynamic_slice_in_dim(
+        jnp.einsum(
+            "mtd,mdhe->mhte",
+            normed,
+            w_key.reshape(2, width, kv_heads, HEAD_DIM),
+            preferred_element_type=jnp.float32,
+        ),
+        kv_head_first,
+        kv_here,
+        1,
+    )
+    values_here = lax.dynamic_slice_in_dim(
+        jnp.einsum(
+            "mtd,mdhe->mhte",
+            normed,
+            w_value.reshape(2, width, kv_heads, HEAD_DIM),
+            preferred_element_type=jnp.float32,
+        ),
+        kv_head_first,
+        kv_here,
+        1,
     )
     for model in range(2):
         attended_list.append(

time: 278 us -> 280 us (level)
    unnamed x1 -> x3, matrix products: 3.19 us -> 11.4 us
    dot_general x2 -> x0, matrix products: 6.56 us -> none  [the longest x1 3.28 us: per_device(): jnp.einsum('mtd,mdhe->mhte', normed, value_columns.reshape(2, width, kv_h...]
where the time goes in v8:
time: 280 us
  waiting for transfers between devices  176 us (63%)
  matrix products  57 us (20%)
  other arithmetic  18.2 us (6%)
  between operations  14.2 us (5%)
  blocking collectives  12.3 us (4%)
    all_gather x1, waiting for transfers between devices, per_device(): lax.all_gather(closing, ('req', 'mp'), axis=0, tiled=True)  78.2 us
    reduce_scatter x1, waiting for transfers between devices, per_device(): lax.psum_scatter(jnp.einsum('kbq,bqo->kbo', selected_rows, output_weight,...  34.6 us
    reduce_scatter x1, waiting for transfers between devices, per_device(): lax.psum_scatter(jnp.einsum('nmf,mfd->nmd', selected_rows, w_down, prefer...  32.3 us
    all_gather x1, waiting for transfers between devices, per_device(): row_block = lax.all_gather(normed_mid, 'mp', axis=0, tiled=True)  30.8 us
    dot_general x1, matrix products, per_device(): jnp.einsum('nmd,mdv->mnv', lax.all_gather(closing, ('req', 'mp'), axis=0,...  16.9 us
    dot_general x1, matrix products, per_device(): jnp.einsum('nmf,mfd->nmd', selected_rows, w_down, preferred_element_type=...  12.6 us
    all_to_all x1, blocking collectives, per_device(): incoming = lax.all_to_all(outgoing, ('req', 'mp'), 0, 0, tiled=True)  12.3 us
    unnamed x3, matrix products  11.4 us
  transfers between devices with their start and end apart: 4, of which 4 were waited for; matrix products, arithmetic and copies ran while one was open for 1% of the time, Pallas kernels for 0%

profile of v8, /device:TPU:1, one launch (start us, length us, event | category | flops | bytes accessed | tf_op | source)
XLA Modules:
  0.0 280.1 jit_solution(2865649471352032626)
XLA Ops:
  7.2 0.0 reduce-scatter.3.cloned.1.call-start
  7.3 1.6 fusion.9
  9.0 2.8 convert_multiply_fusion
  11.7 0.2 reduce-window.4
  11.9 0.1 select_reduce_fusion.2
  12.1 5.7 %fusion.5 = f32[2,256,512]{1,2,0} fusion(bf16[2,2048,512]{2,1,0:T(8,128)(2,1)} %param.21, f32[2,2048]{1,0:T(2,128)S(1)} %copy-done.6, f32[256,2048]{1,0:T(8,128)} %convert_multiply_fusion), kind=kOutput, calls=%fused_computation.9 | convolution fusion | flops 1075838976 | bytes 7356416
  17.8 1.1 fusion.6
  18.9 0.1 fusion.30
  19.1 0.2 multiply_cosine_fusion.1
  19.3 0.9 dynamic-slice_bitcast_fusion.1
  20.2 0.2 fusion.71
  20.4 0.1 subtract_convert_fusion.1
  20.5 0.3 fusion.25
  20.8 1.1 fusion.98
  22.0 1.3 fusion.24
  23.3 0.5 fusion.93
  23.8 4.6 %fusion.4 = f32[2,256,512]{1,2,0:S(1)} fusion(bf16[2,2048,512]{2,1,0:T(8,128)(2,1)} %param.22, f32[2,2048]{1,0:T(2,128)S(1)} %copy-done.6, f32[256,2048]{1,0:T(8,128)} %convert_multiply_fusion), kind=kOutput, calls=%fused_computation.8 | convolution fusion | flops 1075838976 | bytes 7356416
  28.5 0.4 convolution_convert_fusion.3
  28.8 0.1 copy.51
  29.0 1.9 convolution_convert_fusion.2
  30.9 0.1 copy.52
  31.0 2.1 fusion.7
  33.1 0.0 reduce-scatter.3.cloned.1.call-update
  33.1 0.0 all-gather.3.cloned.1.call-start
  33.2 0.9 dynamic-slice_convert_fusion.1
  34.1 34.6 %reduce-scatter.3.cloned.1.call-done = bf16[32,2,2048]{2,0,1:T(8,128)(2,1)} async-done(((bf16[256,2,2048]{2,0,1:T(8,128)(2,1)}), bf16[32,2,2048]{2,0,1:T(8,128)(2,1)}) %reduce-scatter.3.cloned.1.call-update) | async-done | bytes 262160 | tf_op jit(solution)/shard_map/reduce_scatter | solution.py:152
  68.7 1.1 multiply_reduce_fusion.1
  69.8 1.8 multiply_convert_fusion.5
  71.6 0.0 all-gather.3.cloned.1.call-update
  71.6 0.2 reduce-scatter.5.cloned.1.call-start
  71.8 30.8 %all-gather.3.cloned.1.call-done = bf16[256,2,2048]{2,0,1:T(8,128)(2,1)} async-done(((bf16[32,2,2048]{2,0,1:T(8,128)(2,1)}), bf16[256,2,2048]{2,0,1:T(8,128)(2,1)}) %all-gather.3.cloned.1.call-update) | async-done | bytes 2097168 | tf_op jit(solution)/shard_map/all_gather | solution.py:163
  102.6 7.8 %fusion.104 = f32[2,256,1024]{2,1,0:T(8,128)} fusion(bf16[256,2,2048]{2,0,1:T(8,128)(2,1)} %all-gather.3.cloned.1.call-done, bf16[2,2048,1024]{2,1,0:T(8,128)(2,1)} %param.25), kind=kOutput, calls=%fused_computation.150 | convolution fusion | flops 2147483648 | bytes 12582912 | tf_op jit(solution)/shard_map/nmd,mdf->nmf/dot_general | solution.py:164
  110.4 12.6 %fusion.8 = bf16[256,2,2048]{2,0,1:T(8,128)(2,1)} fusion(bf16[2,1024,2048]{2,1,0:T(8,128)(2,1)} %param.27, f32[2,256,1024]{2,1,0:T(8,128)} %fusion.104, bf16[256,2,2048]{2,0,1:T(8,128)(2,1)S(1)} %copy-done.2, bf16[2,2048,1024]{2,1,0:T(8,128)(2,1)} %param.26), kind=kOutput, calls=%fused_computation.14 | convolution fusion | flops 4299161600 | bytes 23068672 | tf_op jit(solution)/shard_map/nmf,mfd->nmd/dot_general | solution.py:169
  123.0 0.3 all-gather.5.cloned.1.call-start
  123.2 32.3 %reduce-scatter.5.cloned.1.call-done = bf16[32,2,2048]{2,0,1:T(8,128)(2,1)} async-done(((bf16[256,2,2048]{2,0,1:T(8,128)(2,1)}), bf16[32,2,2048]{2,0,1:T(8,128)(2,1)}) %reduce-scatter.5.cloned.1.call-update) | async-done | bytes 262160 | tf_op jit(solution)/shard_map/reduce_scatter | solution.py:168
  155.5 1.1 multiply_reduce_fusion
  156.7 1.8 multiply_convert_fusion.4
  158.5 0.0 all-gather.5.cloned.1.call-update
  158.5 0.7 iota_compare_fusion
  159.3 78.2 %all-gather.5.cloned.1.call-done = bf16[1024,2,2048]{2,0,1:T(8,128)(2,1)} async-done(((bf16[32,2,2048]{2,0,1:T(8,128)(2,1)}), bf16[1024,2,2048]{2,0,1:T(8,128)(2,1)}) %all-gather.5.cloned.1.call-update) | async-done | bytes 8388624 | tf_op jit(solution)/shard_map/all_gather | solution.py:182
  237.5 16.9 %fusion.103 = (f32[2,1024]{1,0:T(2,128)S(1)}, f32[2,1024,1002]{1,2,0:T(8,128)}) fusion(bf16[1024,2,2048]{2,0,1:T(8,128)(2,1)} %all-gather.5.cloned.1.call-done, bf16[2,2048,1002]{1,0,2:T(2,128)(2,1)} %param.29), kind=kOutput, calls=%fused_computation.149 | convolution fusion | flops 8407435264 | bytes 24813568 | tf_op jit(solution)/shard_map/nmd,mdv->mnv/dot_general | solution.py:180
  254.4 4.6 %exponential_reduce_fusion = (f32[2,1024]{1,0:T(2,128)S(1)}, f32[2,1024]{1,0:T(2,128)S(1)}) fusion(f32[2,1024,1002]{1,2,0:T(8,128)} %get-tuple-element.30, f32[2,1024]{1,0:T(2,128)S(1)} %get-tuple-element.29, pred[1024,1002]{0,1:T(8,128)(4,1)S(1)} %iota_compare_fusion), kind=kLoop, calls=%fused_computation.5 | loop fusion | flops 8204288 | bytes 9259008 | tf_op jit(solution)/shard_map/reduce_sum | solution.py:187
  259.0 0.1 broadcast_in_dim.45
  259.1 12.3 %all_to_all.5 = f32[32,3,2,256]{3,2,1,0:T(2,128)S(1)} all-to-all(f32[32,3,2,256]{3,2,1,0:T(2,128)S(1)} %bitcast.109), channel_id=1, replica_groups=mesh['req'=4,'mp'=8] {'req','mp'}, dimensions={0} | all-to-all | bytes 393216 | tf_op jit(solution)/shard_map/all_to_all | solution.py:200
  271.4 0.1 fusion.42
  271.6 0.7 select_reduce_fusion.1
  272.3 0.6 dynamic_slice.9
  272.9 0.7 fusion.73
  (56 shorter events, 0.4 us)
Async XLA Ops:
  7.2 23.8 %copy-start = (bf16[2,256,2048]{2,1,0:T(8,128)(2,1)S(1)}, bf16[2,256,2048]{2,1,0:T(8,128)(2,1)}, u32[]{:S(2)}) copy-start(bf16[2,256,2048]{2,1,0:T(8,128)(2,1)} %param.23) | copy-start | bytes 6291460
  7.2 4.6 %copy-start.15 = (s32[1,8]{1,0:T(1,128)S(1)}, s32[1,8]{1,0:T(1,128)}, u32[]{:S(2)}) copy-start(s32[1,8]{1,0:T(1,128)} %param.16) | copy-start | bytes 100
  7.2 4.9 %copy-start.6 = (f32[2,2048]{1,0:T(2,128)S(1)}, f32[2,2048]{1,0:T(2,128)}, u32[]{:S(2)}) copy-start(f32[2,2048]{1,0:T(2,128)} %param.19) | copy-start | bytes 49156
  7.2 61.4 %reduce-scatter.3.cloned.1.call-start = ((), (), s32[]{:S(2)}) async-start(), calls=%async_computation.3 | async-start | bytes 2359296 | tf_op jit(solution)/shard_map/reduce_scatter | solution.py:152
  11.9 7.0 %copy-start.10 = (s32[8,1]{0,1:T(1,128)}, s32[8,1]{0,1:T(1,128)S(1)}, u32[]{:S(2)}) copy-start(s32[8,1]{0,1:T(1,128)S(1)} %reduce-window.4) | copy-start | bytes 100
  11.9 5.8 %copy-start.3 = (f32[256,2048]{1,0:T(8,128)S(1)}, f32[256,2048]{1,0:T(8,128)}, u32[]{:S(2)}) copy-start(f32[256,2048]{1,0:T(8,128)} %convert_multiply_fusion) | copy-start | bytes 6291460
  11.9 5.8 %copy-start.5 = (bf16[2,2048,256]{2,1,0:T(8,128)(2,1)S(1)}, bf16[2,2048,256]{2,1,0:T(8,128)(2,1)}, u32[]{:S(2)}) copy-start(bf16[2,2048,256]{2,1,0:T(8,128)(2,1)} %param.20) | copy-start | bytes 6291460
  11.9 6.9 %copy-start.12 = (s32[8]{0:T(128)}, s32[8]{0:T(128)S(1)}, u32[]{:S(2)}) copy-start(s32[8]{0:T(128)S(1)} %fusion.77) | copy-start | bytes 100
  23.8 4.6 %copy-start.16 = (f32[4,256]{1,0:T(4,128)S(1)}, f32[4,256]{1,0:T(4,128)}, u32[]{:S(2)}) copy-start(f32[4,256]{1,0:T(4,128)} %fusion.98) | copy-start | bytes 12292
  30.9 38.9 %copy-start.8 = (f32[2,2048]{1,0:T(2,128)S(1)}, f32[2,2048]{1,0:T(2,128)}, u32[]{:S(2)}) copy-start(f32[2,2048]{1,0:T(2,128)} %param.24) | copy-start | bytes 49156
  33.1 69.5 %all-gather.3.cloned.1.call-start = ((), (), s32[]{:S(2)}) async-start(), calls=%async_computation.4 | async-start | bytes 2359296 | tf_op jit(solution)/shard_map/all_gather | solution.py:163
  71.6 84.0 %reduce-scatter.5.cloned.1.call-start = ((), (), s32[]{:S(2)}) async-start(), calls=%async_computation.5 | async-start | bytes 2359296 | tf_op jit(solution)/shard_map/reduce_scatter | solution.py:168
  102.6 7.8 %copy-start.2 = (bf16[256,2,2048]{2,0,1:T(8,128)(2,1)S(1)}, bf16[256,2,2048]{2,0,1:T(8,128)(2,1)}, u32[]{:S(2)}) copy-start(bf16[256,2,2048]{2,0,1:T(8,128)(2,1)} %all-gather.3.cloned.1.call-done) | copy-start | bytes 6291460
  110.4 45.2 %copy-start.4 = (bf16[32,2,2048]{2,0,1:T(8,128)(2,1)S(1)}, bf16[32,2,2048]{2,0,1:T(8,128)(2,1)}, u32[]{:S(2)}) copy-start(bf16[32,2,2048]{2,0,1:T(8,128)(2,1)} %reduce-scatter.3.cloned.1.call-done) | copy-start | bytes 786436
  110.4 46.3 %copy-start.7 = (f32[2,2048]{1,0:T(2,128)S(1)}, f32[2,2048]{1,0:T(2,128)}, u32[]{:S(2)}) copy-start(f32[2,2048]{1,0:T(2,128)} %param.28) | copy-start | bytes 49156
  122.9 35.6 %copy-start.9 = (s32[1024]{0:T(1024)S(1)}, s32[1024]{0:T(1024)}, u32[]{:S(2)}) copy-start(s32[1024]{0:T(1024)} %param.18) | copy-start | bytes 12292
  123.0 114.5 %all-gather.5.cloned.1.call-start = ((), (), s32[]{:S(2)}) async-start(), calls=%async_computation.6 | async-start | bytes 8650752 | tf_op jit(solution)/shard_map/all_gather | solution.py:182
  254.3 19.2 %copy-start.1 = (bf16[2,256,2048]{2,1,0:T(8,128)(2,1)S(1)}, bf16[2,256,2048]{2,1,0:T(8,128)(2,1)}, u32[]{:S(2)}) copy-start(bf16[2,256,2048]{2,1,0:T(8,128)(2,1)} %param.23) | copy-start | bytes 6291460
  254.3 17.2 %copy-start.14 = (s32[256]{0:T(256)S(1)}, s32[256]{0:T(256)}, u32[]{:S(2)}) copy-start(s32[256]{0:T(256)} %param.17) | copy-start | bytes 3076
  254.3 17.2 %copy-start.11 = (s32[8,1]{0,1:T(1,128)S(1)}, s32[8,1]{0,1:T(1,128)}, u32[]{:S(2)}) copy-start(s32[8,1]{0,1:T(1,128)} %copy-done.10) | copy-start | bytes 100
  254.4 17.2 %copy-start.13 = (s32[8]{0:T(128)S(1)}, s32[8]{0:T(128)}, u32[]{:S(2)}) copy-start(s32[8]{0:T(128)} %copy-done.12) | copy-start | bytes 100
Sparse Core Ops, SparseCore 0:
  33.2 35.3 reduce-scatter.2
  71.7 30.8 all-gather.2
  123.1 32.4 reduce-scatter.4
  158.6 78.7 all-gather.4

commit v9 on v7

--- a/solution.py
+++ b/solution.py
@@ -114,18 +114,16 @@
         w_query.reshape(2, width, heads_here, HEAD_DIM),
         preferred_element_type=jnp.float32,
     )
-    keys_here = jnp.einsum(
+    key_value = jnp.einsum(
         "mtd,mdhe->mhte",
         normed,
-        key_cols.reshape(2, width, kv_here, HEAD_DIM),
+        jnp.concatenate([key_cols, value_columns], axis=2).reshape(
+            2, width, 2 * kv_here, HEAD_DIM
+        ),
         preferred_element_type=jnp.float32,
     )
-    values_here = jnp.einsum(
-        "mtd,mdhe->mhte",
-        normed,
-        value_columns.reshape(2, width, kv_here, HEAD_DIM),
-        preferred_element_type=jnp.float32,
-    )
+    keys_here = key_value[:, :kv_here]
+    values_here = key_value[:, kv_here:]
     for model in range(2):
         attended_list.append(
             attend_heads(

time: 278 us -> 282 us (1.014)
  local copies, waits for them, and re-layouts: 1.05 us -> 8.61 us
    dot_general x2 -> x1, matrix products: 6.56 us -> 0.83 us  [per_device(): jnp.einsum('mtd,mdhe->mhte', normed, jnp.concatenate([key_cols, value_col...]
  transfers between devices with their start and end apart: 4 -> 4, of which waited for: 4 -> 4; matrix products, arithmetic and copies ran while one was open for 1% -> 0% of each run, Pallas kernels for 0% -> 0%
where the time goes in v9:
time: 282 us
  waiting for transfers between devices  177 us (63%)
  matrix products  53.2 us (19%)
  other arithmetic  16.3 us (6%)
  between operations  14.1 us (5%)
  blocking collectives  12.3 us (4%)
  local copies, waits for them, and re-layouts  8.61 us (3%)
    all_gather x1, waiting for transfers between devices, per_device(): lax.all_gather(closing, ('req', 'mp'), axis=0, tiled=True)  78.3 us
    reduce_scatter x1, waiting for transfers between devices, per_device(): lax.psum_scatter(jnp.einsum('kbq,bqo->kbo', selected_rows, output_weight,...  35.4 us
    reduce_scatter x1, waiting for transfers between devices, per_device(): lax.psum_scatter(jnp.einsum('nmf,mfd->nmd', selected_rows, w_down, prefer...  32.2 us
    all_gather x1, waiting for transfers between devices, per_device(): row_block = lax.all_gather(normed_mid, 'mp', axis=0, tiled=True)  30.8 us
    dot_general x1, matrix products, per_device(): jnp.einsum('nmd,mdv->mnv', lax.all_gather(closing, ('req', 'mp'), axis=0,...  16.9 us
    dot_general x1, matrix products, per_device(): jnp.einsum('nmf,mfd->nmd', selected_rows, w_down, preferred_element_type=...  12.5 us
    all_to_all x1, blocking collectives, per_device(): incoming = lax.all_to_all(outgoing, ('req', 'mp'), 0, 0, tiled=True)  12.3 us
    dot_general x1, matrix products, per_device(): jnp.einsum('nmd,mdf->nmf', row_block, w_gate, preferred_element_type=jnp....  7.79 us
  transfers between devices with their start and end apart: 4, of which 4 were waited for; matrix products, arithmetic and copies ran while one was open for 0% of the time, Pallas kernels for 0%

profile of v9, /device:TPU:1, one launch (start us, length us, event | category | flops | bytes accessed | tf_op | source)
XLA Modules:
  0.0 281.8 jit_solution(5991524996982605885)
XLA Ops:
  7.3 2.3 constant_dynamic-slice_fusion
  9.6 1.6 pad_maximum_fusion
  11.2 2.3 copy.44
  13.5 0.3 fusion.8
  13.8 0.2 convert_multiply_fusion
  14.0 1.3 copy-done.2
  15.3 0.8 fusion.100
  16.2 0.2 reduce-window.4
  16.4 0.1 select_reduce_fusion.2
  16.5 0.4 copy-done.13
  16.9 3.2 %fusion.5 = f32[2,256,256]{1,2,0:S(1)} fusion(bf16[2,2048,256]{2,1,0:T(8,128)(2,1)} %param.20, f32[2,2048]{1,0:T(2,128)S(1)} %copy-done.9, f32[256,2048]{1,0:T(8,128)} %copy-done.2), kind=kOutput, calls=%fused_computation.11 | convolution fusion | flops 538968064 | bytes 4734976
  20.2 0.1 fusion.32
  20.3 0.2 multiply_cosine_fusion.1
  20.5 0.8 fusion.73
  21.3 0.1 subtract_convert_fusion.1
  21.4 0.5 copy-done.8
  21.9 0.1 copy-done.7
  22.0 1.3 fusion.24
  23.3 2.0 fusion.101
  25.3 0.7 pad_maximum_fusion.2
  26.0 1.4 fusion.23
  27.4 0.5 fusion.95
  27.9 0.6 slice_bitcast_fusion.6
  28.5 1.9 convolution_convert_fusion.3
  30.5 0.1 copy.47
  30.6 2.0 convolution_convert_fusion.2
  32.6 0.1 copy.48
  32.7 2.1 fusion.6
  34.9 35.4 %reduce-scatter.3.cloned.1.call-done = bf16[32,2,2048]{2,0,1:T(8,128)(2,1)} async-done(((bf16[256,2,2048]{2,0,1:T(8,128)(2,1)}), bf16[32,2,2048]{2,0,1:T(8,128)(2,1)}) %reduce-scatter.3.cloned.1.call-update) | async-done | bytes 262160 | tf_op jit(solution)/shard_map/reduce_scatter | solution.py:140
  70.3 1.1 multiply_reduce_fusion.1
  71.4 1.8 multiply_convert_fusion.3
  73.3 0.2 reduce-scatter.5.cloned.1.call-start
  73.5 30.8 %all-gather.3.cloned.1.call-done = bf16[256,2,2048]{2,0,1:T(8,128)(2,1)} async-done(((bf16[32,2,2048]{2,0,1:T(8,128)(2,1)}), bf16[256,2,2048]{2,0,1:T(8,128)(2,1)}) %all-gather.3.cloned.1.call-update) | async-done | bytes 2097168 | tf_op jit(solution)/shard_map/all_gather | solution.py:151
  104.3 7.8 %fusion.107 = f32[2,256,1024]{2,1,0:T(8,128)} fusion(bf16[256,2,2048]{2,0,1:T(8,128)(2,1)} %all-gather.3.cloned.1.call-done, bf16[2,2048,1024]{2,1,0:T(8,128)(2,1)} %param.25), kind=kOutput, calls=%fused_computation.152 | convolution fusion | flops 2147483648 | bytes 12582912 | tf_op jit(solution)/shard_map/nmd,mdf->nmf/dot_general | solution.py:152
  112.1 12.5 %fusion.7 = bf16[256,2,2048]{2,0,1:T(8,128)(2,1)} fusion(bf16[2,1024,2048]{2,1,0:T(8,128)(2,1)} %param.27, f32[2,256,1024]{2,1,0:T(8,128)} %fusion.107, bf16[256,2,2048]{2,0,1:T(8,128)(2,1)S(1)} %copy-done.3, bf16[2,2048,1024]{2,1,0:T(8,128)(2,1)} %param.26), kind=kOutput, calls=%fused_computation.13 | convolution fusion | flops 4299161600 | bytes 23068672 | tf_op jit(solution)/shard_map/nmf,mfd->nmd/dot_general | solution.py:157
  124.7 0.3 all-gather.5.cloned.1.call-start
  124.9 32.2 %reduce-scatter.5.cloned.1.call-done = bf16[32,2,2048]{2,0,1:T(8,128)(2,1)} async-done(((bf16[256,2,2048]{2,0,1:T(8,128)(2,1)}), bf16[32,2,2048]{2,0,1:T(8,128)(2,1)}) %reduce-scatter.5.cloned.1.call-update) | async-done | bytes 262160 | tf_op jit(solution)/shard_map/reduce_scatter | solution.py:156
  157.2 1.1 multiply_reduce_fusion
  158.3 1.8 multiply_convert_fusion.2
  160.2 0.7 iota_compare_fusion
  160.9 78.3 %all-gather.5.cloned.1.call-done = bf16[1024,2,2048]{2,0,1:T(8,128)(2,1)} async-done(((bf16[32,2,2048]{2,0,1:T(8,128)(2,1)}), bf16[1024,2,2048]{2,0,1:T(8,128)(2,1)}) %all-gather.5.cloned.1.call-update) | async-done | bytes 8388624 | tf_op jit(solution)/shard_map/all_gather | solution.py:170
  239.2 16.9 %fusion.106 = (f32[2,1024]{1,0:T(2,128)S(1)}, f32[2,1024,1002]{1,2,0:T(8,128)}) fusion(bf16[1024,2,2048]{2,0,1:T(8,128)(2,1)} %all-gather.5.cloned.1.call-done, bf16[2,2048,1002]{1,0,2:T(2,128)(2,1)} %param.29), kind=kOutput, calls=%fused_computation.151 | convolution fusion | flops 8407435264 | bytes 24813568 | tf_op jit(solution)/shard_map/nmd,mdv->mnv/dot_general | solution.py:168
  256.1 4.6 %exponential_reduce_fusion = (f32[2,1024]{1,0:T(2,128)S(1)}, f32[2,1024]{1,0:T(2,128)S(1)}) fusion(f32[2,1024,1002]{1,2,0:T(8,128)} %get-tuple-element.32, f32[2,1024]{1,0:T(2,128)S(1)} %get-tuple-element.31, pred[1024,1002]{0,1:T(8,128)(4,1)S(1)} %iota_compare_fusion), kind=kLoop, calls=%fused_computation.5 | loop fusion | flops 8204288 | bytes 9259008 | tf_op jit(solution)/shard_map/reduce_sum | solution.py:175
  260.8 12.3 %all_to_all.5 = f32[32,3,2,256]{3,2,1,0:T(2,128)S(1)} all-to-all(f32[32,3,2,256]{3,2,1,0:T(2,128)S(1)} %bitcast.113), channel_id=1, replica_groups=mesh['req'=4,'mp'=8] {'req','mp'}, dimensions={0} | all-to-all | bytes 393216 | tf_op jit(solution)/shard_map/all_to_all | solution.py:188
  273.2 0.1 fusion.44
  273.3 0.7 select_reduce_fusion.1
  274.0 0.6 dynamic_slice.15
  274.6 0.7 fusion.75
  (64 shorter events, 0.6 us)
Async XLA Ops:
  7.2 25.6 %copy-start = (bf16[2,256,2048]{2,1,0:T(8,128)(2,1)S(1)}, bf16[2,256,2048]{2,1,0:T(8,128)(2,1)}, u32[]{:S(2)}) copy-start(bf16[2,256,2048]{2,1,0:T(8,128)(2,1)} %param.23) | copy-start | bytes 6291460
  7.2 63.1 %reduce-scatter.3.cloned.1.call-start = ((), (), s32[]{:S(2)}) async-start(), calls=%async_computation.3 | async-start | bytes 2359296 | tf_op jit(solution)/shard_map/reduce_scatter | solution.py:140
  9.6 3.9 %copy-start.4 = (bf16[256,2048]{1,0:T(8,128)(2,1)S(1)}, bf16[256,2048]{1,0:T(8,128)(2,1)}, u32[]{:S(2)}) copy-start(bf16[256,2048]{1,0:T(8,128)(2,1)} %param.15) | copy-start | bytes 3145732
  13.5 1.9 copy-start.5
  13.5 1.9 copy-start.9
  14.0 1.4 copy-start.2
  14.0 2.2 copy-start.18
  16.4 0.5 copy-start.13
  16.4 3.7 %copy-start.15 = (s32[8]{0:T(128)}, s32[8]{0:T(128)S(1)}, u32[]{:S(2)}) copy-start(s32[8]{0:T(128)S(1)} %fusion.79) | copy-start | bytes 100
  21.3 0.6 copy-start.8
  21.4 0.6 copy-start.7
  25.3 3.3 %copy-start.19 = (f32[4,256]{1,0:T(4,128)S(1)}, f32[4,256]{1,0:T(4,128)}, u32[]{:S(2)}) copy-start(f32[4,256]{1,0:T(4,128)} %fusion.101) | copy-start | bytes 12292
  34.8 36.6 %copy-start.11 = (f32[2,2048]{1,0:T(2,128)S(1)}, f32[2,2048]{1,0:T(2,128)}, u32[]{:S(2)}) copy-start(f32[2,2048]{1,0:T(2,128)} %param.24) | copy-start | bytes 49156
  34.8 69.5 %all-gather.3.cloned.1.call-start = ((), (), s32[]{:S(2)}) async-start(), calls=%async_computation.4 | async-start | bytes 2359296 | tf_op jit(solution)/shard_map/all_gather | solution.py:151
  73.3 83.9 %reduce-scatter.5.cloned.1.call-start = ((), (), s32[]{:S(2)}) async-start(), calls=%async_computation.5 | async-start | bytes 2359296 | tf_op jit(solution)/shard_map/reduce_scatter | solution.py:156
  104.3 7.8 %copy-start.3 = (bf16[256,2,2048]{2,0,1:T(8,128)(2,1)S(1)}, bf16[256,2,2048]{2,0,1:T(8,128)(2,1)}, u32[]{:S(2)}) copy-start(bf16[256,2,2048]{2,0,1:T(8,128)(2,1)} %all-gather.3.cloned.1.call-done) | copy-start | bytes 6291460
  124.6 32.5 %copy-start.6 = (bf16[32,2,2048]{2,0,1:T(8,128)(2,1)S(1)}, bf16[32,2,2048]{2,0,1:T(8,128)(2,1)}, u32[]{:S(2)}) copy-start(bf16[32,2,2048]{2,0,1:T(8,128)(2,1)} %reduce-scatter.3.cloned.1.call-done) | copy-start | bytes 786436
  124.6 33.7 %copy-start.10 = (f32[2,2048]{1,0:T(2,128)S(1)}, f32[2,2048]{1,0:T(2,128)}, u32[]{:S(2)}) copy-start(f32[2,2048]{1,0:T(2,128)} %param.28) | copy-start | bytes 49156
  124.6 35.5 %copy-start.12 = (s32[1024]{0:T(1024)S(1)}, s32[1024]{0:T(1024)}, u32[]{:S(2)}) copy-start(s32[1024]{0:T(1024)} %param.18) | copy-start | bytes 12292
  124.7 114.5 %all-gather.5.cloned.1.call-start = ((), (), s32[]{:S(2)}) async-start(), calls=%async_computation.6 | async-start | bytes 8650752 | tf_op jit(solution)/shard_map/all_gather | solution.py:170
  256.1 17.2 %copy-start.17 = (s32[256]{0:T(256)S(1)}, s32[256]{0:T(256)}, u32[]{:S(2)}) copy-start(s32[256]{0:T(256)} %param.17) | copy-start | bytes 3076
  256.1 17.2 %copy-start.14 = (s32[8,1]{0,1:T(1,128)S(1)}, s32[8,1]{0,1:T(1,128)}, u32[]{:S(2)}) copy-start(s32[8,1]{0,1:T(1,128)} %copy-done.13) | copy-start | bytes 100
  256.1 17.2 %copy-start.16 = (s32[8]{0:T(128)S(1)}, s32[8]{0:T(128)}, u32[]{:S(2)}) copy-start(s32[8]{0:T(128)} %copy-done.15) | copy-start | bytes 100
  256.1 19.2 %copy-start.1 = (bf16[2,256,2048]{2,1,0:T(8,128)(2,1)S(1)}, bf16[2,256,2048]{2,1,0:T(8,128)(2,1)}, u32[]{:S(2)}) copy-start(bf16[2,256,2048]{2,1,0:T(8,128)(2,1)} %param.23) | copy-start | bytes 6291460
Sparse Core Ops, SparseCore 0:
  35.0 35.3 reduce-scatter.2
  73.4 30.8 all-gather.2
  124.8 32.3 reduce-scatter.4
  160.3 78.8 all-gather.4

commit v10 on v7

--- a/solution.py
+++ b/solution.py
@@ -169,13 +169,16 @@
     column_ids = jnp.arange(vocab_here, dtype=jnp.int32)
     logits = jnp.einsum(
         "nmd,mdv->mnv",
-        lax.all_gather(closing, ("req", "mp"), axis=0, tiled=True),
+        lax.all_gather(closing, ("mp", "req"), axis=0, tiled=True),
         w_head,
         preferred_element_type=jnp.float32,
     )
     peak_part = jnp.max(logits, axis=-1)
     total_part = jnp.sum(jnp.exp(logits - peak_part[..., None]), axis=-1)
-    wanted = targets - vocab_first
+    gathered_targets = targets.reshape(
+        lax.axis_size("req"), lax.axis_size("mp"), own_rows
+    ).transpose(1, 0, 2).reshape(-1)
+    wanted = gathered_targets - vocab_first
     hit_part = jnp.sum(
         jnp.where(column_ids[None, None, :] == wanted[None, :, None], logits, 0.0), axis=-1
     )
@@ -183,7 +186,11 @@
     groups = lax.axis_size("req")
     parts = lax.axis_size("mp")
     stats = jnp.stack([peak_part, total_part, hit_part])
-    tenant_stats = stats.reshape(3, 2, groups, group_rows).transpose(2, 0, 1, 3)
+    tenant_stats = (
+        stats.reshape(3, 2, parts, groups, own_rows)
+        .transpose(3, 0, 1, 2, 4)
+        .reshape(groups, 3, 2, group_rows)
+    )
     outgoing = jnp.broadcast_to(
         tenant_stats[:, None], (groups, parts, 3, 2, group_rows)
     ).reshape(groups * parts, 3, 2, group_rows)

time: 278 us -> 278 us (level)
  no operation moved by 1% of the time
where the time goes in v10:
time: 278 us
  waiting for transfers between devices  176 us (63%)
  matrix products  55.4 us (20%)
  other arithmetic  18.3 us (7%)
  between operations  14.1 us (5%)
  blocking collectives  12.3 us (4%)
    all_gather x1, waiting for transfers between devices, per_device(): lax.all_gather(closing, ('mp', 'req'), axis=0, tiled=True)  78.1 us
    reduce_scatter x1, waiting for transfers between devices, per_device(): lax.psum_scatter(jnp.einsum('kbq,bqo->kbo', selected_rows, output_weight,...  34.5 us
    reduce_scatter x1, waiting for transfers between devices, per_device(): lax.psum_scatter(jnp.einsum('nmf,mfd->nmd', selected_rows, w_down, prefer...  32.3 us
    all_gather x1, waiting for transfers between devices, per_device(): row_block = lax.all_gather(normed_mid, 'mp', axis=0, tiled=True)  30.9 us
    dot_general x1, matrix products, per_device(): jnp.einsum('nmd,mdv->mnv', lax.all_gather(closing, ('mp', 'req'), axis=0,...  16.8 us
    dot_general x1, matrix products, per_device(): jnp.einsum('nmf,mfd->nmd', selected_rows, w_down, preferred_element_type=...  12.5 us
    all_to_all x1, blocking collectives, per_device(): incoming = lax.all_to_all(outgoing, ('req', 'mp'), 0, 0, tiled=True)  12.3 us
    dot_general x1, matrix products, per_device(): jnp.einsum('nmd,mdf->nmf', row_block, w_gate, preferred_element_type=jnp....  7.79 us
  transfers between devices with their start and end apart: 4, of which 4 were waited for; matrix products, arithmetic and copies ran while one was open for 1% of the time, Pallas kernels for 0%

profile of v10, /device:TPU:1, one launch (start us, length us, event | category | flops | bytes accessed | tf_op | source)
XLA Modules:
  0.0 278.0 jit_solution(596894073613968078)
XLA Ops:
  7.3 1.6 fusion.9
  8.9 2.8 %convert_multiply_fusion = f32[256,2048]{1,0:T(8,128)} fusion(bf16[256,2048]{1,0:T(8,128)(2,1)} %param.15, f32[256]{0:T(256)S(1)} %add_rsqrt_fusion.2), kind=kLoop, calls=%fused_computation.15 | loop fusion | flops 1048576 | bytes 3146752 | tf_op jit(solution)/shard_map/mul | solution.py:29
  11.7 3.3 %fusion.5 = f32[2,64,256]{2,1,0:T(8,128)S(1)} fusion(f32[2,2048]{1,0:T(2,128)S(1)} %copy-done.4, f32[256,2048]{1,0:T(8,128)} %convert_multiply_fusion, bf16[2,2048,512]{2,1,0:T(8,128)(2,1)} %param.21, s32[]{:T(128)S(6)} %select_n.31), kind=kOutput, calls=%fused_computation.9 | convolution fusion | flops 136314880 | bytes 3293188 | tf_op jit(solution)/shard_map/mtd,mdhe->mhte/dot_general | solution.py:117
  15.1 0.2 reduce-window.4
  15.2 0.1 select_reduce_fusion.2
  15.3 3.2 %fusion.6 = f32[2,256,256]{1,2,0:S(1)} fusion(bf16[2,2048,256]{2,1,0:T(8,128)(2,1)} %param.20, f32[2,2048]{1,0:T(2,128)S(1)} %copy-done.4, f32[256,2048]{1,0:T(8,128)} %convert_multiply_fusion), kind=kOutput, calls=%fused_computation.10 | convolution fusion | flops 538968064 | bytes 4734976
  18.6 0.1 fusion.34
  18.7 0.2 multiply_cosine_fusion.1
  18.9 0.2 fusion.75
  19.1 0.1 subtract_convert_fusion.1
  19.2 0.3 fusion.25
  19.6 1.1 fusion.104
  20.7 1.3 fusion.24
  22.0 0.5 fusion.99
  22.6 3.3 %fusion.27 = bf16[2,1,256,64]{2,3,0,1:T(8,128)(2,1)S(1)} fusion(f32[2,2048]{1,0:T(2,128)S(1)} %copy-done.4, f32[256,2048]{1,0:T(8,128)} %convert_multiply_fusion, bf16[2,2048,512]{2,1,0:T(8,128)(2,1)} %param.22, s32[]{:T(128)S(6)} %select_n.31), kind=kOutput, calls=%fused_computation.42 | convolution fusion | flops 136347648 | bytes 3227652 | tf_op jit(solution)/shard_map/mtd,mdhe->mhte/dot_general | solution.py:123
  25.9 0.4 convolution_convert_fusion.3
  26.3 0.1 copy.68
  26.4 1.9 convolution_convert_fusion.2
  28.3 0.1 copy.69
  28.5 2.1 fusion.7
  30.6 0.9 dynamic-slice_convert_fusion
  31.5 34.5 %reduce-scatter.3.cloned.1.call-done = bf16[32,2,2048]{2,0,1:T(8,128)(2,1)} async-done(((bf16[256,2,2048]{2,0,1:T(8,128)(2,1)}), bf16[32,2,2048]{2,0,1:T(8,128)(2,1)}) %reduce-scatter.3.cloned.1.call-update) | async-done | bytes 262160 | tf_op jit(solution)/shard_map/reduce_scatter | solution.py:142
  66.1 1.1 multiply_reduce_fusion.1
  67.2 1.8 multiply_convert_fusion.9
  69.0 0.2 reduce-scatter.5.cloned.1.call-start
  69.2 30.9 %all-gather.3.cloned.1.call-done = bf16[256,2,2048]{2,0,1:T(8,128)(2,1)} async-done(((bf16[32,2,2048]{2,0,1:T(8,128)(2,1)}), bf16[256,2,2048]{2,0,1:T(8,128)(2,1)}) %all-gather.3.cloned.1.call-update) | async-done | bytes 2097168 | tf_op jit(solution)/shard_map/all_gather | solution.py:153
  100.1 7.8 %fusion.110 = f32[2,256,1024]{2,1,0:T(8,128)} fusion(bf16[256,2,2048]{2,0,1:T(8,128)(2,1)} %all-gather.3.cloned.1.call-done, bf16[2,2048,1024]{2,1,0:T(8,128)(2,1)} %param.25), kind=kOutput, calls=%fused_computation.155 | convolution fusion | flops 2147483648 | bytes 12582912 | tf_op jit(solution)/shard_map/nmd,mdf->nmf/dot_general | solution.py:154
  107.9 12.5 %fusion.8 = bf16[256,2,2048]{2,0,1:T(8,128)(2,1)} fusion(bf16[2,1024,2048]{2,1,0:T(8,128)(2,1)} %param.27, f32[2,256,1024]{2,1,0:T(8,128)} %fusion.110, bf16[256,2,2048]{2,0,1:T(8,128)(2,1)S(1)} %copy-done.2, bf16[2,2048,1024]{2,1,0:T(8,128)(2,1)} %param.26), kind=kOutput, calls=%fused_computation.14 | convolution fusion | flops 4299161600 | bytes 23068672 | tf_op jit(solution)/shard_map/nmf,mfd->nmd/dot_general | solution.py:159
  120.5 0.3 all-gather.5.cloned.1.call-start
  120.7 32.3 %reduce-scatter.5.cloned.1.call-done = bf16[32,2,2048]{2,0,1:T(8,128)(2,1)} async-done(((bf16[256,2,2048]{2,0,1:T(8,128)(2,1)}), bf16[32,2,2048]{2,0,1:T(8,128)(2,1)}) %reduce-scatter.5.cloned.1.call-update) | async-done | bytes 262160 | tf_op jit(solution)/shard_map/reduce_scatter | solution.py:158
  153.0 1.1 multiply_reduce_fusion
  154.2 1.8 multiply_convert_fusion.8
  156.0 0.1 sub.102
  156.1 0.1 sub.104
  156.2 0.7 iota_compare_fusion
  156.9 78.1 %all-gather.5.cloned.1.call-done = bf16[1024,2,2048]{2,0,1:T(8,128)(2,1)} async-done(((bf16[32,2,2048]{2,0,1:T(8,128)(2,1)}), bf16[1024,2,2048]{2,0,1:T(8,128)(2,1)}) %all-gather.5.cloned.1.call-update) | async-done | bytes 8388624 | tf_op jit(solution)/shard_map/all_gather | solution.py:172
  235.0 16.8 %fusion.109 = (f32[2,1024]{1,0:T(2,128)S(1)}, f32[2,1024,1002]{1,2,0:T(8,128)}) fusion(bf16[1024,2,2048]{2,0,1:T(8,128)(2,1)} %all-gather.5.cloned.1.call-done, bf16[2,2048,1002]{1,0,2:T(2,128)(2,1)} %param.29), kind=kOutput, calls=%fused_computation.154 | convolution fusion | flops 8407435264 | bytes 24813568 | tf_op jit(solution)/shard_map/nmd,mdv->mnv/dot_general | solution.py:170
  251.8 0.1 stack.16
  252.0 4.6 %exponential_reduce_fusion = (f32[2,1024]{1,0:T(2,128)S(1)}, f32[2,1024]{1,0:T(2,128)S(1)}) fusion(f32[2,1024,1002]{1,2,0:T(8,128)} %get-tuple-element.28, f32[2,1024]{1,0:T(2,128)S(1)} %get-tuple-element.27, pred[1024,1002]{0,1:T(8,128)(4,1)S(1)} %iota_compare_fusion), kind=kLoop, calls=%fused_computation.5 | loop fusion | flops 8204288 | bytes 9259008 | tf_op jit(solution)/shard_map/reduce_sum | solution.py:177
  256.6 0.1 stack.17
  256.6 0.1 stack.18
  256.8 0.1 broadcast_in_dim.47
  256.9 0.1 broadcast_in_dim.48
  257.0 12.3 %all_to_all.5 = f32[32,3,2,256]{3,2,1,0:T(2,128)S(1)} all-to-all(f32[32,3,2,256]{3,2,1,0:T(2,128)S(1)} %bitcast.111), channel_id=1, replica_groups=mesh['req'=4,'mp'=8] {'req','mp'}, dimensions={0} | all-to-all | bytes 393216 | tf_op jit(solution)/shard_map/all_to_all | solution.py:197
  269.3 0.1 fusion.46
  269.5 0.7 select_reduce_fusion.1
  270.2 0.6 dynamic_slice.15
  270.8 0.7 fusion.77
  (56 shorter events, 0.5 us)
Async XLA Ops:
  7.2 21.3 %copy-start = (bf16[2,256,2048]{2,1,0:T(8,128)(2,1)S(1)}, bf16[2,256,2048]{2,1,0:T(8,128)(2,1)}, u32[]{:S(2)}) copy-start(bf16[2,256,2048]{2,1,0:T(8,128)(2,1)} %param.23) | copy-start | bytes 6291460
  7.2 58.9 %reduce-scatter.3.cloned.1.call-start = ((), (), s32[]{:S(2)}) async-start(), calls=%async_computation.3 | async-start | bytes 2359296 | tf_op jit(solution)/shard_map/reduce_scatter | solution.py:142
  7.3 4.5 %copy-start.4 = (f32[2,2048]{1,0:T(2,128)S(1)}, f32[2,2048]{1,0:T(2,128)}, u32[]{:S(2)}) copy-start(f32[2,2048]{1,0:T(2,128)} %param.19) | copy-start | bytes 49156
  11.7 3.3 %copy-start.13 = (s32[1,8]{1,0:T(1,128)S(1)}, s32[1,8]{1,0:T(1,128)}, u32[]{:S(2)}) copy-start(s32[1,8]{1,0:T(1,128)} %param.16) | copy-start | bytes 100
  15.2 3.3 %copy-start.8 = (s32[8,1]{0,1:T(1,128)}, s32[8,1]{0,1:T(1,128)S(1)}, u32[]{:S(2)}) copy-start(s32[8,1]{0,1:T(1,128)S(1)} %reduce-window.4) | copy-start | bytes 100
  15.2 3.3 %copy-start.10 = (s32[8]{0:T(128)}, s32[8]{0:T(128)S(1)}, u32[]{:S(2)}) copy-start(s32[8]{0:T(128)S(1)} %fusion.83) | copy-start | bytes 100
  22.6 3.3 %copy-start.14 = (f32[4,256]{1,0:T(4,128)S(1)}, f32[4,256]{1,0:T(4,128)}, u32[]{:S(2)}) copy-start(f32[4,256]{1,0:T(4,128)} %fusion.104) | copy-start | bytes 12292
  30.5 36.6 %copy-start.6 = (f32[2,2048]{1,0:T(2,128)S(1)}, f32[2,2048]{1,0:T(2,128)}, u32[]{:S(2)}) copy-start(f32[2,2048]{1,0:T(2,128)} %param.24) | copy-start | bytes 49156
  30.6 69.6 %all-gather.3.cloned.1.call-start = ((), (), s32[]{:S(2)}) async-start(), calls=%async_computation.4 | async-start | bytes 2359296 | tf_op jit(solution)/shard_map/all_gather | solution.py:153
  69.0 84.0 %reduce-scatter.5.cloned.1.call-start = ((), (), s32[]{:S(2)}) async-start(), calls=%async_computation.5 | async-start | bytes 2359296 | tf_op jit(solution)/shard_map/reduce_scatter | solution.py:158
  100.1 7.8 %copy-start.2 = (bf16[256,2,2048]{2,0,1:T(8,128)(2,1)S(1)}, bf16[256,2,2048]{2,0,1:T(8,128)(2,1)}, u32[]{:S(2)}) copy-start(bf16[256,2,2048]{2,0,1:T(8,128)(2,1)} %all-gather.3.cloned.1.call-done) | copy-start | bytes 6291460
  120.4 32.6 %copy-start.3 = (bf16[32,2,2048]{2,0,1:T(8,128)(2,1)S(1)}, bf16[32,2,2048]{2,0,1:T(8,128)(2,1)}, u32[]{:S(2)}) copy-start(bf16[32,2,2048]{2,0,1:T(8,128)(2,1)} %reduce-scatter.3.cloned.1.call-done) | copy-start | bytes 786436
  120.4 33.8 %copy-start.5 = (f32[2,2048]{1,0:T(2,128)S(1)}, f32[2,2048]{1,0:T(2,128)}, u32[]{:S(2)}) copy-start(f32[2,2048]{1,0:T(2,128)} %param.28) | copy-start | bytes 49156
  120.4 35.6 %copy-start.7 = (s32[1024]{0:T(1024)S(1)}, s32[1024]{0:T(1024)}, u32[]{:S(2)}) copy-start(s32[1024]{0:T(1024)} %param.18) | copy-start | bytes 12292
  120.5 114.5 %all-gather.5.cloned.1.call-start = ((), (), s32[]{:S(2)}) async-start(), calls=%async_computation.6 | async-start | bytes 8650752 | tf_op jit(solution)/shard_map/all_gather | solution.py:172
  251.9 17.5 %copy-start.12 = (s32[256]{0:T(256)S(1)}, s32[256]{0:T(256)}, u32[]{:S(2)}) copy-start(s32[256]{0:T(256)} %param.17) | copy-start | bytes 3076
  252.0 17.5 %copy-start.9 = (s32[8,1]{0,1:T(1,128)S(1)}, s32[8,1]{0,1:T(1,128)}, u32[]{:S(2)}) copy-start(s32[8,1]{0,1:T(1,128)} %copy-done.8) | copy-start | bytes 100
  252.0 17.5 %copy-start.11 = (s32[8]{0:T(128)S(1)}, s32[8]{0:T(128)}, u32[]{:S(2)}) copy-start(s32[8]{0:T(128)} %copy-done.10) | copy-start | bytes 100
  252.0 19.5 %copy-start.1 = (bf16[2,256,2048]{2,1,0:T(8,128)(2,1)S(1)}, bf16[2,256,2048]{2,1,0:T(8,128)(2,1)}, u32[]{:S(2)}) copy-start(bf16[2,256,2048]{2,1,0:T(8,128)(2,1)} %param.23) | copy-start | bytes 6291460
Sparse Core Ops, SparseCore 0:
  30.7 35.3 reduce-scatter.2
  69.1 30.9 all-gather.2
  120.6 32.4 reduce-scatter.4
  156.1 78.8 all-gather.4
